TPU v7x, 128 devices: a whole 4x4x4 slice. The times are simulated.
128 devices in a mesh: cfg: 2 (over core), orbit: 32 (over z, x_lo, y), tp: 2 (over x_hi).
Axes of the slice: x: 4 (x_hi: 2, x_lo: 2; x = x_hi * 2 + x_lo), y: 4, z: 4, core: 2. Of those that a mesh axis runs over, the one named last changes fastest.
Arguments:
- tokens: bfloat16 [2, 32, 1024, 1536], P('cfg', 'orbit', 'tp'), may hold values from -6 to 6
- modulation: float32 [2, 2, 1536], P('cfg'), may hold values from -2 to 6
- w_qkv: bfloat16 [1536, 3, 1536], P(None, None, 'tp'), may hold values from -1 to 1
- w_out: bfloat16 [1536, 1536], P('tp'), may hold values from -0.15625 to 0.15625
- adjacency: int32 [32, 4, 8], P('orbit'), may hold values 0 or 1
Outputs:
- guided: bfloat16 [32, 1024, 1536], P('orbit', 'tp', 'cfg')
All inputs are finite; a program needn't handle non-finite values. No bound on the sum of `adjacency` on one device may be relied on, other than what follows from the above.
Results may differ from a plain program's by a relative error of at most 0.0075.
Values may be sent and summed in bfloat16 or wider, within the bound.
No kernel may reach another device: no remote copies, remote signals or barrier semaphores. Data moves between devices by JAX's collectives and lax.ppermute only.
A program may use at most 128 MiB of HBM per device.

v0:
```python
import jax
import jax.numpy as jnp
from jax import lax
from jax.sharding import PartitionSpec as P

HEAD_DIM = 128
REACH = 2


guide_scale = 4.0


def from_behind(array, axis, by):
    count = lax.axis_size(axis)
    return lax.ppermute(array, axis, [(i, (i + by) % count) for i in range(count)])


def attend_head(queries, keyset, valueset, keymask):
    scores = jnp.dot(queries, keyset.T, preferred_element_type=jnp.float32) * queries.shape[1] ** (
        -0.5
    )
    scores = jnp.where(keymask[None, :], scores, -1e30)
    peak = jnp.max(scores, axis=1, keepdims=True)
    expon = jnp.exp(scores - peak)
    total = jnp.sum(expon, axis=1, keepdims=True)
    weights = expon.astype(jnp.bfloat16)
    return (jnp.dot(weights, valueset, preferred_element_type=jnp.float32) / total).astype(
        jnp.bfloat16
    )


def direct_send(payload, amount):
    return from_behind(payload, "orbit", amount)


def per_device(tokens, modulation, w_qkv, w_out, adjacency):
    inputs = tokens[0, 0].astype(jnp.float32)
    width = inputs.shape[1]
    half_heads = w_qkv.shape[2]
    shift_scale = modulation[0]
    squares = jnp.mean(inputs * inputs, axis=1, keepdims=True)
    normed = (inputs * lax.rsqrt(squares + 1e-06) * (1.0 + shift_scale[1]) + shift_scale[0]).astype(
        jnp.bfloat16
    )
    whole = lax.all_gather(normed, "tp", axis=0, tiled=True)
    rows_view = whole.shape[0]
    qkv = jnp.dot(whole, w_qkv.reshape(width, 3 * half_heads), preferred_element_type=jnp.float32)
    qkv = qkv.astype(jnp.bfloat16).reshape(rows_view, 3, half_heads)
    queries = qkv[:, 0]
    own_pair = qkv[:, 1:]
    received = {}
    for offset in range(1, REACH + 1):
        received[offset] = direct_send(own_pair, -offset)
        received[-offset] = direct_send(own_pair, offset)
    received[0] = own_pair
    stacked = jnp.stack([received[offset] for offset in range(-REACH, REACH + 1)], axis=0)
    keyflat = stacked[:, :, 0].reshape((2 * REACH + 1) * rows_view, half_heads)
    valflat = stacked[:, :, 1].reshape((2 * REACH + 1) * rows_view, half_heads)
    flags = adjacency[0]
    blocks = flags.shape[1]
    allowed = jnp.concatenate(
        [flags[:REACH], jnp.ones((1, blocks), jnp.int32), flags[REACH:]], axis=0
    )
    keymask = jnp.repeat(allowed, rows_view // blocks, axis=1).reshape(-1) > 0

    def one_head(head_index):
        start = head_index * HEAD_DIM
        return attend_head(
            lax.dynamic_slice_in_dim(queries, start, HEAD_DIM, 1),
            lax.dynamic_slice_in_dim(keyflat, start, HEAD_DIM, 1),
            lax.dynamic_slice_in_dim(valflat, start, HEAD_DIM, 1),
            keymask,
        )

    heads_out = lax.map(one_head, jnp.arange(half_heads // HEAD_DIM, dtype=jnp.int32))
    context = jnp.transpose(heads_out, (1, 0, 2)).reshape(rows_view, half_heads)
    summed = lax.psum_scatter(
        jnp.dot(context, w_out, preferred_element_type=jnp.float32),
        "tp",
        scatter_dimension=0,
        tiled=True,
    )
    branch_out = summed.astype(jnp.bfloat16)
    owner = lax.axis_index("cfg")
    half_width = width // 2
    weight_now = jnp.where(owner == 0, guide_scale, 1.0 - guide_scale).astype(jnp.float32)
    combined = lax.psum(
        (weight_now * branch_out.astype(jnp.float32)).astype(jnp.bfloat16), "cfg"
    ).astype(jnp.float32)
    guided = lax.dynamic_slice_in_dim(combined, owner * half_width, half_width, 1)
    return guided.astype(jnp.bfloat16)[None]


def solution(mesh):
    return jax.shard_map(
        per_device,
        mesh=mesh,
        in_specs=(
            P("cfg", "orbit", "tp", None),
            P("cfg", None, None),
            P(None, None, "tp"),
            P("tp", None),
            P("orbit", None, None),
        ),
        out_specs=P("orbit", "tp", "cfg"),
        check_vma=False,
    )
```

profile of v0, /device:TPU:1, one launch (start us, length us, event | category | flops | bytes accessed | tf_op | source)
XLA Modules:
  0.0 622.0 jit_solution(14413159048128313213)
XLA Ops:
  12.5 10.3 %copy.7 = bf16[1536,3,768]{0,2,1:T(8,128)(2,1)} copy(bf16[1536,3,768]{2,0,1:T(8,128)(2,1)} %param.9) | data formatting | bytes 14155776 | tf_op args[2]
  22.7 41.8 %all-gather.2.cloned.1.call-done = bf16[1024,1536]{1,0:T(8,128)(2,1)} async-done(((bf16[512,1536]{1,0:T(8,128)(2,1)}), bf16[1024,1536]{1,0:T(8,128)(2,1)}) %all-gather.2.cloned.1.call-update) | async-done | bytes 3145744 | tf_op jit(solution)/shard_map/all_gather | solution.py:45
  64.5 12.6 %convolution_convert_fusion = bf16[1024,2304]{1,0:T(8,128)(2,1)} fusion(bf16[1024,1536]{1,0:T(8,128)(2,1)} %all-gather.2.cloned.1.call-done, bf16[1536,2304]{0,1:T(8,128)(2,1)} %bitcast.52), kind=kOutput, calls=%fused_computation.21 | convolution fusion | flops 7250116608 | bytes 14942208 | tf_op jit(solution)/shard_map/dot_general | solution.py:47
  77.2 6.6 %copy.8 = bf16[1024,2304]{0,1:T(8,128)(2,1)} copy(bf16[1024,2304]{1,0:T(8,128)(2,1)} %convolution_convert_fusion) | data formatting | bytes 9437184 | tf_op jit(solution)/shard_map/convert_element_type | solution.py:48
  90.7 5.4 collective-permute-start.2
  99.1 62.3 %collective-permute-done = bf16[1024,2,768]{0,2,1:T(8,128)(2,1)} collective-permute-done((bf16[1024,2,768]{0,2,1:T(8,128)(2,1)}, bf16[1024,2,768]{0,2,1:T(8,128)(2,1)}, u32[]{:S(2)}, u32[]{:S(2)}) %collective-permute-start) | collective-permute-done | bytes 3145760 | tf_op jit(solution)/shard_map/ppermute | solution.py:15
  163.6 65.9 %collective-permute-done.1 = bf16[1024,2,768]{0,2,1:T(8,128)(2,1)} collective-permute-done((bf16[1024,2,768]{0,2,1:T(8,128)(2,1)}, bf16[1024,2,768]{0,2,1:T(8,128)(2,1)}, u32[]{:S(2)}, u32[]{:S(2)}) %collective-permute-start.1) | collective-permute-done | bytes 3145760 | tf_op jit(solution)/shard_map/ppermute | solution.py:15
  232.0 128.5 %collective-permute-done.2 = bf16[1024,2,768]{0,2,1:T(8,128)(2,1)} collective-permute-done((bf16[1024,2,768]{0,2,1:T(8,128)(2,1)}, bf16[1024,2,768]{0,2,1:T(8,128)(2,1)}, u32[]{:S(2)}, u32[]{:S(2)}) %collective-permute-start.2) | collective-permute-done | bytes 3145760 | tf_op jit(solution)/shard_map/ppermute | solution.py:15
  365.0 6.0 fusion.36
  370.9 10.6 %copy.9 = bf16[5,1024,1,768]{3,1,0,2:T(8,128)(2,1)} copy(bf16[5,1024,1,768]{1,3,2,0:T(8,128)(2,1)} %get-tuple-element.86) | data formatting | bytes 15728640 | tf_op jit(solution)/shard_map/slice | solution.py:57
  381.6 10.5 %copy.10 = bf16[5,1024,1,768]{3,1,0,2:T(8,128)(2,1)} copy(bf16[5,1024,1,768]{1,3,2,0:T(8,128)(2,1)} %get-tuple-element.85) | data formatting | bytes 15728640 | tf_op jit(solution)/shard_map/slice | solution.py:58
  392.1 106.5 %while.11 = (s32[]{:T(128)}, bf16[6,1024,128]{1,2,0:T(8,128)(2,1)}, s32[6]{0:T(128)S(1)}, bf16[1024,768]{0,1:T(8,128)(2,1)}, bf16[5120,768]{1,0:T(8,128)(2,1)}, ...) while((s32[]{:T(128)}, bf16[6,1024,128]{1,2,0:T(8,128)(2,1)}, ...), condition=%wide.region_4.5_spmd.clone, body=%wide.region_1.4_spmd.clone.sunk | while | flops 2742286336 | bytes 67151568 | solution.py:75
  398.4 5.1 fusion.50
  403.5 5.4 fusion.51
  416.2 5.1 fusion.50
  421.3 5.4 fusion.51
  433.9 5.1 fusion.50
  439.0 5.4 fusion.51
  456.8 5.4 fusion.51
  474.6 5.4 fusion.51
  492.3 5.4 fusion.51
  498.6 6.1 fusion.37
  504.8 79.1 %reduce-scatter.2.cloned.1.call-done = f32[512,1536]{1,0:T(8,128)} async-done(((f32[1024,1536]{1,0:T(8,128)}), f32[512,1536]{1,0:T(8,128)}) %reduce-scatter.2.cloned.1.call-update) | async-done | bytes 3145744 | tf_op jit(solution)/shard_map/reduce_scatter | solution.py:77
  587.3 26.1 %all-reduce.2.cloned.1.call-done = bf16[512,1536]{1,0:T(8,128)(2,1)} async-done(((bf16[512,1536]{1,0:T(8,128)(2,1)}), bf16[512,1536]{1,0:T(8,128)(2,1)}) %all-reduce.2.cloned.1.call-update) | async-done | bytes 1572880 | tf_op jit(solution)/shard_map/psum | solution.py:87
  (70 shorter events, 84.7 us)
Async XLA Ops:
  6.5 492.1 %copy-start = (bf16[768,1536]{1,0:T(8,128)(2,1)S(1)}, bf16[768,1536]{1,0:T(8,128)(2,1)}, u32[]{:S(2)}) copy-start(bf16[768,1536]{1,0:T(8,128)(2,1)} %param.10) | copy-start | bytes 7077892
  6.5 58.0 %all-gather.2.cloned.1.call-start = ((), (), s32[]{:S(2)}) async-start(), calls=%async_computation.1 | async-start | bytes 4718592 | tf_op jit(solution)/shard_map/all_gather | solution.py:45
  12.4 571.5 %reduce-scatter.2.cloned.1.call-start = ((), (), s32[]{:S(2)}) async-start(), calls=%async_computation.2 | async-start | bytes 9437184 | tf_op jit(solution)/shard_map/reduce_scatter | solution.py:77
  83.8 12.4 %copy-start.1 = (s32[1,4,8]{2,1,0:T(4,128)S(1)}, s32[1,4,8]{2,1,0:T(4,128)}, u32[]{:S(2)}) copy-start(s32[1,4,8]{2,1,0:T(4,128)} %param.11) | copy-start | bytes 388
  87.7 73.7 %collective-permute-start = (bf16[1024,2,768]{0,2,1:T(8,128)(2,1)}, bf16[1024,2,768]{0,2,1:T(8,128)(2,1)}, u32[]{:S(2)}, u32[]{:S(2)}) collective-permute-start(bf16[1024,2,768]{0,2,1:T(8,128)(2,1)} %slice.43), channel_id=1, source_target_pairs={{0,4},{2,6},{4,8},{6,10},{8,12},{10,14},{12,16},{14,18},{16,20},{1... | collective-permute-start | bytes 9437192 | tf_op jit(solution)/shard_map/ppermute | solution.py:15
  90.4 139.1 %collective-permute-start.1 = (bf16[1024,2,768]{0,2,1:T(8,128)(2,1)}, bf16[1024,2,768]{0,2,1:T(8,128)(2,1)}, u32[]{:S(2)}, u32[]{:S(2)}) collective-permute-start(bf16[1024,2,768]{0,2,1:T(8,128)(2,1)} %slice.43), channel_id=1, source_target_pairs={{0,2},{2,4},{4,6},{6,8},{8,10},{10,12},{12,14},{14,16},{16,18},{18... | collective-permute-start | bytes 9437192 | tf_op jit(solution)/shard_map/ppermute | solution.py:15
  90.7 269.8 %collective-permute-start.2 = (bf16[1024,2,768]{0,2,1:T(8,128)(2,1)}, bf16[1024,2,768]{0,2,1:T(8,128)(2,1)}, u32[]{:S(2)}, u32[]{:S(2)}) collective-permute-start(bf16[1024,2,768]{0,2,1:T(8,128)(2,1)} %slice.43), channel_id=1, source_target_pairs={{0,62},{2,0},{4,2},{6,4},{8,6},{10,8},{12,10},{14,12},{16,14},{18,... | collective-permute-start | bytes 9437192 | tf_op jit(solution)/shard_map/ppermute | solution.py:15
  96.1 266.7 %collective-permute-start.3 = (bf16[1024,2,768]{0,2,1:T(8,128)(2,1)}, bf16[1024,2,768]{0,2,1:T(8,128)(2,1)}, u32[]{:S(2)}, u32[]{:S(2)}) collective-permute-start(bf16[1024,2,768]{0,2,1:T(8,128)(2,1)} %slice.43), channel_id=1, source_target_pairs={{0,60},{2,62},{4,0},{6,2},{8,4},{10,6},{12,8},{14,10},{16,12},{18,... | collective-permute-start | bytes 9437192 | tf_op jit(solution)/shard_map/ppermute | solution.py:15
  96.3 135.4 %slice-start = ((s8[4718592]{0:T(1024)(128)(4,1)}), s8[4194304]{0:T(1024)(128)(4,1)S(1)}, s32[]{:S(2)}) async-start(s8[4718592]{0:T(1024)(128)(4,1)} %bitcast.47), calls=%async_computation.4 | async-start | bytes 8388608
  99.1 132.6 %slice-start.1 = ((s8[4718592]{0:T(1024)(128)(4,1)}), s8[524288]{0:T(1024)(128)(4,1)S(1)}, s32[]{:S(2)}) async-start(s8[4718592]{0:T(1024)(128)(4,1)} %bitcast.47), calls=%async_computation.5 | async-start | bytes 1048576
  504.7 108.7 %all-reduce.2.cloned.1.call-start = ((), (), s32[]{:S(2)}) async-start(), calls=%async_computation.3 | async-start | bytes 3145728 | tf_op jit(solution)/shard_map/psum | solution.py:87
Sparse Core Ops, SparseCore 0:
  12.5 51.9 all-gather.1
  504.9 79.0 reduce-scatter.1
  587.5 25.9 all-reduce.1
where the time goes:
time: 624 us; the launch traced here: 622 us
  waiting for transfers between devices  404 us (65%)
  matrix products  80.6 us (13%)
  local copies, waits for them, and re-layouts  69.7 us (11%)
  other arithmetic  41.9 us (7%)
  between operations  13.2 us (2%)
  starting transfers between devices  8.5 us (1%)
    ppermute x4, waiting for transfers between devices, from_behind(): lax.ppermute(array, axis, [(i, (i + by) % count) for i in range(count)])  257 us
    reduce_scatter x1, waiting for transfers between devices, per_device(): lax.psum_scatter(jnp.dot(context, w_out, preferred_element_type=jnp.float...  79.1 us
    all_gather x1, waiting for transfers between devices, per_device(): whole = lax.all_gather(normed, 'tp', axis=0, tiled=True)  41.8 us
    dot_general x6, matrix products, attend_head(): jnp.dot(weights, valueset, preferred_element_type=jnp.float32) / total  32.6 us
    reduce_sum x6, other arithmetic, attend_head(): total = jnp.sum(expon, axis=1, keepdims=True)  30.5 us
    dot_general x6, matrix products, attend_head(): jnp.dot(queries, keyset.T, preferred_element_type=jnp.float32)  29.3 us
    psum x1, waiting for transfers between devices, per_device(): lax.psum((weight_now * branch_out.astype(jnp.float32)).astype(jnp.bfloat1...  26.1 us
    unnamed x13, local copies, waits for them, and re-layouts  17.2 us
  transfers between devices with their start and end apart: 7, of which 6 were waited for; matrix products, arithmetic and copies ran while one was open for 3% of the time, Pallas kernels for 0%

commit v1 on v0

--- a/solution.py
+++ b/solution.py
@@ -48,10 +48,14 @@
     qkv = qkv.astype(jnp.bfloat16).reshape(rows_view, 3, half_heads)
     queries = qkv[:, 0]
     own_pair = qkv[:, 1:]
+    chunks = 2
+    pieces = jnp.split(own_pair, chunks, axis=2)
     received = {}
-    for offset in range(1, REACH + 1):
-        received[offset] = direct_send(own_pair, -offset)
-        received[-offset] = direct_send(own_pair, offset)
+    for sign in (1, -1):
+        near = [direct_send(piece, -sign) for piece in pieces]
+        far = [direct_send(piece, -sign) for piece in near]
+        received[sign] = jnp.concatenate(near, axis=2)
+        received[2 * sign] = jnp.concatenate(far, axis=2)
     received[0] = own_pair
     stacked = jnp.stack([received[offset] for offset in range(-REACH, REACH + 1)], axis=0)
     keyflat = stacked[:, :, 0].reshape((2 * REACH + 1) * rows_view, half_heads)
@@ -74,20 +78,11 @@
 
     heads_out = lax.map(one_head, jnp.arange(half_heads // HEAD_DIM, dtype=jnp.int32))
     context = jnp.transpose(heads_out, (1, 0, 2)).reshape(rows_view, half_heads)
-    summed = lax.psum_scatter(
-        jnp.dot(context, w_out, preferred_element_type=jnp.float32),
-        "tp",
-        scatter_dimension=0,
-        tiled=True,
-    )
-    branch_out = summed.astype(jnp.bfloat16)
+    partial = jnp.dot(context, w_out, preferred_element_type=jnp.float32)
     owner = lax.axis_index("cfg")
-    half_width = width // 2
     weight_now = jnp.where(owner == 0, guide_scale, 1.0 - guide_scale).astype(jnp.float32)
-    combined = lax.psum(
-        (weight_now * branch_out.astype(jnp.float32)).astype(jnp.bfloat16), "cfg"
-    ).astype(jnp.float32)
-    guided = lax.dynamic_slice_in_dim(combined, owner * half_width, half_width, 1)
+    by_columns = lax.psum_scatter(weight_now * partial, "cfg", scatter_dimension=1, tiled=True)
+    guided = lax.psum_scatter(by_columns, "tp", scatter_dimension=0, tiled=True)
     return guided.astype(jnp.bfloat16)[None]
 
 

time: 624 us -> 452 us (0.72)
  waiting for transfers between devices: 404 us -> 233 us
  local copies, waits for them, and re-layouts: 69.7 us -> 59 us
    ppermute x4 -> x8, waiting for transfers between devices: 257 us -> 124 us  [from_behind(): lax.ppermute(array, axis, [(i, (i + by) % count) for i in range(count)])]
    psum x1 -> x0, waiting for transfers between devices: 26.1 us -> none  [per_device(): lax.psum((weight_now * branch_out.astype(jnp.float32)).astype(jnp.bfloat1...]
    reduce_scatter x1 -> x2, waiting for transfers between devices: 79.1 us -> 67.1 us  [the longest x1 50.8 us: per_device(): guided = lax.psum_scatter(by_columns, 'tp', scatter_dimension=0, tiled=True)]
    unnamed x1 -> x4, other arithmetic: 0.01 us -> 6.58 us
    unnamed x13 -> x10, local copies, waits for them, and re-layouts: 17.2 us -> 10.6 us
    ppermute x4 -> x8, starting transfers between devices: 8.41 us -> 13.5 us  [from_behind(): lax.ppermute(array, axis, [(i, (i + by) % count) for i in range(count)])]
  transfers between devices with their start and end apart: 7 -> 11, of which waited for: 6 -> 7; matrix products, arithmetic and copies ran while one was open for 3% -> 4% of each run, Pallas kernels for 0% -> 0%
where the time goes in v1:
time: 452 us; the launch traced here: 451 us
  waiting for transfers between devices  233 us (52%)
  matrix products  80.5 us (18%)
  local copies, waits for them, and re-layouts  59 us (13%)
  other arithmetic  47.6 us (11%)
  starting transfers between devices  13.6 us (3%)
  between operations  13.2 us (3%)
    ppermute x8, waiting for transfers between devices, from_behind(): lax.ppermute(array, axis, [(i, (i + by) % count) for i in range(count)])  124 us
    reduce_scatter x1, waiting for transfers between devices, per_device(): guided = lax.psum_scatter(by_columns, 'tp', scatter_dimension=0, tiled=True)  50.8 us
    all_gather x1, waiting for transfers between devices, per_device(): whole = lax.all_gather(normed, 'tp', axis=0, tiled=True)  41.8 us
    dot_general x6, matrix products, attend_head(): jnp.dot(weights, valueset, preferred_element_type=jnp.float32) / total  32.6 us
    reduce_sum x6, other arithmetic, attend_head(): total = jnp.sum(expon, axis=1, keepdims=True)  30.5 us
    dot_general x6, matrix products, attend_head(): jnp.dot(queries, keyset.T, preferred_element_type=jnp.float32)  29.3 us
    slice x2, local copies, waits for them, and re-layouts, per_device(): valflat = stacked[:, :, 1].reshape((2 * REACH + 1) * rows_view, half_heads)  16.5 us
    reduce_scatter x1, waiting for transfers between devices, per_device(): lax.psum_scatter(weight_now * partial, 'cfg', scatter_dimension=1, tiled=...  16.3 us
  transfers between devices with their start and end apart: 11, of which 7 were waited for; matrix products, arithmetic and copies ran while one was open for 4% of the time, Pallas kernels for 0%

profile of v1, /device:TPU:1, one launch (start us, length us, event | category | flops | bytes accessed | tf_op | source)
XLA Modules:
  0.0 450.9 jit_solution(16324541657179550504)
XLA Ops:
  12.5 10.3 %copy.7 = bf16[1536,3,768]{0,2,1:T(8,128)(2,1)} copy(bf16[1536,3,768]{2,0,1:T(8,128)(2,1)} %param.9) | data formatting | bytes 14155776 | tf_op args[2]
  22.8 41.8 %all-gather.2.cloned.1.call-done = bf16[1024,1536]{1,0:T(8,128)(2,1)} async-done(((bf16[512,1536]{1,0:T(8,128)(2,1)}), bf16[1024,1536]{1,0:T(8,128)(2,1)}) %all-gather.2.cloned.1.call-update) | async-done | bytes 3145744 | tf_op jit(solution)/shard_map/all_gather | solution.py:45
  64.5 12.6 %convolution_convert_fusion = bf16[1024,2304]{1,0:T(8,128)(2,1)} fusion(bf16[1024,1536]{1,0:T(8,128)(2,1)} %all-gather.2.cloned.1.call-done, bf16[1536,2304]{0,1:T(8,128)(2,1)} %bitcast.62), kind=kOutput, calls=%fused_computation.21 | convolution fusion | flops 7250116608 | bytes 14942208 | tf_op jit(solution)/shard_map/dot_general | solution.py:47
  77.1 6.6 %copy.8 = bf16[1024,2304]{0,1:T(8,128)(2,1)} copy(bf16[1024,2304]{1,0:T(8,128)(2,1)} %convolution_convert_fusion) | data formatting | bytes 9437184 | tf_op jit(solution)/shard_map/convert_element_type | solution.py:48
  93.2 32.3 %collective-permute-done = bf16[1024,2,384]{0,2,1:T(8,128)(2,1)} collective-permute-done((bf16[1024,2,384]{0,2,1:T(8,128)(2,1)S(1)}, bf16[1024,2,384]{0,2,1:T(8,128)(2,1)}, u32[]{:S(2)}, u32[]{:S(2)}) %collective-permute-start) | collective-permute-done | bytes 1572896 | tf_op jit(solution)/shard_map/ppermute | solution.py:15
  125.5 33.7 %collective-permute-done.2 = bf16[1024,2,384]{0,2,1:T(8,128)(2,1)} collective-permute-done((bf16[1024,2,384]{0,2,1:T(8,128)(2,1)S(1)}, bf16[1024,2,384]{0,2,1:T(8,128)(2,1)}, u32[]{:S(2)}, u32[]{:S(2)}) %collective-permute-start.2) | collective-permute-done | bytes 1572896 | tf_op jit(solution)/shard_map/ppermute | solution.py:15
  159.2 5.7 %collective-permute-start.6 = (bf16[1024,2,384]{0,2,1:T(8,128)(2,1)}, bf16[1024,2,384]{0,2,1:T(8,128)(2,1)}, u32[]{:S(2)}, u32[]{:S(2)}) collective-permute-start(bf16[1024,2,384]{0,2,1:T(8,128)(2,1)} %collective-permute-done.4), channel_id=1, source_target_pairs={{0,62},{2,0},{4,2},{6,4},{8,6},{10,8},{12,10},{14,12},{16,14},{18,... | collective-permute-start | bytes 4718600 | tf_op jit(solution)/shard_map/ppermute | solution.py:15
  168.6 24.4 %collective-permute-done.1 = bf16[1024,2,384]{0,2,1:T(8,128)(2,1)} collective-permute-done((bf16[1024,2,384]{0,2,1:T(8,128)(2,1)}, bf16[1024,2,384]{0,2,1:T(8,128)(2,1)}, u32[]{:S(2)}, u32[]{:S(2)}) %collective-permute-start.1) | collective-permute-done | bytes 1572896 | tf_op jit(solution)/shard_map/ppermute | solution.py:15
  192.9 33.7 %collective-permute-done.3 = bf16[1024,2,384]{0,2,1:T(8,128)(2,1)} collective-permute-done((bf16[1024,2,384]{0,2,1:T(8,128)(2,1)}, bf16[1024,2,384]{0,2,1:T(8,128)(2,1)}, u32[]{:S(2)}, u32[]{:S(2)}) %collective-permute-start.3) | collective-permute-done | bytes 1572896 | tf_op jit(solution)/shard_map/ppermute | solution.py:15
  235.8 6.1 %fusion.40 = (bf16[5,1024,1,768]{1,3,2,0:T(8,128)(2,1)}, bf16[5,1024,1,768]{1,3,2,0:T(8,128)(2,1)}) fusion(bf16[5,1024,2,768]{1,3,2,0:T(8,128)(2,1)S(1)} %fusion.39), kind=kLoop, calls=%fused_computation.47 | loop fusion | bytes 31457280 | tf_op jit(solution)/shard_map/slice | solution.py:62
  241.8 10.7 %copy.9 = bf16[5,1024,1,768]{3,1,0,2:T(8,128)(2,1)} copy(bf16[5,1024,1,768]{1,3,2,0:T(8,128)(2,1)} %get-tuple-element.86) | data formatting | bytes 15728640 | tf_op jit(solution)/shard_map/slice | solution.py:61
  252.5 10.5 %copy.10 = bf16[5,1024,1,768]{3,1,0,2:T(8,128)(2,1)} copy(bf16[5,1024,1,768]{1,3,2,0:T(8,128)(2,1)} %get-tuple-element.85) | data formatting | bytes 15728640 | tf_op jit(solution)/shard_map/slice | solution.py:62
  263.0 105.8 %while.11 = (s32[]{:T(128)}, bf16[6,1024,128]{1,2,0:T(8,128)(2,1)}, s32[6]{0:T(128)S(1)}, bf16[1024,768]{0,1:T(8,128)(2,1)}, bf16[5120,768]{1,0:T(8,128)(2,1)}, ...) while((s32[]{:T(128)}, bf16[6,1024,128]{1,2,0:T(8,128)(2,1)}, ...), condition=%wide.region_4.5_spmd.clone, body=%wide.region_1.4_spmd.clone.sunk | while | flops 2742286336 | bytes 67151568 | solution.py:79
  269.2 5.1 %fusion.54 = f32[1024]{0:T(1024)S(1)} fusion(f32[1024,5120]{1,0:T(8,128)S(1)} %get-tuple-element.136, f32[1024]{0:T(1024)S(1)} %get-tuple-element.137, pred[5120]{0:T(1024)(128)(4,1)S(1)} %broadcast_bitcast_fusion.2), kind=kLoop, calls=%fused_computation.4.clone.1 | loop fusion | flops 20970496 | bytes 20984832 | tf_op jit(solution)/shard_map/while/body/eval_jaxpr/reduce_sum | solution.py:25
  274.3 5.4 %fusion.55 = bf16[1,1024,128]{2,1,0:T(8,128)(2,1)S(1)} fusion(bf16[5120,768]{1,0:T(8,128)(2,1)} %get-tuple-element.165, s32[]{:T(128)S(6)} %select_n.39, f32[1024,5120]{1,0:T(8,128)S(1)} %get-tuple-element.136, f32[1024]{0:T(1024)S(1)} %get-tuple-element.137, pred[5120]{0:T(1024)(128)(4,1)S(1)} %broadcast_bitcast_fusion.2, f32[1024]{0:T(1024)S(1)} %fusion.54), kind=kOutput, calls=%fused_computation.13.clone.1 | convolution fusion | flops 1363410944 | bytes 22557700 | tf_op jit(solution)/shard_map/while/body/eval_jaxpr/dot_general | solution.py:27
  286.8 5.1 %fusion.54 = f32[1024]{0:T(1024)S(1)} fusion(f32[1024,5120]{1,0:T(8,128)S(1)} %get-tuple-element.136, f32[1024]{0:T(1024)S(1)} %get-tuple-element.137, pred[5120]{0:T(1024)(128)(4,1)S(1)} %broadcast_bitcast_fusion.2), kind=kLoop, calls=%fused_computation.4.clone.1 | loop fusion | flops 20970496 | bytes 20984832 | tf_op jit(solution)/shard_map/while/body/eval_jaxpr/reduce_sum | solution.py:25
  291.9 5.4 %fusion.55 = bf16[1,1024,128]{2,1,0:T(8,128)(2,1)S(1)} fusion(bf16[5120,768]{1,0:T(8,128)(2,1)} %get-tuple-element.165, s32[]{:T(128)S(6)} %select_n.39, f32[1024,5120]{1,0:T(8,128)S(1)} %get-tuple-element.136, f32[1024]{0:T(1024)S(1)} %get-tuple-element.137, pred[5120]{0:T(1024)(128)(4,1)S(1)} %broadcast_bitcast_fusion.2, f32[1024]{0:T(1024)S(1)} %fusion.54), kind=kOutput, calls=%fused_computation.13.clone.1 | convolution fusion | flops 1363410944 | bytes 22557700 | tf_op jit(solution)/shard_map/while/body/eval_jaxpr/dot_general | solution.py:27
  309.6 5.4 %fusion.55 = bf16[1,1024,128]{2,1,0:T(8,128)(2,1)S(1)} fusion(bf16[5120,768]{1,0:T(8,128)(2,1)} %get-tuple-element.165, s32[]{:T(128)S(6)} %select_n.39, f32[1024,5120]{1,0:T(8,128)S(1)} %get-tuple-element.136, f32[1024]{0:T(1024)S(1)} %get-tuple-element.137, pred[5120]{0:T(1024)(128)(4,1)S(1)} %broadcast_bitcast_fusion.2, f32[1024]{0:T(1024)S(1)} %fusion.54), kind=kOutput, calls=%fused_computation.13.clone.1 | convolution fusion | flops 1363410944 | bytes 22557700 | tf_op jit(solution)/shard_map/while/body/eval_jaxpr/dot_general | solution.py:27
  327.2 5.4 %fusion.55 = bf16[1,1024,128]{2,1,0:T(8,128)(2,1)S(1)} fusion(bf16[5120,768]{1,0:T(8,128)(2,1)} %get-tuple-element.165, s32[]{:T(128)S(6)} %select_n.39, f32[1024,5120]{1,0:T(8,128)S(1)} %get-tuple-element.136, f32[1024]{0:T(1024)S(1)} %get-tuple-element.137, pred[5120]{0:T(1024)(128)(4,1)S(1)} %broadcast_bitcast_fusion.2, f32[1024]{0:T(1024)S(1)} %fusion.54), kind=kOutput, calls=%fused_computation.13.clone.1 | convolution fusion | flops 1363410944 | bytes 22557700 | tf_op jit(solution)/shard_map/while/body/eval_jaxpr/dot_general | solution.py:27
  344.9 5.4 %fusion.55 = bf16[1,1024,128]{2,1,0:T(8,128)(2,1)S(1)} fusion(bf16[5120,768]{1,0:T(8,128)(2,1)} %get-tuple-element.165, s32[]{:T(128)S(6)} %select_n.39, f32[1024,5120]{1,0:T(8,128)S(1)} %get-tuple-element.136, f32[1024]{0:T(1024)S(1)} %get-tuple-element.137, pred[5120]{0:T(1024)(128)(4,1)S(1)} %broadcast_bitcast_fusion.2, f32[1024]{0:T(1024)S(1)} %fusion.54), kind=kOutput, calls=%fused_computation.13.clone.1 | convolution fusion | flops 1363410944 | bytes 22557700 | tf_op jit(solution)/shard_map/while/body/eval_jaxpr/dot_general | solution.py:27
  362.5 5.4 %fusion.55 = bf16[1,1024,128]{2,1,0:T(8,128)(2,1)S(1)} fusion(bf16[5120,768]{1,0:T(8,128)(2,1)} %get-tuple-element.165, s32[]{:T(128)S(6)} %select_n.39, f32[1024,5120]{1,0:T(8,128)S(1)} %get-tuple-element.136, f32[1024]{0:T(1024)S(1)} %get-tuple-element.137, pred[5120]{0:T(1024)(128)(4,1)S(1)} %broadcast_bitcast_fusion.2, f32[1024]{0:T(1024)S(1)} %fusion.54), kind=kOutput, calls=%fused_computation.13.clone.1 | convolution fusion | flops 1363410944 | bytes 22557700 | tf_op jit(solution)/shard_map/while/body/eval_jaxpr/dot_general | solution.py:27
  368.8 6.0 %convolution_multiply_fusion = f32[1024,1536]{1,0:T(8,128)} fusion(bf16[1024,768]{0,1:T(8,128)(2,1)} %bitcast.63, bf16[768,1536]{1,0:T(8,128)(2,1)S(1)} %copy-done, f32[]{:T(128)S(6)} %select_n.13), kind=kOutput, calls=%fused_computation.22 | convolution fusion | flops 2417491968 | bytes 10223620 | tf_op jit(solution)/shard_map/dot_general | solution.py:81
  374.9 16.3 %reduce-scatter.3.cloned.1.call-done = f32[1024,768]{1,0:T(8,128)} async-done(((f32[1024,1536]{1,0:T(8,128)}), f32[1024,768]{1,0:T(8,128)}) %reduce-scatter.3.cloned.1.call-update) | async-done | bytes 3145744 | tf_op jit(solution)/shard_map/reduce_scatter | solution.py:84
  391.2 50.8 %reduce-scatter.5.cloned.1.call-done = f32[512,768]{1,0:T(8,128)} async-done(((f32[1024,768]{1,0:T(8,128)}), f32[512,768]{1,0:T(8,128)}) %reduce-scatter.5.cloned.1.call-update) | async-done | bytes 1572880 | tf_op jit(solution)/shard_map/reduce_scatter | solution.py:85
  (77 shorter events, 89.6 us)
Async XLA Ops:
  6.5 362.3 %copy-start = (bf16[768,1536]{1,0:T(8,128)(2,1)S(1)}, bf16[768,1536]{1,0:T(8,128)(2,1)}, u32[]{:S(2)}) copy-start(bf16[768,1536]{1,0:T(8,128)(2,1)} %param.10) | copy-start | bytes 7077892
  6.5 58.0 %all-gather.2.cloned.1.call-start = ((), (), s32[]{:S(2)}) async-start(), calls=%async_computation.2 | async-start | bytes 4718592 | tf_op jit(solution)/shard_map/all_gather | solution.py:45
  12.4 378.7 %reduce-scatter.3.cloned.1.call-start = ((), (), s32[]{:S(2)}) async-start(), calls=%async_computation.3 | async-start | bytes 9437184 | tf_op jit(solution)/shard_map/reduce_scatter | solution.py:84
  83.8 81.8 %copy-start.1 = (s32[1,4,8]{2,1,0:T(4,128)S(1)}, s32[1,4,8]{2,1,0:T(4,128)}, u32[]{:S(2)}) copy-start(s32[1,4,8]{2,1,0:T(4,128)} %param.11) | copy-start | bytes 388
  86.0 39.5 %collective-permute-start = (bf16[1024,2,384]{0,2,1:T(8,128)(2,1)S(1)}, bf16[1024,2,384]{0,2,1:T(8,128)(2,1)}, u32[]{:S(2)}, u32[]{:S(2)}) collective-permute-start(bf16[1024,2,384]{0,2,1:T(8,128)(2,1)S(1)} %get-tuple-element.87), channel_id=1, source_target_pairs={{0,2},{2,4},{4,6},{6,8},{8,10},{10,12},{12,14},{14,16},{16,18},{18... | collective-permute-start | bytes 4718600 | tf_op jit(solution)/shard_map/ppermute | solution.py:15
  87.3 71.9 %collective-permute-start.2 = (bf16[1024,2,384]{0,2,1:T(8,128)(2,1)S(1)}, bf16[1024,2,384]{0,2,1:T(8,128)(2,1)}, u32[]{:S(2)}, u32[]{:S(2)}) collective-permute-start(bf16[1024,2,384]{0,2,1:T(8,128)(2,1)S(1)} %get-tuple-element.88), channel_id=1, source_target_pairs={{0,2},{2,4},{4,6},{6,8},{8,10},{10,12},{12,14},{14,16},{16,18},{18... | collective-permute-start | bytes 4718600 | tf_op jit(solution)/shard_map/ppermute | solution.py:15
  88.5 70.7 %collective-permute-start.4 = (bf16[1024,2,384]{0,2,1:T(8,128)(2,1)S(1)}, bf16[1024,2,384]{0,2,1:T(8,128)(2,1)}, u32[]{:S(2)}, u32[]{:S(2)}) collective-permute-start(bf16[1024,2,384]{0,2,1:T(8,128)(2,1)S(1)} %get-tuple-element.87), channel_id=1, source_target_pairs={{0,62},{2,0},{4,2},{6,4},{8,6},{10,8},{12,10},{14,12},{16,14},{18,... | collective-permute-start | bytes 4718600 | tf_op jit(solution)/shard_map/ppermute | solution.py:15
  93.0 71.9 %collective-permute-start.5 = (bf16[1024,2,384]{0,2,1:T(8,128)(2,1)S(1)}, bf16[1024,2,384]{0,2,1:T(8,128)(2,1)}, u32[]{:S(2)}, u32[]{:S(2)}) collective-permute-start(bf16[1024,2,384]{0,2,1:T(8,128)(2,1)S(1)} %get-tuple-element.88), channel_id=1, source_target_pairs={{0,62},{2,0},{4,2},{6,4},{8,6},{10,8},{12,10},{14,12},{16,14},{18,... | collective-permute-start | bytes 4718600 | tf_op jit(solution)/shard_map/ppermute | solution.py:15
  125.5 67.4 %collective-permute-start.1 = (bf16[1024,2,384]{0,2,1:T(8,128)(2,1)}, bf16[1024,2,384]{0,2,1:T(8,128)(2,1)}, u32[]{:S(2)}, u32[]{:S(2)}) collective-permute-start(bf16[1024,2,384]{0,2,1:T(8,128)(2,1)} %collective-permute-done), channel_id=1, source_target_pairs={{0,2},{2,4},{4,6},{6,8},{8,10},{10,12},{12,14},{14,16},{16,18},{18... | collective-permute-start | bytes 4718600 | tf_op jit(solution)/shard_map/ppermute | solution.py:15
  159.2 67.4 %collective-permute-start.3 = (bf16[1024,2,384]{0,2,1:T(8,128)(2,1)}, bf16[1024,2,384]{0,2,1:T(8,128)(2,1)}, u32[]{:S(2)}, u32[]{:S(2)}) collective-permute-start(bf16[1024,2,384]{0,2,1:T(8,128)(2,1)} %collective-permute-done.2), channel_id=1, source_target_pairs={{0,2},{2,4},{4,6},{6,8},{8,10},{10,12},{12,14},{14,16},{16,18},{18... | collective-permute-start | bytes 4718600 | tf_op jit(solution)/shard_map/ppermute | solution.py:15
  159.2 74.3 %collective-permute-start.6 = (bf16[1024,2,384]{0,2,1:T(8,128)(2,1)}, bf16[1024,2,384]{0,2,1:T(8,128)(2,1)}, u32[]{:S(2)}, u32[]{:S(2)}) collective-permute-start(bf16[1024,2,384]{0,2,1:T(8,128)(2,1)} %collective-permute-done.4), channel_id=1, source_target_pairs={{0,62},{2,0},{4,2},{6,4},{8,6},{10,8},{12,10},{14,12},{16,14},{18,... | collective-permute-start | bytes 4718600 | tf_op jit(solution)/shard_map/ppermute | solution.py:15
  164.9 68.7 %collective-permute-start.7 = (bf16[1024,2,384]{0,2,1:T(8,128)(2,1)}, bf16[1024,2,384]{0,2,1:T(8,128)(2,1)}, u32[]{:S(2)}, u32[]{:S(2)}) collective-permute-start(bf16[1024,2,384]{0,2,1:T(8,128)(2,1)} %collective-permute-done.5), channel_id=1, source_target_pairs={{0,62},{2,0},{4,2},{6,4},{8,6},{10,8},{12,10},{14,12},{16,14},{18,... | collective-permute-start | bytes 4718600 | tf_op jit(solution)/shard_map/ppermute | solution.py:15
  165.7 65.3 %slice-start = ((s8[4718592]{0:T(1024)(128)(4,1)}), s8[4194304]{0:T(1024)(128)(4,1)S(1)}, s32[]{:S(2)}) async-start(s8[4718592]{0:T(1024)(128)(4,1)} %bitcast.57), calls=%async_computation.5 | async-start | bytes 8388608
  168.5 62.5 %slice-start.1 = ((s8[4718592]{0:T(1024)(128)(4,1)}), s8[524288]{0:T(1024)(128)(4,1)S(1)}, s32[]{:S(2)}) async-start(s8[4718592]{0:T(1024)(128)(4,1)} %bitcast.57), calls=%async_computation.6 | async-start | bytes 1048576
  374.8 67.1 %reduce-scatter.5.cloned.1.call-start = ((), (), s32[]{:S(2)}) async-start(), calls=%async_computation.4 | async-start | bytes 4718592 | tf_op jit(solution)/shard_map/reduce_scatter | solution.py:85
Sparse Core Ops, SparseCore 0:
  12.6 51.9 all-gather.1
  375.0 16.1 reduce-scatter.2
  393.5 48.4 reduce-scatter.4

commit v2 on v1

v2 whole, which is shorter than its diff:
```python
import functools

import jax
import jax.numpy as jnp
from jax import lax
from jax.experimental import pallas as pl
from jax.experimental.pallas import tpu as pltpu
from jax.sharding import PartitionSpec as P

HEAD_DIM = 128
REACH = 2
BLOCK = 128


guide_scale = 4.0


def from_behind(array, axis, by):
    count = lax.axis_size(axis)
    return lax.ppermute(array, axis, [(i, (i + by) % count) for i in range(count)])


def swap(array, axis):
    return lax.ppermute(array, axis, [(0, 1), (1, 0)])


def stage_kernel(*refs, n_chunks, first, last, masked, scale):
    flags_ref = refs[0]
    q_ref = refs[1]
    chunk_refs = refs[2 : 2 + 2 * n_chunks]
    rest = refs[2 + 2 * n_chunks :]
    if first:
        outs = rest
    else:
        m_in, l_in, acc_in = rest[:3]
        outs = rest[3:]
    q = q_ref[...]
    rows = q.shape[0]
    if first:
        m = jnp.full((rows, 1), -jnp.inf, jnp.float32)
        l = jnp.zeros((rows, 1), jnp.float32)
        acc = jnp.zeros((rows, HEAD_DIM), jnp.float32)
    else:
        m = m_in[:, :1]
        l = l_in[:, :1]
        acc = acc_in[...]
    for index in range(n_chunks):
        keys = chunk_refs[2 * index][...]
        values = chunk_refs[2 * index + 1][...]
        scores = lax.dot_general(
            q, keys, (((1,), (1,)), ((), ())), preferred_element_type=jnp.float32
        ) * scale
        if masked:
            width = keys.shape[0]
            column_block = lax.broadcasted_iota(jnp.int32, (1, width), 1) // BLOCK
            allowed = jnp.zeros((1, width), jnp.int32)
            for block in range(width // BLOCK):
                allowed = jnp.where(
                    column_block == block, flags_ref[index * (width // BLOCK) + block], allowed
                )
            scores = jnp.where(allowed > 0, scores, -1e30)
        m_new = jnp.maximum(m, jnp.max(scores, axis=1, keepdims=True))
        alpha = jnp.exp(m - m_new)
        expon = jnp.exp(scores - m_new)
        l = alpha * l + jnp.sum(expon, axis=1, keepdims=True)
        acc = alpha * acc + jnp.dot(
            expon.astype(jnp.bfloat16), values, preferred_element_type=jnp.float32
        )
        m = m_new
    if last:
        outs[0][...] = (acc / l).astype(outs[0].dtype)
    else:
        outs[0][...] = jnp.broadcast_to(m, outs[0].shape)
        outs[1][...] = jnp.broadcast_to(l, outs[1].shape)
        outs[2][...] = acc


def attend_stage(flags, queries, chunks, carry, *, first, last, masked, heads):
    rows = queries.shape[0]
    n_chunks = len(chunks)
    kernel = functools.partial(
        stage_kernel,
        n_chunks=n_chunks,
        first=first,
        last=last,
        masked=masked,
        scale=HEAD_DIM ** (-0.5),
    )
    q_spec = pl.BlockSpec((rows, HEAD_DIM), lambda h, f: (0, h))
    in_specs = [q_spec]
    operands = [queries]
    for chunk in chunks:
        width = chunk.shape[0]
        in_specs.append(pl.BlockSpec((width, HEAD_DIM), lambda h, f: (0, h)))
        in_specs.append(pl.BlockSpec((width, HEAD_DIM), lambda h, f: (0, heads + h)))
        operands += [chunk, chunk]
    carry_spec = pl.BlockSpec((rows, HEAD_DIM), lambda h, f: (0, h))
    if not first:
        in_specs += [carry_spec] * 3
        operands += list(carry)
    if last:
        out_shape = jax.ShapeDtypeStruct((rows, heads * HEAD_DIM), jnp.bfloat16)
        out_specs = carry_spec
    else:
        out_shape = [jax.ShapeDtypeStruct((rows, heads * HEAD_DIM), jnp.float32)] * 3
        out_specs = [carry_spec] * 3
    return pl.pallas_call(
        kernel,
        out_shape=out_shape,
        grid_spec=pltpu.PrefetchScalarGridSpec(
            num_scalar_prefetch=1,
            grid=(heads,),
            in_specs=in_specs,
            out_specs=out_specs,
        ),
        compiler_params=pltpu.CompilerParams(dimension_semantics=("arbitrary",)),
    )(flags, *operands)


def per_device(tokens, modulation, w_qkv, w_out, adjacency):
    inputs = tokens[0, 0].astype(jnp.float32)
    width = inputs.shape[1]
    half_heads = w_qkv.shape[2]
    heads = half_heads // HEAD_DIM
    shift_scale = modulation[0]
    squares = jnp.mean(inputs * inputs, axis=1, keepdims=True)
    normed = (inputs * lax.rsqrt(squares + 1e-06) * (1.0 + shift_scale[1]) + shift_scale[0]).astype(
        jnp.bfloat16
    )
    half_rows = normed.shape[0]
    partner_normed = swap(normed, "tp")
    flat_w = w_qkv.reshape(width, 3 * half_heads)
    qkv_own = jnp.dot(normed, flat_w, preferred_element_type=jnp.float32).astype(jnp.bfloat16)
    pair_own = qkv_own[:, half_heads:]
    qkv_other = jnp.dot(partner_normed, flat_w, preferred_element_type=jnp.float32).astype(
        jnp.bfloat16
    )
    pair_other = qkv_other[:, half_heads:]
    queries = jnp.concatenate([qkv_own[:, :half_heads], qkv_other[:, :half_heads]], axis=0)

    received = {}
    for sign in (1, -1):
        near = [from_behind(piece, "orbit", -sign) for piece in (pair_own, pair_other)]
        far = [from_behind(piece, "orbit", -sign) for piece in near]
        received[sign] = near
        received[2 * sign] = far

    tp_index = lax.axis_index("tp")
    flags = adjacency[0]
    blocks = flags.shape[1]
    per_chunk = blocks // 2
    own_start = tp_index * per_chunk
    other_start = (1 - tp_index) * per_chunk

    def chunk_flags(offsets):
        rows_of = []
        for offset in offsets:
            row = flags[offset + REACH if offset < 0 else offset + REACH - 1]
            rows_of.append(lax.dynamic_slice_in_dim(row, own_start, per_chunk))
            rows_of.append(lax.dynamic_slice_in_dim(row, other_start, per_chunk))
        return jnp.concatenate(rows_of).astype(jnp.int32)

    no_flags = jnp.ones((2 * per_chunk,), jnp.int32)
    carry = attend_stage(
        no_flags, queries, [pair_own, pair_other], None,
        first=True, last=False, masked=False, heads=heads,
    )
    carry = attend_stage(
        chunk_flags((-1, 1)), queries, received[-1] + received[1], carry,
        first=False, last=False, masked=True, heads=heads,
    )
    context = attend_stage(
        chunk_flags((-2, 2)), queries, received[-2] + received[2], carry,
        first=False, last=True, masked=True, heads=heads,
    )

    owner = lax.axis_index("cfg")
    half_width = width // 2
    weight_now = jnp.where(owner == 0, guide_scale, 1.0 - guide_scale).astype(jnp.float32)
    w_mine = lax.dynamic_slice_in_dim(w_out, owner * half_width, half_width, 1)
    w_theirs = lax.dynamic_slice_in_dim(w_out, (1 - owner) * half_width, half_width, 1)
    theirs = weight_now * jnp.dot(context, w_theirs, preferred_element_type=jnp.float32)
    mine = weight_now * jnp.dot(context, w_mine, preferred_element_type=jnp.float32)
    mine = mine + swap(theirs, "cfg")
    guided = mine[:half_rows] + swap(mine[half_rows:], "tp")
    return guided.astype(jnp.bfloat16)[None]


def solution(mesh):
    return jax.shard_map(
        per_device,
        mesh=mesh,
        in_specs=(
            P("cfg", "orbit", "tp", None),
            P("cfg", None, None),
            P(None, None, "tp"),
            P("tp", None),
            P("orbit", None, None),
        ),
        out_specs=P("orbit", "tp", "cfg"),
        check_vma=False,
    )
```

time: 452 us -> 318 us (0.70)
  Pallas kernels: 0 us -> 138 us
  waiting for transfers between devices: 233 us -> 103 us
  matrix products: 80.5 us -> 20.1 us
  local copies, waits for them, and re-layouts: 59 us -> 12.6 us
  other arithmetic: 47.6 us -> 10.3 us
  starting transfers between devices: 13.6 us -> 34 us
  between operations: 13.2 us -> 0.2 us
    pallas_call x0 -> x3, Pallas kernels: none -> 138 us  [attend_stage(): pl.pallas_call(kernel, out_shape=out_shape, grid_spec=pltpu.PrefetchScala...]
    ppermute x8, waiting for transfers between devices: 124 us -> 55 us  [from_behind(): lax.ppermute(array, axis, [(i, (i + by) % count) for i in range(count)])]
    reduce_scatter x2 -> x0, waiting for transfers between devices: 67.1 us -> none  [the longest x1 50.8 us: per_device(): guided = lax.psum_scatter(by_columns, 'tp', scatter_dimension=0, tiled=True)]
    dot_general x14 -> x4, matrix products: 80.5 us -> 20.1 us  [the longest x1 7.59 us: per_device(): jnp.dot(normed, flat_w, preferred_element_type=jnp.float32)]
    ppermute x0 -> x3, waiting for transfers between devices: none -> 47.7 us  [swap(): return lax.ppermute(array, axis, [(0, 1), (1, 0)])]
    all_gather x1 -> x0, waiting for transfers between devices: 41.8 us -> none  [per_device(): whole = lax.all_gather(normed, 'tp', axis=0, tiled=True)]
    reduce_sum x6 -> x0, other arithmetic: 30.5 us -> none  [attend_head(): total = jnp.sum(expon, axis=1, keepdims=True)]
    slice x4 -> x7, local copies, waits for them, and re-layouts: 27.2 us -> 1.52 us  [the longest x1 1.18 us: per_device(): qkv_other[:, :half_heads]]
  transfers between devices with their start and end apart: 11 -> 11, of which waited for: 7 -> 5; matrix products, arithmetic and copies ran while one was open for 4% -> 10% of each run, Pallas kernels for 0% -> 24%
where the time goes in v2:
time: 318 us
  Pallas kernels  138 us (43%)
  waiting for transfers between devices  103 us (32%)
  starting transfers between devices  34 us (11%)
  matrix products  20.1 us (6%)
  local copies, waits for them, and re-layouts  12.6 us (4%)
  other arithmetic  10.3 us (3%)
    pallas_call x3, Pallas kernels, attend_stage(): pl.pallas_call(kernel, out_shape=out_shape, grid_spec=pltpu.PrefetchScala...  138 us
    ppermute x8, waiting for transfers between devices, from_behind(): lax.ppermute(array, axis, [(i, (i + by) % count) for i in range(count)])  55 us
    ppermute x3, waiting for transfers between devices, swap(): return lax.ppermute(array, axis, [(0, 1), (1, 0)])  47.7 us
    ppermute x8, starting transfers between devices, from_behind(): lax.ppermute(array, axis, [(i, (i + by) % count) for i in range(count)])  25.4 us
    unnamed x17, local copies, waits for them, and re-layouts  10.4 us
    ppermute x3, starting transfers between devices, swap(): return lax.ppermute(array, axis, [(0, 1), (1, 0)])  8.6 us
    dot_general x1, matrix products, per_device(): jnp.dot(normed, flat_w, preferred_element_type=jnp.float32)  7.59 us
  transfers between devices with their start and end apart: 11, of which 5 were waited for; matrix products, arithmetic and copies ran while one was open for 10% of the time, Pallas kernels for 24%

profile of v2, /device:TPU:1, one launch (start us, length us, event | category | flops | bytes accessed | tf_op | source)
XLA Modules:
  0.0 317.6 jit_solution(4823762880142130149)
XLA Ops:
  0.9 1.9 fusion.2
  2.8 1.7 fusion.5
  4.6 3.6 %collective-permute-start = (bf16[512,1536]{1,0:T(8,128)(2,1)}, bf16[512,1536]{1,0:T(8,128)(2,1)}, u32[]{:S(2)}, u32[]{:S(2)}) collective-permute-start(bf16[512,1536]{1,0:T(8,128)(2,1)} %fusion.5), channel_id=1, source_target_pairs={{0,1},{1,0},{2,3},{3,2},{4,5},{5,4},{6,7},{7,6},{8,9},{9,8},{10,11... | collective-permute-start | bytes 4718600 | tf_op jit(solution)/shard_map/ppermute | solution.py:24
  8.1 10.4 %copy.6 = bf16[1536,3,768]{0,2,1:T(8,128)(2,1)} copy(bf16[1536,3,768]{2,0,1:T(8,128)(2,1)} %param.7) | data formatting | bytes 14155776 | tf_op args[2]
  18.5 7.6 %convolution_convert_fusion.1 = bf16[512,2304]{1,0:T(8,128)(2,1)S(1)} fusion(bf16[1536,2304]{0,1:T(8,128)(2,1)} %bitcast.41, bf16[1,1,512,1536]{3,2,1,0:T(8,128)(2,1)} %param.5, f32[1536]{0:T(1024)S(1)} %get-tuple-element.18, f32[1536]{0:T(1024)S(1)} %get-tuple-element.17, f32[512]{0:T(512)S(1)} %add_rsqrt_fusion), kind=kOutput, calls=%fused_computation.1 | convolution fusion | flops 3628990464 | bytes 11024384 | tf_op jit(solution)/shard_map/dot_general | solution.py:133
  27.6 5.0 %collective-permute-start.5 = (bf16[512,1536]{1,0:T(8,128)(2,1)S(1)}, bf16[512,1536]{1,0:T(8,128)(2,1)}, u32[]{:S(2)}, u32[]{:S(2)}) collective-permute-start(bf16[512,1536]{1,0:T(8,128)(2,1)S(1)} %slice.56.refs_2_.refs_3_), channel_id=1, source_target_pairs={{0,62},{2,0},{4,2},{6,4},{8,6},{10,8},{12,10},{14,12},{16,14},{18,... | collective-permute-start | bytes 4718600 | tf_op jit(solution)/shard_map/ppermute | solution.py:20
  32.6 9.5 %collective-permute-done = bf16[512,1536]{1,0:T(8,128)(2,1)} collective-permute-done((bf16[512,1536]{1,0:T(8,128)(2,1)}, bf16[512,1536]{1,0:T(8,128)(2,1)}, u32[]{:S(2)}, u32[]{:S(2)}) %collective-permute-start) | collective-permute-done | bytes 1572896 | tf_op jit(solution)/shard_map/ppermute | solution.py:24
  42.1 5.3 %convolution_convert_fusion = bf16[512,2304]{1,0:T(8,128)(2,1)S(1)} fusion(bf16[512,1536]{1,0:T(8,128)(2,1)} %collective-permute-done, bf16[1536,2304]{0,1:T(8,128)(2,1)S(1)} %bitcast.42), kind=kOutput, calls=%fused_computation | convolution fusion | flops 3625058304 | bytes 11010048 | tf_op jit(solution)/shard_map/dot_general | solution.py:135
  47.6 1.7 collective-permute-start.3
  49.3 5.9 %collective-permute-start.7 = (bf16[512,1536]{1,0:T(8,128)(2,1)S(1)}, bf16[512,1536]{1,0:T(8,128)(2,1)}, u32[]{:S(2)}, u32[]{:S(2)}) collective-permute-start(bf16[512,1536]{1,0:T(8,128)(2,1)S(1)} %slice.57.refs_4_.refs_5_), channel_id=1, source_target_pairs={{0,62},{2,0},{4,2},{6,4},{8,6},{10,8},{12,10},{14,12},{16,14},{18,... | collective-permute-start | bytes 4718600 | tf_op jit(solution)/shard_map/ppermute | solution.py:20
  55.2 26.9 %collective-permute-done.1.refs_2_.refs_3_ = bf16[512,1536]{1,0:T(8,128)(2,1)} collective-permute-done((bf16[512,1536]{1,0:T(8,128)(2,1)S(1)}, bf16[512,1536]{1,0:T(8,128)(2,1)}, u32[]{:S(2)}, u32[]{:S(2)}) %collective-permute-start.1) | collective-permute-done | bytes 1572896 | tf_op jit(solution)/shard_map/ppermute | solution.py:20
  82.2 5.7 %collective-permute-start.6 = (bf16[512,1536]{1,0:T(8,128)(2,1)}, bf16[512,1536]{1,0:T(8,128)(2,1)}, u32[]{:S(2)}, u32[]{:S(2)}) collective-permute-start(bf16[512,1536]{1,0:T(8,128)(2,1)} %collective-permute-done.5.refs_6_.refs_7_), channel_id=1, source_target_pairs={{0,62},{2,0},{4,2},{6,4},{8,6},{10,8},{12,10},{14,12},{16,14},{18,... | collective-permute-start | bytes 4718600 | tf_op jit(solution)/shard_map/ppermute | solution.py:20
  87.9 28.0 %collective-permute-done.3.refs_4_.refs_5_ = bf16[512,1536]{1,0:T(8,128)(2,1)} collective-permute-done((bf16[512,1536]{1,0:T(8,128)(2,1)S(1)}, bf16[512,1536]{1,0:T(8,128)(2,1)}, u32[]{:S(2)}, u32[]{:S(2)}) %collective-permute-start.3) | collective-permute-done | bytes 1572896 | tf_op jit(solution)/shard_map/ppermute | solution.py:20
  115.9 5.7 %collective-permute-start.8 = (bf16[512,1536]{1,0:T(8,128)(2,1)}, bf16[512,1536]{1,0:T(8,128)(2,1)}, u32[]{:S(2)}, u32[]{:S(2)}) collective-permute-start(bf16[512,1536]{1,0:T(8,128)(2,1)} %collective-permute-done.7.refs_8_.refs_9_), channel_id=1, source_target_pairs={{0,62},{2,0},{4,2},{6,4},{8,6},{10,8},{12,10},{14,12},{16,14},{18,... | collective-permute-start | bytes 4718600 | tf_op jit(solution)/shard_map/ppermute | solution.py:20
  126.0 14.0 %shard_map.55 = (f32[1024,768]{1,0:T(8,128)}, f32[1024,768]{1,0:T(8,128)}, f32[1024,768]{1,0:T(8,128)}) custom-call(s32[8]{0:T(128)} %broadcast_1_refs_0_.2.refs_0_, bf16[1024,768]{1,0:T(8,128)(2,1)} %pad_maximum_fusion.refs_1_, bf16[512,1536]{1,0:T(8,128)(2,1)} %copy-done.1, bf16[512,1536]{1,0:T(8,128)(2,1)} %copy-done.1, bf16[512,1536]{1,0:T(8,128)(2,1)} %copy-done.2, ...), custom_call_target="tpu_custom_call" | custom-call | tf_op jit(solution)/shard_map/pallas_call | solution.py:107
  140.0 61.9 %shard_map.56 = (f32[1024,768]{1,0:T(8,128)}, f32[1024,768]{1,0:T(8,128)}, f32[1024,768]{1,0:T(8,128)}) custom-call(s32[16]{0:T(128)} %pad_add_fusion.1.refs_0_, bf16[1024,768]{1,0:T(8,128)(2,1)} %pad_maximum_fusion.refs_1_, bf16[512,1536]{1,0:T(8,128)(2,1)} %collective-permute-done.1.refs_2_.refs_3_, ...), custom_call_target="tpu_custom_call" | custom-call | tf_op jit(solution)/shard_map/pallas_call | solution.py:107
  202.0 61.7 %shard_map.57 = bf16[1024,768]{1,0:T(8,128)(2,1)} custom-call(s32[16]{0:T(128)} %pad_add_fusion.refs_0_, bf16[1024,768]{1,0:T(8,128)(2,1)} %pad_maximum_fusion.refs_1_, bf16[512,1536]{1,0:T(8,128)(2,1)} %collective-permute-done.2.refs_2_.refs_3_, bf16[512,1536]{1,0:T(8,128)(2,1)} %collective-permute-done.2.refs_2_.refs_3_, ...), custom_call_target="tpu_custom_call" | custom-call | tf_op jit(solution)/shard_map/pallas_call | solution.py:107
  263.7 4.4 %convolution_multiply_fusion = f32[1024,768]{1,0:T(8,128)} fusion(bf16[1024,768]{1,0:T(8,128)(2,1)} %shard_map.57, f32[]{:T(128)S(6)} %select_n.22, bf16[768,1536]{1,0:T(8,128)(2,1)S(1)} %copy-done, s32[]{:T(128)S(6)} %select_n.26), kind=kOutput, calls=%fused_computation.14 | convolution fusion | flops 1208745984 | bytes 5898248 | tf_op jit(solution)/shard_map/dot_general | solution.py:182
  268.1 3.2 %collective-permute-start.9 = (f32[1024,768]{1,0:T(8,128)}, f32[1024,768]{1,0:T(8,128)}, u32[]{:S(2)}, u32[]{:S(2)}) collective-permute-start(f32[1024,768]{1,0:T(8,128)} %convolution_multiply_fusion), channel_id=1, source_target_pairs={{0,64},{64,0},{1,65},{65,1},{2,66},{66,2},{3,67},{67,3},{4,68},{68... | collective-permute-start | bytes 9437192 | tf_op jit(solution)/shard_map/ppermute | solution.py:24
  271.4 2.8 fusion.16
  274.2 2.8 collective-permute-done.9
  277.0 2.3 multiply_add_fusion
  279.4 1.8 collective-permute-start.10
  281.2 35.3 %collective-permute-done.10 = f32[512,768]{1,0:T(8,128)S(1)} collective-permute-done((f32[512,768]{1,0:T(8,128)S(1)}, f32[512,768]{1,0:T(8,128)S(1)}, u32[]{:S(2)}, u32[]{:S(2)}) %collective-permute-start.10) | collective-permute-done | bytes 1572896 | tf_op jit(solution)/shard_map/ppermute | solution.py:24
  (41 shorter events, 8.1 us)
Async XLA Ops:
  0.0 263.7 %copy-start = (bf16[768,1536]{1,0:T(8,128)(2,1)S(1)}, bf16[768,1536]{1,0:T(8,128)(2,1)}, u32[]{:S(2)}) copy-start(bf16[768,1536]{1,0:T(8,128)(2,1)} %param.8) | copy-start | bytes 7077892
  0.0 2.8 copy-start.4
  4.6 37.6 %collective-permute-start = (bf16[512,1536]{1,0:T(8,128)(2,1)}, bf16[512,1536]{1,0:T(8,128)(2,1)}, u32[]{:S(2)}, u32[]{:S(2)}) collective-permute-start(bf16[512,1536]{1,0:T(8,128)(2,1)} %fusion.5), channel_id=1, source_target_pairs={{0,1},{1,0},{2,3},{3,2},{4,5},{5,4},{6,7},{7,6},{8,9},{9,8},{10,11... | collective-permute-start | bytes 4718600 | tf_op jit(solution)/shard_map/ppermute | solution.py:24
  18.5 23.7 %copy-start.3 = (bf16[1536,3,768]{0,2,1:T(8,128)(2,1)S(1)}, bf16[1536,3,768]{0,2,1:T(8,128)(2,1)}, u32[]{:S(2)}) copy-start(bf16[1536,3,768]{0,2,1:T(8,128)(2,1)} %copy.6) | copy-start | bytes 21233668
  26.1 21.4 %copy-start.5 = (bf16[512,2304]{1,0:T(8,128)(2,1)}, bf16[512,2304]{1,0:T(8,128)(2,1)S(1)}, u32[]{:S(2)}) copy-start(bf16[512,2304]{1,0:T(8,128)(2,1)S(1)} %convolution_convert_fusion.1) | copy-start | bytes 7077892
  26.2 21.2 %copy-start.1 = (bf16[512,1536]{1,0:T(8,128)(2,1)}, bf16[512,1536]{1,0:T(8,128)(2,1)S(1)}, u32[]{:S(2)}) copy-start(bf16[512,1536]{1,0:T(8,128)(2,1)S(1)} %slice.56.refs_2_.refs_3_) | copy-start | bytes 4718596
  26.2 56.0 %collective-permute-start.1 = (bf16[512,1536]{1,0:T(8,128)(2,1)S(1)}, bf16[512,1536]{1,0:T(8,128)(2,1)}, u32[]{:S(2)}, u32[]{:S(2)}) collective-permute-start(bf16[512,1536]{1,0:T(8,128)(2,1)S(1)} %slice.56.refs_2_.refs_3_), channel_id=1, source_target_pairs={{0,2},{2,4},{4,6},{6,8},{8,10},{10,12},{12,14},{14,16},{16,18},{18... | collective-permute-start | bytes 4718600 | tf_op jit(solution)/shard_map/ppermute | solution.py:20
  27.6 54.6 %collective-permute-start.5 = (bf16[512,1536]{1,0:T(8,128)(2,1)S(1)}, bf16[512,1536]{1,0:T(8,128)(2,1)}, u32[]{:S(2)}, u32[]{:S(2)}) collective-permute-start(bf16[512,1536]{1,0:T(8,128)(2,1)S(1)} %slice.56.refs_2_.refs_3_), channel_id=1, source_target_pairs={{0,62},{2,0},{4,2},{6,4},{8,6},{10,8},{12,10},{14,12},{16,14},{18,... | collective-permute-start | bytes 4718600 | tf_op jit(solution)/shard_map/ppermute | solution.py:20
  47.5 68.4 %copy-start.6 = (bf16[512,2304]{1,0:T(8,128)(2,1)}, bf16[512,2304]{1,0:T(8,128)(2,1)S(1)}, u32[]{:S(2)}) copy-start(bf16[512,2304]{1,0:T(8,128)(2,1)S(1)} %convolution_convert_fusion) | copy-start | bytes 7077892
  47.5 74.1 %copy-start.7 = (s32[1,4,8]{2,1,0:T(4,128)S(1)}, s32[1,4,8]{2,1,0:T(4,128)}, u32[]{:S(2)}) copy-start(s32[1,4,8]{2,1,0:T(4,128)} %param.9) | copy-start | bytes 388
  47.6 34.6 %copy-start.2 = (bf16[512,1536]{1,0:T(8,128)(2,1)}, bf16[512,1536]{1,0:T(8,128)(2,1)S(1)}, u32[]{:S(2)}) copy-start(bf16[512,1536]{1,0:T(8,128)(2,1)S(1)} %slice.57.refs_4_.refs_5_) | copy-start | bytes 4718596
  47.6 76.5 %slice-start = ((bf16[512,2304]{1,0:T(8,128)(2,1)}), bf16[512,768]{1,0:T(8,128)(2,1)S(1)}, s32[]{:S(2)}) async-start(bf16[512,2304]{1,0:T(8,128)(2,1)} %copy-done.5), calls=%async_computation | async-start | bytes 1572864 | tf_op jit(solution)/shard_map/slice | solution.py:139
  47.6 68.3 %collective-permute-start.3 = (bf16[512,1536]{1,0:T(8,128)(2,1)S(1)}, bf16[512,1536]{1,0:T(8,128)(2,1)}, u32[]{:S(2)}, u32[]{:S(2)}) collective-permute-start(bf16[512,1536]{1,0:T(8,128)(2,1)S(1)} %slice.57.refs_4_.refs_5_), channel_id=1, source_target_pairs={{0,2},{2,4},{4,6},{6,8},{8,10},{10,12},{12,14},{14,16},{16,18},{18... | collective-permute-start | bytes 4718600 | tf_op jit(solution)/shard_map/ppermute | solution.py:20
  49.3 66.6 %collective-permute-start.7 = (bf16[512,1536]{1,0:T(8,128)(2,1)S(1)}, bf16[512,1536]{1,0:T(8,128)(2,1)}, u32[]{:S(2)}, u32[]{:S(2)}) collective-permute-start(bf16[512,1536]{1,0:T(8,128)(2,1)S(1)} %slice.57.refs_4_.refs_5_), channel_id=1, source_target_pairs={{0,62},{2,0},{4,2},{6,4},{8,6},{10,8},{12,10},{14,12},{16,14},{18,... | collective-permute-start | bytes 4718600 | tf_op jit(solution)/shard_map/ppermute | solution.py:20
  82.2 119.7 %collective-permute-start.2 = (bf16[512,1536]{1,0:T(8,128)(2,1)}, bf16[512,1536]{1,0:T(8,128)(2,1)}, u32[]{:S(2)}, u32[]{:S(2)}) collective-permute-start(bf16[512,1536]{1,0:T(8,128)(2,1)} %collective-permute-done.1.refs_2_.refs_3_), channel_id=1, source_target_pairs={{0,2},{2,4},{4,6},{6,8},{8,10},{10,12},{12,14},{14,16},{16,18},{18... | collective-permute-start | bytes 4718600 | tf_op jit(solution)/shard_map/ppermute | solution.py:20
  82.2 119.7 %collective-permute-start.6 = (bf16[512,1536]{1,0:T(8,128)(2,1)}, bf16[512,1536]{1,0:T(8,128)(2,1)}, u32[]{:S(2)}, u32[]{:S(2)}) collective-permute-start(bf16[512,1536]{1,0:T(8,128)(2,1)} %collective-permute-done.5.refs_6_.refs_7_), channel_id=1, source_target_pairs={{0,62},{2,0},{4,2},{6,4},{8,6},{10,8},{12,10},{14,12},{16,14},{18,... | collective-permute-start | bytes 4718600 | tf_op jit(solution)/shard_map/ppermute | solution.py:20
  115.9 86.0 %collective-permute-start.4 = (bf16[512,1536]{1,0:T(8,128)(2,1)}, bf16[512,1536]{1,0:T(8,128)(2,1)}, u32[]{:S(2)}, u32[]{:S(2)}) collective-permute-start(bf16[512,1536]{1,0:T(8,128)(2,1)} %collective-permute-done.3.refs_4_.refs_5_), channel_id=1, source_target_pairs={{0,2},{2,4},{4,6},{6,8},{8,10},{10,12},{12,14},{14,16},{16,18},{18... | collective-permute-start | bytes 4718600 | tf_op jit(solution)/shard_map/ppermute | solution.py:20
  115.9 86.0 %collective-permute-start.8 = (bf16[512,1536]{1,0:T(8,128)(2,1)}, bf16[512,1536]{1,0:T(8,128)(2,1)}, u32[]{:S(2)}, u32[]{:S(2)}) collective-permute-start(bf16[512,1536]{1,0:T(8,128)(2,1)} %collective-permute-done.7.refs_8_.refs_9_), channel_id=1, source_target_pairs={{0,62},{2,0},{4,2},{6,4},{8,6},{10,8},{12,10},{14,12},{16,14},{18,... | collective-permute-start | bytes 4718600 | tf_op jit(solution)/shard_map/ppermute | solution.py:20
  268.1 8.8 %collective-permute-start.9 = (f32[1024,768]{1,0:T(8,128)}, f32[1024,768]{1,0:T(8,128)}, u32[]{:S(2)}, u32[]{:S(2)}) collective-permute-start(f32[1024,768]{1,0:T(8,128)} %convolution_multiply_fusion), channel_id=1, source_target_pairs={{0,64},{64,0},{1,65},{65,1},{2,66},{66,2},{3,67},{67,3},{4,68},{68... | collective-permute-start | bytes 9437192 | tf_op jit(solution)/shard_map/ppermute | solution.py:24
  279.4 37.2 %collective-permute-start.10 = (f32[512,768]{1,0:T(8,128)S(1)}, f32[512,768]{1,0:T(8,128)S(1)}, u32[]{:S(2)}, u32[]{:S(2)}) collective-permute-start(f32[512,768]{1,0:T(8,128)S(1)} %slice.59), channel_id=1, source_target_pairs={{0,1},{1,0},{2,3},{3,2},{4,5},{5,4},{6,7},{7,6},{8,9},{9,8},{10,11... | collective-permute-start | bytes 4718600 | tf_op jit(solution)/shard_map/ppermute | solution.py:24

commit v3 on v2

--- a/solution.py
+++ b/solution.py
@@ -25,10 +25,11 @@
 
 
 def stage_kernel(*refs, n_chunks, first, last, masked, scale):
-    flags_ref = refs[0]
-    q_ref = refs[1]
-    chunk_refs = refs[2 : 2 + 2 * n_chunks]
-    rest = refs[2 + 2 * n_chunks :]
+    refs = list(refs)
+    bias_ref = refs.pop(0) if masked else None
+    q_ref = refs.pop(0)
+    chunk_refs = refs[: 2 * n_chunks]
+    rest = refs[2 * n_chunks :]
     if first:
         outs = rest
     else:
@@ -47,18 +48,12 @@
     for index in range(n_chunks):
         keys = chunk_refs[2 * index][...]
         values = chunk_refs[2 * index + 1][...]
+        width = keys.shape[0]
         scores = lax.dot_general(
             q, keys, (((1,), (1,)), ((), ())), preferred_element_type=jnp.float32
         ) * scale
         if masked:
-            width = keys.shape[0]
-            column_block = lax.broadcasted_iota(jnp.int32, (1, width), 1) // BLOCK
-            allowed = jnp.zeros((1, width), jnp.int32)
-            for block in range(width // BLOCK):
-                allowed = jnp.where(
-                    column_block == block, flags_ref[index * (width // BLOCK) + block], allowed
-                )
-            scores = jnp.where(allowed > 0, scores, -1e30)
+            scores = scores + bias_ref[:, index * width : (index + 1) * width]
         m_new = jnp.maximum(m, jnp.max(scores, axis=1, keepdims=True))
         alpha = jnp.exp(m - m_new)
         expon = jnp.exp(scores - m_new)
@@ -75,9 +70,10 @@
         outs[2][...] = acc
 
 
-def attend_stage(flags, queries, chunks, carry, *, first, last, masked, heads):
-    rows = queries.shape[0]
+def attend_stage(queries, chunks, bias, carry, *, first, last, heads, row_block=0, rows=None):
+    rows = queries.shape[0] if rows is None else rows
     n_chunks = len(chunks)
+    masked = bias is not None
     kernel = functools.partial(
         stage_kernel,
         n_chunks=n_chunks,
@@ -86,35 +82,37 @@
         masked=masked,
         scale=HEAD_DIM ** (-0.5),
     )
-    q_spec = pl.BlockSpec((rows, HEAD_DIM), lambda h, f: (0, h))
-    in_specs = [q_spec]
-    operands = [queries]
+    row_spec = pl.BlockSpec((rows, HEAD_DIM), lambda h: (row_block, h))
+    in_specs = []
+    operands = []
+    if masked:
+        in_specs.append(pl.BlockSpec(bias.shape, lambda h: (0, 0)))
+        operands.append(bias)
+    in_specs.append(row_spec)
+    operands.append(queries)
     for chunk in chunks:
         width = chunk.shape[0]
-        in_specs.append(pl.BlockSpec((width, HEAD_DIM), lambda h, f: (0, h)))
-        in_specs.append(pl.BlockSpec((width, HEAD_DIM), lambda h, f: (0, heads + h)))
+        in_specs.append(pl.BlockSpec((width, HEAD_DIM), lambda h: (0, h)))
+        in_specs.append(pl.BlockSpec((width, HEAD_DIM), lambda h: (0, heads + h)))
         operands += [chunk, chunk]
-    carry_spec = pl.BlockSpec((rows, HEAD_DIM), lambda h, f: (0, h))
     if not first:
-        in_specs += [carry_spec] * 3
+        in_specs += [row_spec] * 3
         operands += list(carry)
+    out_spec = pl.BlockSpec((rows, HEAD_DIM), lambda h: (0, h))
     if last:
         out_shape = jax.ShapeDtypeStruct((rows, heads * HEAD_DIM), jnp.bfloat16)
-        out_specs = carry_spec
+        out_specs = out_spec
     else:
         out_shape = [jax.ShapeDtypeStruct((rows, heads * HEAD_DIM), jnp.float32)] * 3
-        out_specs = [carry_spec] * 3
+        out_specs = [out_spec] * 3
     return pl.pallas_call(
         kernel,
         out_shape=out_shape,
-        grid_spec=pltpu.PrefetchScalarGridSpec(
-            num_scalar_prefetch=1,
-            grid=(heads,),
-            in_specs=in_specs,
-            out_specs=out_specs,
-        ),
+        grid=(heads,),
+        in_specs=in_specs,
+        out_specs=out_specs,
         compiler_params=pltpu.CompilerParams(dimension_semantics=("arbitrary",)),
-    )(flags, *operands)
+    )(*operands)
 
 
 def per_device(tokens, modulation, w_qkv, w_out, adjacency):
@@ -152,26 +150,31 @@
     own_start = tp_index * per_chunk
     other_start = (1 - tp_index) * per_chunk
 
-    def chunk_flags(offsets):
+    def chunk_bias(offsets):
         rows_of = []
         for offset in offsets:
             row = flags[offset + REACH if offset < 0 else offset + REACH - 1]
             rows_of.append(lax.dynamic_slice_in_dim(row, own_start, per_chunk))
             rows_of.append(lax.dynamic_slice_in_dim(row, other_start, per_chunk))
-        return jnp.concatenate(rows_of).astype(jnp.int32)
-
-    no_flags = jnp.ones((2 * per_chunk,), jnp.int32)
+        allowed = jnp.repeat(jnp.concatenate(rows_of), BLOCK) > 0
+        return jnp.where(allowed, 0.0, -1e30).astype(jnp.float32)[None, :]
+
     carry = attend_stage(
-        no_flags, queries, [pair_own, pair_other], None,
-        first=True, last=False, masked=False, heads=heads,
+        queries, [pair_own, pair_other], None, None, first=True, last=False, heads=heads
     )
     carry = attend_stage(
-        chunk_flags((-1, 1)), queries, received[-1] + received[1], carry,
-        first=False, last=False, masked=True, heads=heads,
-    )
-    context = attend_stage(
-        chunk_flags((-2, 2)), queries, received[-2] + received[2], carry,
-        first=False, last=True, masked=True, heads=heads,
+        queries, received[-1] + received[1], chunk_bias((-1, 1)), carry,
+        first=False, last=False, heads=heads,
+    )
+    far_chunks = received[-2] + received[2]
+    far_bias = chunk_bias((-2, 2))
+    context_other = attend_stage(
+        queries, far_chunks, far_bias, carry,
+        first=False, last=True, heads=heads, row_block=1, rows=half_rows,
+    )
+    context_own = attend_stage(
+        queries, far_chunks, far_bias, carry,
+        first=False, last=True, heads=heads, row_block=0, rows=half_rows,
     )
 
     owner = lax.axis_index("cfg")
@@ -179,10 +182,13 @@
     weight_now = jnp.where(owner == 0, guide_scale, 1.0 - guide_scale).astype(jnp.float32)
     w_mine = lax.dynamic_slice_in_dim(w_out, owner * half_width, half_width, 1)
     w_theirs = lax.dynamic_slice_in_dim(w_out, (1 - owner) * half_width, half_width, 1)
-    theirs = weight_now * jnp.dot(context, w_theirs, preferred_element_type=jnp.float32)
-    mine = weight_now * jnp.dot(context, w_mine, preferred_element_type=jnp.float32)
-    mine = mine + swap(theirs, "cfg")
-    guided = mine[:half_rows] + swap(mine[half_rows:], "tp")
+
+    def project(context):
+        theirs = weight_now * jnp.dot(context, w_theirs, preferred_element_type=jnp.float32)
+        mine = weight_now * jnp.dot(context, w_mine, preferred_element_type=jnp.float32)
+        return mine + swap(theirs, "cfg")
+
+    guided = project(context_own) + swap(project(context_other), "tp")
     return guided.astype(jnp.bfloat16)[None]
 
 

time: 318 us -> 317 us (level)
  waiting for transfers between devices: 103 us -> 96.7 us
  Pallas kernels: 138 us -> 142 us
    ppermute x3 -> x4, waiting for transfers between devices: 47.7 us -> 42.9 us  [swap(): return lax.ppermute(array, axis, [(0, 1), (1, 0)])]
    pallas_call x3 -> x4, Pallas kernels: 138 us -> 142 us  [attend_stage(): pl.pallas_call(kernel, out_shape=out_shape, grid=(heads,), in_specs=in_sp...]
    unnamed x17 -> x21, local copies, waits for them, and re-layouts: 10.4 us -> 13 us
    dot_general x2 -> x4, matrix products: 7.24 us -> 6.64 us  [the longest x2 5.07 us: project(): jnp.dot(context, w_theirs, preferred_element_type=jnp.float32)]
    ppermute x3 -> x4, starting transfers between devices: 8.6 us -> 8.68 us  [swap(): return lax.ppermute(array, axis, [(0, 1), (1, 0)])]
  transfers between devices with their start and end apart: 11 -> 12, of which waited for: 5 -> 4; matrix products, arithmetic and copies ran while one was open for 10% -> 10% of each run, Pallas kernels for 24% -> 34%
where the time goes in v3:
time: 317 us; the launch traced here: 316 us
  Pallas kernels  142 us (45%)
  waiting for transfers between devices  96.7 us (31%)
  starting transfers between devices  33.8 us (11%)
  matrix products  19.5 us (6%)
  local copies, waits for them, and re-layouts  15.7 us (5%)
  other arithmetic  8.78 us (3%)
    pallas_call x4, Pallas kernels, attend_stage(): pl.pallas_call(kernel, out_shape=out_shape, grid=(heads,), in_specs=in_sp...  142 us
    ppermute x8, waiting for transfers between devices, from_behind(): lax.ppermute(array, axis, [(i, (i + by) % count) for i in range(count)])  53.8 us
    ppermute x4, waiting for transfers between devices, swap(): return lax.ppermute(array, axis, [(0, 1), (1, 0)])  42.9 us
    ppermute x8, starting transfers between devices, from_behind(): lax.ppermute(array, axis, [(i, (i + by) % count) for i in range(count)])  25.1 us
    unnamed x21, local copies, waits for them, and re-layouts  13 us
    ppermute x4, starting transfers between devices, swap(): return lax.ppermute(array, axis, [(0, 1), (1, 0)])  8.68 us
    dot_general x1, matrix products, per_device(): jnp.dot(normed, flat_w, preferred_element_type=jnp.float32)  7.6 us
  transfers between devices with their start and end apart: 12, of which 4 were waited for; matrix products, arithmetic and copies ran while one was open for 10% of the time, Pallas kernels for 34%

profile of v3, /device:TPU:1, one launch (start us, length us, event | category | flops | bytes accessed | tf_op | source)
XLA Modules:
  0.0 316.4 jit_solution(1044250040665859633)
XLA Ops:
  0.9 1.9 fusion.2
  2.8 1.7 fusion.5
  4.5 3.6 %collective-permute-start = (bf16[512,1536]{1,0:T(8,128)(2,1)}, bf16[512,1536]{1,0:T(8,128)(2,1)}, u32[]{:S(2)}, u32[]{:S(2)}) collective-permute-start(bf16[512,1536]{1,0:T(8,128)(2,1)} %fusion.5), channel_id=1, source_target_pairs={{0,1},{1,0},{2,3},{3,2},{4,5},{5,4},{6,7},{7,6},{8,9},{9,8},{10,11... | collective-permute-start | bytes 4718600 | tf_op jit(solution)/shard_map/ppermute | solution.py:24
  8.1 10.3 %copy.6 = bf16[1536,3,768]{0,2,1:T(8,128)(2,1)} copy(bf16[1536,3,768]{2,0,1:T(8,128)(2,1)} %param.7) | data formatting | bytes 14155776 | tf_op args[2]
  18.4 7.6 %convolution_convert_fusion.1 = bf16[512,2304]{1,0:T(8,128)(2,1)S(1)} fusion(bf16[1536,2304]{0,1:T(8,128)(2,1)} %bitcast.45, bf16[1,1,512,1536]{3,2,1,0:T(8,128)(2,1)} %param.5, f32[1536]{0:T(1024)S(1)} %get-tuple-element.18, f32[1536]{0:T(1024)S(1)} %get-tuple-element.17, f32[512]{0:T(512)S(1)} %add_rsqrt_fusion), kind=kOutput, calls=%fused_computation.1 | convolution fusion | flops 3628990464 | bytes 11024384 | tf_op jit(solution)/shard_map/dot_general | solution.py:131
  28.7 4.9 %collective-permute-start.5 = (bf16[512,1536]{1,0:T(8,128)(2,1)S(1)}, bf16[512,1536]{1,0:T(8,128)(2,1)}, u32[]{:S(2)}, u32[]{:S(2)}) collective-permute-start(bf16[512,1536]{1,0:T(8,128)(2,1)S(1)} %slice.48.refs_1_.refs_2_), channel_id=1, source_target_pairs={{0,62},{2,0},{4,2},{6,4},{8,6},{10,8},{12,10},{14,12},{16,14},{18,... | collective-permute-start | bytes 4718600 | tf_op jit(solution)/shard_map/ppermute | solution.py:20
  33.7 8.4 %collective-permute-done = bf16[512,1536]{1,0:T(8,128)(2,1)} collective-permute-done((bf16[512,1536]{1,0:T(8,128)(2,1)}, bf16[512,1536]{1,0:T(8,128)(2,1)}, u32[]{:S(2)}, u32[]{:S(2)}) %collective-permute-start) | collective-permute-done | bytes 1572896 | tf_op jit(solution)/shard_map/ppermute | solution.py:24
  42.1 5.3 %convolution_convert_fusion = bf16[512,2304]{1,0:T(8,128)(2,1)S(1)} fusion(bf16[512,1536]{1,0:T(8,128)(2,1)} %collective-permute-done, bf16[1536,2304]{0,1:T(8,128)(2,1)S(1)} %bitcast.46), kind=kOutput, calls=%fused_computation | convolution fusion | flops 3625058304 | bytes 11010048 | tf_op jit(solution)/shard_map/dot_general | solution.py:133
  48.9 1.6 collective-permute-start.3
  50.5 5.8 %collective-permute-start.7 = (bf16[512,1536]{1,0:T(8,128)(2,1)S(1)}, bf16[512,1536]{1,0:T(8,128)(2,1)}, u32[]{:S(2)}, u32[]{:S(2)}) collective-permute-start(bf16[512,1536]{1,0:T(8,128)(2,1)S(1)} %slice.49.refs_3_.refs_4_), channel_id=1, source_target_pairs={{0,62},{2,0},{4,2},{6,4},{8,6},{10,8},{12,10},{14,12},{16,14},{18,... | collective-permute-start | bytes 4718600 | tf_op jit(solution)/shard_map/ppermute | solution.py:20
  56.4 25.8 %collective-permute-done.1.refs_2_.refs_3_ = bf16[512,1536]{1,0:T(8,128)(2,1)} collective-permute-done((bf16[512,1536]{1,0:T(8,128)(2,1)S(1)}, bf16[512,1536]{1,0:T(8,128)(2,1)}, u32[]{:S(2)}, u32[]{:S(2)}) %collective-permute-start.1) | collective-permute-done | bytes 1572896 | tf_op jit(solution)/shard_map/ppermute | solution.py:20
  82.2 5.7 %collective-permute-start.6 = (bf16[512,1536]{1,0:T(8,128)(2,1)}, bf16[512,1536]{1,0:T(8,128)(2,1)}, u32[]{:S(2)}, u32[]{:S(2)}) collective-permute-start(bf16[512,1536]{1,0:T(8,128)(2,1)} %collective-permute-done.5.refs_6_.refs_7_), channel_id=1, source_target_pairs={{0,62},{2,0},{4,2},{6,4},{8,6},{10,8},{12,10},{14,12},{16,14},{18,... | collective-permute-start | bytes 4718600 | tf_op jit(solution)/shard_map/ppermute | solution.py:20
  87.9 28.0 %collective-permute-done.3.refs_4_.refs_5_ = bf16[512,1536]{1,0:T(8,128)(2,1)} collective-permute-done((bf16[512,1536]{1,0:T(8,128)(2,1)S(1)}, bf16[512,1536]{1,0:T(8,128)(2,1)}, u32[]{:S(2)}, u32[]{:S(2)}) %collective-permute-start.3) | collective-permute-done | bytes 1572896 | tf_op jit(solution)/shard_map/ppermute | solution.py:20
  115.9 5.7 %collective-permute-start.8 = (bf16[512,1536]{1,0:T(8,128)(2,1)}, bf16[512,1536]{1,0:T(8,128)(2,1)}, u32[]{:S(2)}, u32[]{:S(2)}) collective-permute-start(bf16[512,1536]{1,0:T(8,128)(2,1)} %collective-permute-done.7.refs_8_.refs_9_), channel_id=1, source_target_pairs={{0,62},{2,0},{4,2},{6,4},{8,6},{10,8},{12,10},{14,12},{16,14},{18,... | collective-permute-start | bytes 4718600 | tf_op jit(solution)/shard_map/ppermute | solution.py:20
  124.2 13.3 %shard_map.55 = (f32[1024,768]{1,0:T(8,128)}, f32[1024,768]{1,0:T(8,128)}, f32[1024,768]{1,0:T(8,128)}) custom-call(bf16[1024,768]{1,0:T(8,128)(2,1)} %pad_maximum_fusion.refs_0_.refs_1_, bf16[512,1536]{1,0:T(8,128)(2,1)} %copy-done.1, bf16[512,1536]{1,0:T(8,128)(2,1)} %copy-done.1, bf16[512,1536]{1,0:T(8,128)(2,1)} %copy-done.2, bf16[512,1536]{1,0:T(8,128)(2,1)} %copy-done.2), custom_call_target="tpu_custom_call" | custom-call | tf_op jit(solution)/shard_map/pallas_call | solution.py:108
  138.1 61.2 %shard_map.56 = (f32[1024,768]{1,0:T(8,128)}, f32[1024,768]{1,0:T(8,128)}, f32[1024,768]{1,0:T(8,128)}) custom-call(f32[1,2048]{1,0:T(1,128)} %bitcast.49, bf16[1024,768]{1,0:T(8,128)(2,1)} %pad_maximum_fusion.refs_0_.refs_1_, bf16[512,1536]{1,0:T(8,128)(2,1)} %collective-permute-done.1.refs_2_.refs_3_, ...), custom_call_target="tpu_custom_call" | custom-call | tf_op jit(solution)/shard_map/pallas_call | solution.py:108
  200.0 33.7 %shard_map.58 = bf16[512,768]{1,0:T(8,128)(2,1)} custom-call(f32[1,2048]{1,0:T(1,128)} %bitcast.47, bf16[1024,768]{1,0:T(8,128)(2,1)} %pad_maximum_fusion.refs_0_.refs_1_, bf16[512,1536]{1,0:T(8,128)(2,1)} %collective-permute-done.2.refs_2_.refs_3_, bf16[512,1536]{1,0:T(8,128)(2,1)} %collective-permute-done.2.refs_2_.refs_3_, ...), custom_call_target="tpu_custom_call" | custom-call | tf_op jit(solution)/shard_map/pallas_call | solution.py:108
  233.7 3.1 convolution_multiply_fusion
  236.8 3.2 %collective-permute-start.10 = (f32[512,768]{1,0:T(8,128)}, f32[512,768]{1,0:T(8,128)}, u32[]{:S(2)}, u32[]{:S(2)}) collective-permute-start(f32[512,768]{1,0:T(8,128)} %convolution_multiply_fusion), channel_id=1, source_target_pairs={{0,64},{64,0},{1,65},{65,1},{2,66},{66,2},{3,67},{67,3},{4,68},{68... | collective-permute-start | bytes 4718600 | tf_op jit(solution)/shard_map/ppermute | solution.py:24
  240.0 33.5 %shard_map.57 = bf16[512,768]{1,0:T(8,128)(2,1)} custom-call(f32[1,2048]{1,0:T(1,128)} %bitcast.48, bf16[1024,768]{1,0:T(8,128)(2,1)} %pad_maximum_fusion.refs_0_.refs_1_, bf16[512,1536]{1,0:T(8,128)(2,1)} %collective-permute-done.2.refs_2_.refs_3_, bf16[512,1536]{1,0:T(8,128)(2,1)} %collective-permute-done.2.refs_2_.refs_3_, ...), custom_call_target="tpu_custom_call" | custom-call | tf_op jit(solution)/shard_map/pallas_call | solution.py:108
  273.6 2.0 convolution_multiply_fusion.1
  276.5 1.7 multiply_add_fusion
  278.2 1.8 collective-permute-start.11
  280.8 34.4 %collective-permute-done.11 = f32[512,768]{1,0:T(8,128)S(1)} collective-permute-done((f32[512,768]{1,0:T(8,128)S(1)}, f32[512,768]{1,0:T(8,128)S(1)}, u32[]{:S(2)}, u32[]{:S(2)}) %collective-permute-start.11) | collective-permute-done | bytes 1572896 | tf_op jit(solution)/shard_map/ppermute | solution.py:24
  (51 shorter events, 11.9 us)
Async XLA Ops:
  0.0 233.7 %copy-start = (bf16[768,1536]{1,0:T(8,128)(2,1)S(1)}, bf16[768,1536]{1,0:T(8,128)(2,1)}, u32[]{:S(2)}) copy-start(bf16[768,1536]{1,0:T(8,128)(2,1)} %param.8) | copy-start | bytes 7077892
  0.0 2.8 copy-start.4
  4.5 37.6 %collective-permute-start = (bf16[512,1536]{1,0:T(8,128)(2,1)}, bf16[512,1536]{1,0:T(8,128)(2,1)}, u32[]{:S(2)}, u32[]{:S(2)}) collective-permute-start(bf16[512,1536]{1,0:T(8,128)(2,1)} %fusion.5), channel_id=1, source_target_pairs={{0,1},{1,0},{2,3},{3,2},{4,5},{5,4},{6,7},{7,6},{8,9},{9,8},{10,11... | collective-permute-start | bytes 4718600 | tf_op jit(solution)/shard_map/ppermute | solution.py:24
  18.4 23.7 %copy-start.3 = (bf16[1536,3,768]{0,2,1:T(8,128)(2,1)S(1)}, bf16[1536,3,768]{0,2,1:T(8,128)(2,1)}, u32[]{:S(2)}) copy-start(bf16[1536,3,768]{0,2,1:T(8,128)(2,1)} %copy.6) | copy-start | bytes 21233668
  26.0 1.4 copy-start.5
  27.4 20.0 %copy-start.1 = (bf16[512,1536]{1,0:T(8,128)(2,1)}, bf16[512,1536]{1,0:T(8,128)(2,1)S(1)}, u32[]{:S(2)}) copy-start(bf16[512,1536]{1,0:T(8,128)(2,1)S(1)} %slice.48.refs_1_.refs_2_) | copy-start | bytes 4718596
  27.4 54.7 %collective-permute-start.1 = (bf16[512,1536]{1,0:T(8,128)(2,1)S(1)}, bf16[512,1536]{1,0:T(8,128)(2,1)}, u32[]{:S(2)}, u32[]{:S(2)}) collective-permute-start(bf16[512,1536]{1,0:T(8,128)(2,1)S(1)} %slice.48.refs_1_.refs_2_), channel_id=1, source_target_pairs={{0,2},{2,4},{4,6},{6,8},{8,10},{10,12},{12,14},{14,16},{16,18},{18... | collective-permute-start | bytes 4718600 | tf_op jit(solution)/shard_map/ppermute | solution.py:20
  28.7 53.4 %collective-permute-start.5 = (bf16[512,1536]{1,0:T(8,128)(2,1)S(1)}, bf16[512,1536]{1,0:T(8,128)(2,1)}, u32[]{:S(2)}, u32[]{:S(2)}) collective-permute-start(bf16[512,1536]{1,0:T(8,128)(2,1)S(1)} %slice.48.refs_1_.refs_2_), channel_id=1, source_target_pairs={{0,62},{2,0},{4,2},{6,4},{8,6},{10,8},{12,10},{14,12},{16,14},{18,... | collective-permute-start | bytes 4718600 | tf_op jit(solution)/shard_map/ppermute | solution.py:20
  47.4 1.5 copy-start.6
  48.9 33.3 %copy-start.2 = (bf16[512,1536]{1,0:T(8,128)(2,1)}, bf16[512,1536]{1,0:T(8,128)(2,1)S(1)}, u32[]{:S(2)}) copy-start(bf16[512,1536]{1,0:T(8,128)(2,1)S(1)} %slice.49.refs_3_.refs_4_) | copy-start | bytes 4718596
  48.9 72.7 %copy-start.9 = (s32[1,4,8]{2,1,0:T(4,128)S(1)}, s32[1,4,8]{2,1,0:T(4,128)}, u32[]{:S(2)}) copy-start(s32[1,4,8]{2,1,0:T(4,128)} %param.9) | copy-start | bytes 388
  48.9 67.0 %collective-permute-start.3 = (bf16[512,1536]{1,0:T(8,128)(2,1)S(1)}, bf16[512,1536]{1,0:T(8,128)(2,1)}, u32[]{:S(2)}, u32[]{:S(2)}) collective-permute-start(bf16[512,1536]{1,0:T(8,128)(2,1)S(1)} %slice.49.refs_3_.refs_4_), channel_id=1, source_target_pairs={{0,2},{2,4},{4,6},{6,8},{8,10},{10,12},{12,14},{14,16},{16,18},{18... | collective-permute-start | bytes 4718600 | tf_op jit(solution)/shard_map/ppermute | solution.py:20
  50.5 65.4 %collective-permute-start.7 = (bf16[512,1536]{1,0:T(8,128)(2,1)S(1)}, bf16[512,1536]{1,0:T(8,128)(2,1)}, u32[]{:S(2)}, u32[]{:S(2)}) collective-permute-start(bf16[512,1536]{1,0:T(8,128)(2,1)S(1)} %slice.49.refs_3_.refs_4_), channel_id=1, source_target_pairs={{0,62},{2,0},{4,2},{6,4},{8,6},{10,8},{12,10},{14,12},{16,14},{18,... | collective-permute-start | bytes 4718600 | tf_op jit(solution)/shard_map/ppermute | solution.py:20
  82.2 117.1 %collective-permute-start.2 = (bf16[512,1536]{1,0:T(8,128)(2,1)}, bf16[512,1536]{1,0:T(8,128)(2,1)}, u32[]{:S(2)}, u32[]{:S(2)}) collective-permute-start(bf16[512,1536]{1,0:T(8,128)(2,1)} %collective-permute-done.1.refs_2_.refs_3_), channel_id=1, source_target_pairs={{0,2},{2,4},{4,6},{6,8},{8,10},{10,12},{12,14},{14,16},{16,18},{18... | collective-permute-start | bytes 4718600 | tf_op jit(solution)/shard_map/ppermute | solution.py:20
  82.2 117.1 %collective-permute-start.6 = (bf16[512,1536]{1,0:T(8,128)(2,1)}, bf16[512,1536]{1,0:T(8,128)(2,1)}, u32[]{:S(2)}, u32[]{:S(2)}) collective-permute-start(bf16[512,1536]{1,0:T(8,128)(2,1)} %collective-permute-done.5.refs_6_.refs_7_), channel_id=1, source_target_pairs={{0,62},{2,0},{4,2},{6,4},{8,6},{10,8},{12,10},{14,12},{16,14},{18,... | collective-permute-start | bytes 4718600 | tf_op jit(solution)/shard_map/ppermute | solution.py:20
  115.9 83.5 %collective-permute-start.4 = (bf16[512,1536]{1,0:T(8,128)(2,1)}, bf16[512,1536]{1,0:T(8,128)(2,1)}, u32[]{:S(2)}, u32[]{:S(2)}) collective-permute-start(bf16[512,1536]{1,0:T(8,128)(2,1)} %collective-permute-done.3.refs_4_.refs_5_), channel_id=1, source_target_pairs={{0,2},{2,4},{4,6},{6,8},{8,10},{10,12},{12,14},{14,16},{16,18},{18... | collective-permute-start | bytes 4718600 | tf_op jit(solution)/shard_map/ppermute | solution.py:20
  115.9 83.5 %collective-permute-start.8 = (bf16[512,1536]{1,0:T(8,128)(2,1)}, bf16[512,1536]{1,0:T(8,128)(2,1)}, u32[]{:S(2)}, u32[]{:S(2)}) collective-permute-start(bf16[512,1536]{1,0:T(8,128)(2,1)} %collective-permute-done.7.refs_8_.refs_9_), channel_id=1, source_target_pairs={{0,62},{2,0},{4,2},{6,4},{8,6},{10,8},{12,10},{14,12},{16,14},{18,... | collective-permute-start | bytes 4718600 | tf_op jit(solution)/shard_map/ppermute | solution.py:20
  121.6 1.1 slice-start
  121.6 1.4 slice-start.1
  236.8 39.7 %collective-permute-start.10 = (f32[512,768]{1,0:T(8,128)}, f32[512,768]{1,0:T(8,128)}, u32[]{:S(2)}, u32[]{:S(2)}) collective-permute-start(f32[512,768]{1,0:T(8,128)} %convolution_multiply_fusion), channel_id=1, source_target_pairs={{0,64},{64,0},{1,65},{65,1},{2,66},{66,2},{3,67},{67,3},{4,68},{68... | collective-permute-start | bytes 4718600 | tf_op jit(solution)/shard_map/ppermute | solution.py:24
  273.5 2.1 copy-start.7
  275.5 5.2 %collective-permute-start.9 = (f32[512,768]{1,0:T(8,128)S(1)}, f32[512,768]{1,0:T(8,128)S(1)}, u32[]{:S(2)}, u32[]{:S(2)}) collective-permute-start(f32[512,768]{1,0:T(8,128)S(1)} %convolution_multiply_fusion.1), channel_id=1, source_target_pairs={{0,64},{64,0},{1,65},{65,1},{2,66},{66,2},{3,67},{67,3},{4,68},{68... | collective-permute-start | bytes 4718600 | tf_op jit(solution)/shard_map/ppermute | solution.py:24
  276.4 3.5 %copy-start.8 = (bf16[512,768]{1,0:T(8,128)(2,1)S(1)}, bf16[512,768]{1,0:T(8,128)(2,1)}, u32[]{:S(2)}) copy-start(bf16[512,768]{1,0:T(8,128)(2,1)} %shard_map.57) | copy-start | bytes 2359300
  278.2 37.0 %collective-permute-start.11 = (f32[512,768]{1,0:T(8,128)S(1)}, f32[512,768]{1,0:T(8,128)S(1)}, u32[]{:S(2)}, u32[]{:S(2)}) collective-permute-start(f32[512,768]{1,0:T(8,128)S(1)} %multiply_add_fusion), channel_id=1, source_target_pairs={{0,1},{1,0},{2,3},{3,2},{4,5},{5,4},{6,7},{7,6},{8,9},{9,8},{10,11... | collective-permute-start | bytes 4718600 | tf_op jit(solution)/shard_map/ppermute | solution.py:24

commit v4 on v3

--- a/solution.py
+++ b/solution.py
@@ -38,12 +38,12 @@
     q = q_ref[...]
     rows = q.shape[0]
     if first:
-        m = jnp.full((rows, 1), -jnp.inf, jnp.float32)
-        l = jnp.zeros((rows, 1), jnp.float32)
+        m = jnp.full((rows, HEAD_DIM), -jnp.inf, jnp.float32)
+        l = jnp.zeros((rows, HEAD_DIM), jnp.float32)
         acc = jnp.zeros((rows, HEAD_DIM), jnp.float32)
     else:
-        m = m_in[:, :1]
-        l = l_in[:, :1]
+        m = m_in[...]
+        l = l_in[...]
         acc = acc_in[...]
     for index in range(n_chunks):
         keys = chunk_refs[2 * index][...]
@@ -56,7 +56,7 @@
             scores = scores + bias_ref[:, index * width : (index + 1) * width]
         m_new = jnp.maximum(m, jnp.max(scores, axis=1, keepdims=True))
         alpha = jnp.exp(m - m_new)
-        expon = jnp.exp(scores - m_new)
+        expon = jnp.exp(scores - jnp.tile(m_new, (1, width // HEAD_DIM)))
         l = alpha * l + jnp.sum(expon, axis=1, keepdims=True)
         acc = alpha * acc + jnp.dot(
             expon.astype(jnp.bfloat16), values, preferred_element_type=jnp.float32
@@ -65,8 +65,8 @@
     if last:
         outs[0][...] = (acc / l).astype(outs[0].dtype)
     else:
-        outs[0][...] = jnp.broadcast_to(m, outs[0].shape)
-        outs[1][...] = jnp.broadcast_to(l, outs[1].shape)
+        outs[0][...] = m
+        outs[1][...] = l
         outs[2][...] = acc
 
 

time: 317 us -> 261 us (0.82)
  Pallas kernels: 142 us -> 66 us
  waiting for transfers between devices: 96.7 us -> 118 us
    pallas_call x4, Pallas kernels: 142 us -> 66 us  [attend_stage(): pl.pallas_call(kernel, out_shape=out_shape, grid=(heads,), in_specs=in_sp...]
    ppermute x8, waiting for transfers between devices: 53.8 us -> 75 us  [from_behind(): lax.ppermute(array, axis, [(i, (i + by) % count) for i in range(count)])]
  transfers between devices with their start and end apart: 12 -> 12, of which waited for: 4 -> 5; matrix products, arithmetic and copies ran while one was open for 10% -> 12% of each run, Pallas kernels for 34% -> 20%
where the time goes in v4:
time: 261 us; the launch traced here: 260 us
  waiting for transfers between devices  118 us (45%)
  Pallas kernels  66 us (25%)
  starting transfers between devices  32.1 us (12%)
  matrix products  19.5 us (7%)
  local copies, waits for them, and re-layouts  15.7 us (6%)
  other arithmetic  8.78 us (3%)
    ppermute x8, waiting for transfers between devices, from_behind(): lax.ppermute(array, axis, [(i, (i + by) % count) for i in range(count)])  75 us
    pallas_call x4, Pallas kernels, attend_stage(): pl.pallas_call(kernel, out_shape=out_shape, grid=(heads,), in_specs=in_sp...  66 us
    ppermute x4, waiting for transfers between devices, swap(): return lax.ppermute(array, axis, [(0, 1), (1, 0)])  42.9 us
    ppermute x8, starting transfers between devices, from_behind(): lax.ppermute(array, axis, [(i, (i + by) % count) for i in range(count)])  25.1 us
    unnamed x21, local copies, waits for them, and re-layouts  13 us
    dot_general x1, matrix products, per_device(): jnp.dot(normed, flat_w, preferred_element_type=jnp.float32)  7.6 us
    ppermute x4, starting transfers between devices, swap(): return lax.ppermute(array, axis, [(0, 1), (1, 0)])  7 us
    dot_general x1, matrix products, per_device(): jnp.dot(partner_normed, flat_w, preferred_element_type=jnp.float32)  5.29 us
  transfers between devices with their start and end apart: 12, of which 5 were waited for; matrix products, arithmetic and copies ran while one was open for 12% of the time, Pallas kernels for 20%

profile of v4, /device:TPU:1, one launch (start us, length us, event | category | flops | bytes accessed | tf_op | source)
XLA Modules:
  0.0 260.2 jit_solution(18015105065197195594)
XLA Ops:
  0.9 1.9 fusion.2
  2.8 1.7 fusion.5
  4.5 3.6 %collective-permute-start = (bf16[512,1536]{1,0:T(8,128)(2,1)}, bf16[512,1536]{1,0:T(8,128)(2,1)}, u32[]{:S(2)}, u32[]{:S(2)}) collective-permute-start(bf16[512,1536]{1,0:T(8,128)(2,1)} %fusion.5), channel_id=1, source_target_pairs={{0,1},{1,0},{2,3},{3,2},{4,5},{5,4},{6,7},{7,6},{8,9},{9,8},{10,11... | collective-permute-start | bytes 4718600 | tf_op jit(solution)/shard_map/ppermute | solution.py:24
  8.1 10.3 %copy.6 = bf16[1536,3,768]{0,2,1:T(8,128)(2,1)} copy(bf16[1536,3,768]{2,0,1:T(8,128)(2,1)} %param.7) | data formatting | bytes 14155776 | tf_op args[2]
  18.4 7.6 %convolution_convert_fusion.1 = bf16[512,2304]{1,0:T(8,128)(2,1)S(1)} fusion(bf16[1536,2304]{0,1:T(8,128)(2,1)} %bitcast.45, bf16[1,1,512,1536]{3,2,1,0:T(8,128)(2,1)} %param.5, f32[1536]{0:T(1024)S(1)} %get-tuple-element.18, f32[1536]{0:T(1024)S(1)} %get-tuple-element.17, f32[512]{0:T(512)S(1)} %add_rsqrt_fusion), kind=kOutput, calls=%fused_computation.1 | convolution fusion | flops 3628990464 | bytes 11024384 | tf_op jit(solution)/shard_map/dot_general | solution.py:131
  28.7 4.9 %collective-permute-start.5 = (bf16[512,1536]{1,0:T(8,128)(2,1)S(1)}, bf16[512,1536]{1,0:T(8,128)(2,1)}, u32[]{:S(2)}, u32[]{:S(2)}) collective-permute-start(bf16[512,1536]{1,0:T(8,128)(2,1)S(1)} %slice.48.refs_1_.refs_2_), channel_id=1, source_target_pairs={{0,62},{2,0},{4,2},{6,4},{8,6},{10,8},{12,10},{14,12},{16,14},{18,... | collective-permute-start | bytes 4718600 | tf_op jit(solution)/shard_map/ppermute | solution.py:20
  33.7 8.4 %collective-permute-done = bf16[512,1536]{1,0:T(8,128)(2,1)} collective-permute-done((bf16[512,1536]{1,0:T(8,128)(2,1)}, bf16[512,1536]{1,0:T(8,128)(2,1)}, u32[]{:S(2)}, u32[]{:S(2)}) %collective-permute-start) | collective-permute-done | bytes 1572896 | tf_op jit(solution)/shard_map/ppermute | solution.py:24
  42.1 5.3 %convolution_convert_fusion = bf16[512,2304]{1,0:T(8,128)(2,1)S(1)} fusion(bf16[512,1536]{1,0:T(8,128)(2,1)} %collective-permute-done, bf16[1536,2304]{0,1:T(8,128)(2,1)S(1)} %bitcast.46), kind=kOutput, calls=%fused_computation | convolution fusion | flops 3625058304 | bytes 11010048 | tf_op jit(solution)/shard_map/dot_general | solution.py:133
  48.9 1.6 collective-permute-start.3
  50.5 5.8 %collective-permute-start.7 = (bf16[512,1536]{1,0:T(8,128)(2,1)S(1)}, bf16[512,1536]{1,0:T(8,128)(2,1)}, u32[]{:S(2)}, u32[]{:S(2)}) collective-permute-start(bf16[512,1536]{1,0:T(8,128)(2,1)S(1)} %slice.49.refs_3_.refs_4_), channel_id=1, source_target_pairs={{0,62},{2,0},{4,2},{6,4},{8,6},{10,8},{12,10},{14,12},{16,14},{18,... | collective-permute-start | bytes 4718600 | tf_op jit(solution)/shard_map/ppermute | solution.py:20
  56.4 25.8 %collective-permute-done.1.refs_2_.refs_3_ = bf16[512,1536]{1,0:T(8,128)(2,1)} collective-permute-done((bf16[512,1536]{1,0:T(8,128)(2,1)S(1)}, bf16[512,1536]{1,0:T(8,128)(2,1)}, u32[]{:S(2)}, u32[]{:S(2)}) %collective-permute-start.1) | collective-permute-done | bytes 1572896 | tf_op jit(solution)/shard_map/ppermute | solution.py:20
  82.2 5.7 %collective-permute-start.6 = (bf16[512,1536]{1,0:T(8,128)(2,1)}, bf16[512,1536]{1,0:T(8,128)(2,1)}, u32[]{:S(2)}, u32[]{:S(2)}) collective-permute-start(bf16[512,1536]{1,0:T(8,128)(2,1)} %collective-permute-done.5.refs_6_.refs_7_), channel_id=1, source_target_pairs={{0,62},{2,0},{4,2},{6,4},{8,6},{10,8},{12,10},{14,12},{16,14},{18,... | collective-permute-start | bytes 4718600 | tf_op jit(solution)/shard_map/ppermute | solution.py:20
  87.9 28.0 %collective-permute-done.3.refs_4_.refs_5_ = bf16[512,1536]{1,0:T(8,128)(2,1)} collective-permute-done((bf16[512,1536]{1,0:T(8,128)(2,1)S(1)}, bf16[512,1536]{1,0:T(8,128)(2,1)}, u32[]{:S(2)}, u32[]{:S(2)}) %collective-permute-start.3) | collective-permute-done | bytes 1572896 | tf_op jit(solution)/shard_map/ppermute | solution.py:20
  115.9 5.7 %collective-permute-start.8 = (bf16[512,1536]{1,0:T(8,128)(2,1)}, bf16[512,1536]{1,0:T(8,128)(2,1)}, u32[]{:S(2)}, u32[]{:S(2)}) collective-permute-start(bf16[512,1536]{1,0:T(8,128)(2,1)} %collective-permute-done.7.refs_8_.refs_9_), channel_id=1, source_target_pairs={{0,62},{2,0},{4,2},{6,4},{8,6},{10,8},{12,10},{14,12},{16,14},{18,... | collective-permute-start | bytes 4718600 | tf_op jit(solution)/shard_map/ppermute | solution.py:20
  124.2 13.3 %shard_map.55 = (f32[1024,768]{1,0:T(8,128)}, f32[1024,768]{1,0:T(8,128)}, f32[1024,768]{1,0:T(8,128)}) custom-call(bf16[1024,768]{1,0:T(8,128)(2,1)} %pad_maximum_fusion.refs_0_.refs_1_, bf16[512,1536]{1,0:T(8,128)(2,1)} %copy-done.1, bf16[512,1536]{1,0:T(8,128)(2,1)} %copy-done.1, bf16[512,1536]{1,0:T(8,128)(2,1)} %copy-done.2, bf16[512,1536]{1,0:T(8,128)(2,1)} %copy-done.2), custom_call_target="tpu_custom_call" | custom-call | tf_op jit(solution)/shard_map/pallas_call | solution.py:108
  138.1 23.9 %shard_map.56 = (f32[1024,768]{1,0:T(8,128)}, f32[1024,768]{1,0:T(8,128)}, f32[1024,768]{1,0:T(8,128)}) custom-call(f32[1,2048]{1,0:T(1,128)} %bitcast.49, bf16[1024,768]{1,0:T(8,128)(2,1)} %pad_maximum_fusion.refs_0_.refs_1_, bf16[512,1536]{1,0:T(8,128)(2,1)} %collective-permute-done.1.refs_2_.refs_3_, ...), custom_call_target="tpu_custom_call" | custom-call | tf_op jit(solution)/shard_map/pallas_call | solution.py:108
  162.1 21.2 %collective-permute-done.4.refs_4_.refs_5_ = bf16[512,1536]{1,0:T(8,128)(2,1)} collective-permute-done((bf16[512,1536]{1,0:T(8,128)(2,1)}, bf16[512,1536]{1,0:T(8,128)(2,1)}, u32[]{:S(2)}, u32[]{:S(2)}) %collective-permute-start.4) | collective-permute-done | bytes 1572896 | tf_op jit(solution)/shard_map/ppermute | solution.py:20
  183.9 14.3 %shard_map.58 = bf16[512,768]{1,0:T(8,128)(2,1)} custom-call(f32[1,2048]{1,0:T(1,128)} %bitcast.47, bf16[1024,768]{1,0:T(8,128)(2,1)} %pad_maximum_fusion.refs_0_.refs_1_, bf16[512,1536]{1,0:T(8,128)(2,1)} %collective-permute-done.2.refs_2_.refs_3_, bf16[512,1536]{1,0:T(8,128)(2,1)} %collective-permute-done.2.refs_2_.refs_3_, ...), custom_call_target="tpu_custom_call" | custom-call | tf_op jit(solution)/shard_map/pallas_call | solution.py:108
  198.3 3.1 %convolution_multiply_fusion = f32[512,768]{1,0:T(8,128)} fusion(bf16[512,768]{1,0:T(8,128)(2,1)} %shard_map.58, bf16[768,1536]{1,0:T(8,128)(2,1)S(1)} %copy-done, s32[]{:T(128)S(6)} %select_n.59, f32[]{:T(128)S(6)} %select_n.51), kind=kOutput, calls=%fused_computation.20 | convolution fusion | flops 604372992 | bytes 3538952 | tf_op jit(solution)/shard_map/dot_general | solution.py:187
  202.9 14.4 %shard_map.57 = bf16[512,768]{1,0:T(8,128)(2,1)} custom-call(f32[1,2048]{1,0:T(1,128)} %bitcast.48, bf16[1024,768]{1,0:T(8,128)(2,1)} %pad_maximum_fusion.refs_0_.refs_1_, bf16[512,1536]{1,0:T(8,128)(2,1)} %collective-permute-done.2.refs_2_.refs_3_, bf16[512,1536]{1,0:T(8,128)(2,1)} %collective-permute-done.2.refs_2_.refs_3_, ...), custom_call_target="tpu_custom_call" | custom-call | tf_op jit(solution)/shard_map/pallas_call | solution.py:108
  217.4 2.0 convolution_multiply_fusion.1
  220.3 1.7 multiply_add_fusion
  222.0 1.8 collective-permute-start.11
  224.6 34.4 %collective-permute-done.11 = f32[512,768]{1,0:T(8,128)S(1)} collective-permute-done((f32[512,768]{1,0:T(8,128)S(1)}, f32[512,768]{1,0:T(8,128)S(1)}, u32[]{:S(2)}, u32[]{:S(2)}) %collective-permute-start.11) | collective-permute-done | bytes 1572896 | tf_op jit(solution)/shard_map/ppermute | solution.py:24
  (51 shorter events, 13.4 us)
Async XLA Ops:
  0.0 198.3 %copy-start = (bf16[768,1536]{1,0:T(8,128)(2,1)S(1)}, bf16[768,1536]{1,0:T(8,128)(2,1)}, u32[]{:S(2)}) copy-start(bf16[768,1536]{1,0:T(8,128)(2,1)} %param.8) | copy-start | bytes 7077892
  0.0 2.8 %copy-start.4 = (bf16[1,1,512,1536]{3,2,1,0:T(8,128)(2,1)S(1)}, bf16[1,1,512,1536]{3,2,1,0:T(8,128)(2,1)}, u32[]{:S(2)}) copy-start(bf16[1,1,512,1536]{3,2,1,0:T(8,128)(2,1)} %param.5) | copy-start | bytes 4718596
  4.5 37.6 %collective-permute-start = (bf16[512,1536]{1,0:T(8,128)(2,1)}, bf16[512,1536]{1,0:T(8,128)(2,1)}, u32[]{:S(2)}, u32[]{:S(2)}) collective-permute-start(bf16[512,1536]{1,0:T(8,128)(2,1)} %fusion.5), channel_id=1, source_target_pairs={{0,1},{1,0},{2,3},{3,2},{4,5},{5,4},{6,7},{7,6},{8,9},{9,8},{10,11... | collective-permute-start | bytes 4718600 | tf_op jit(solution)/shard_map/ppermute | solution.py:24
  18.4 23.7 %copy-start.3 = (bf16[1536,3,768]{0,2,1:T(8,128)(2,1)S(1)}, bf16[1536,3,768]{0,2,1:T(8,128)(2,1)}, u32[]{:S(2)}) copy-start(bf16[1536,3,768]{0,2,1:T(8,128)(2,1)} %copy.6) | copy-start | bytes 21233668
  26.0 1.4 copy-start.5
  27.4 20.0 %copy-start.1 = (bf16[512,1536]{1,0:T(8,128)(2,1)}, bf16[512,1536]{1,0:T(8,128)(2,1)S(1)}, u32[]{:S(2)}) copy-start(bf16[512,1536]{1,0:T(8,128)(2,1)S(1)} %slice.48.refs_1_.refs_2_) | copy-start | bytes 4718596
  27.4 54.7 %collective-permute-start.1 = (bf16[512,1536]{1,0:T(8,128)(2,1)S(1)}, bf16[512,1536]{1,0:T(8,128)(2,1)}, u32[]{:S(2)}, u32[]{:S(2)}) collective-permute-start(bf16[512,1536]{1,0:T(8,128)(2,1)S(1)} %slice.48.refs_1_.refs_2_), channel_id=1, source_target_pairs={{0,2},{2,4},{4,6},{6,8},{8,10},{10,12},{12,14},{14,16},{16,18},{18... | collective-permute-start | bytes 4718600 | tf_op jit(solution)/shard_map/ppermute | solution.py:20
  28.7 53.4 %collective-permute-start.5 = (bf16[512,1536]{1,0:T(8,128)(2,1)S(1)}, bf16[512,1536]{1,0:T(8,128)(2,1)}, u32[]{:S(2)}, u32[]{:S(2)}) collective-permute-start(bf16[512,1536]{1,0:T(8,128)(2,1)S(1)} %slice.48.refs_1_.refs_2_), channel_id=1, source_target_pairs={{0,62},{2,0},{4,2},{6,4},{8,6},{10,8},{12,10},{14,12},{16,14},{18,... | collective-permute-start | bytes 4718600 | tf_op jit(solution)/shard_map/ppermute | solution.py:20
  47.4 1.5 copy-start.6
  48.9 33.3 %copy-start.2 = (bf16[512,1536]{1,0:T(8,128)(2,1)}, bf16[512,1536]{1,0:T(8,128)(2,1)S(1)}, u32[]{:S(2)}) copy-start(bf16[512,1536]{1,0:T(8,128)(2,1)S(1)} %slice.49.refs_3_.refs_4_) | copy-start | bytes 4718596
  48.9 72.7 %copy-start.9 = (s32[1,4,8]{2,1,0:T(4,128)S(1)}, s32[1,4,8]{2,1,0:T(4,128)}, u32[]{:S(2)}) copy-start(s32[1,4,8]{2,1,0:T(4,128)} %param.9) | copy-start | bytes 388
  48.9 67.0 %collective-permute-start.3 = (bf16[512,1536]{1,0:T(8,128)(2,1)S(1)}, bf16[512,1536]{1,0:T(8,128)(2,1)}, u32[]{:S(2)}, u32[]{:S(2)}) collective-permute-start(bf16[512,1536]{1,0:T(8,128)(2,1)S(1)} %slice.49.refs_3_.refs_4_), channel_id=1, source_target_pairs={{0,2},{2,4},{4,6},{6,8},{8,10},{10,12},{12,14},{14,16},{16,18},{18... | collective-permute-start | bytes 4718600 | tf_op jit(solution)/shard_map/ppermute | solution.py:20
  50.5 65.4 %collective-permute-start.7 = (bf16[512,1536]{1,0:T(8,128)(2,1)S(1)}, bf16[512,1536]{1,0:T(8,128)(2,1)}, u32[]{:S(2)}, u32[]{:S(2)}) collective-permute-start(bf16[512,1536]{1,0:T(8,128)(2,1)S(1)} %slice.49.refs_3_.refs_4_), channel_id=1, source_target_pairs={{0,62},{2,0},{4,2},{6,4},{8,6},{10,8},{12,10},{14,12},{16,14},{18,... | collective-permute-start | bytes 4718600 | tf_op jit(solution)/shard_map/ppermute | solution.py:20
  82.2 79.9 %collective-permute-start.2 = (bf16[512,1536]{1,0:T(8,128)(2,1)}, bf16[512,1536]{1,0:T(8,128)(2,1)}, u32[]{:S(2)}, u32[]{:S(2)}) collective-permute-start(bf16[512,1536]{1,0:T(8,128)(2,1)} %collective-permute-done.1.refs_2_.refs_3_), channel_id=1, source_target_pairs={{0,2},{2,4},{4,6},{6,8},{8,10},{10,12},{12,14},{14,16},{16,18},{18... | collective-permute-start | bytes 4718600 | tf_op jit(solution)/shard_map/ppermute | solution.py:20
  82.2 79.9 %collective-permute-start.6 = (bf16[512,1536]{1,0:T(8,128)(2,1)}, bf16[512,1536]{1,0:T(8,128)(2,1)}, u32[]{:S(2)}, u32[]{:S(2)}) collective-permute-start(bf16[512,1536]{1,0:T(8,128)(2,1)} %collective-permute-done.5.refs_6_.refs_7_), channel_id=1, source_target_pairs={{0,62},{2,0},{4,2},{6,4},{8,6},{10,8},{12,10},{14,12},{16,14},{18,... | collective-permute-start | bytes 4718600 | tf_op jit(solution)/shard_map/ppermute | solution.py:20
  115.9 67.4 %collective-permute-start.4 = (bf16[512,1536]{1,0:T(8,128)(2,1)}, bf16[512,1536]{1,0:T(8,128)(2,1)}, u32[]{:S(2)}, u32[]{:S(2)}) collective-permute-start(bf16[512,1536]{1,0:T(8,128)(2,1)} %collective-permute-done.3.refs_4_.refs_5_), channel_id=1, source_target_pairs={{0,2},{2,4},{4,6},{6,8},{8,10},{10,12},{12,14},{14,16},{16,18},{18... | collective-permute-start | bytes 4718600 | tf_op jit(solution)/shard_map/ppermute | solution.py:20
  115.9 67.4 %collective-permute-start.8 = (bf16[512,1536]{1,0:T(8,128)(2,1)}, bf16[512,1536]{1,0:T(8,128)(2,1)}, u32[]{:S(2)}, u32[]{:S(2)}) collective-permute-start(bf16[512,1536]{1,0:T(8,128)(2,1)} %collective-permute-done.7.refs_8_.refs_9_), channel_id=1, source_target_pairs={{0,62},{2,0},{4,2},{6,4},{8,6},{10,8},{12,10},{14,12},{16,14},{18,... | collective-permute-start | bytes 4718600 | tf_op jit(solution)/shard_map/ppermute | solution.py:20
  121.6 1.1 slice-start
  121.6 1.4 slice-start.1
  201.4 18.9 %collective-permute-start.10 = (f32[512,768]{1,0:T(8,128)}, f32[512,768]{1,0:T(8,128)}, u32[]{:S(2)}, u32[]{:S(2)}) collective-permute-start(f32[512,768]{1,0:T(8,128)} %convolution_multiply_fusion), channel_id=1, source_target_pairs={{0,64},{64,0},{1,65},{65,1},{2,66},{66,2},{3,67},{67,3},{4,68},{68... | collective-permute-start | bytes 4718600 | tf_op jit(solution)/shard_map/ppermute | solution.py:24
  217.4 2.1 copy-start.7
  219.4 5.2 %collective-permute-start.9 = (f32[512,768]{1,0:T(8,128)S(1)}, f32[512,768]{1,0:T(8,128)S(1)}, u32[]{:S(2)}, u32[]{:S(2)}) collective-permute-start(f32[512,768]{1,0:T(8,128)S(1)} %convolution_multiply_fusion.1), channel_id=1, source_target_pairs={{0,64},{64,0},{1,65},{65,1},{2,66},{66,2},{3,67},{67,3},{4,68},{68... | collective-permute-start | bytes 4718600 | tf_op jit(solution)/shard_map/ppermute | solution.py:24
  220.3 3.5 %copy-start.8 = (bf16[512,768]{1,0:T(8,128)(2,1)S(1)}, bf16[512,768]{1,0:T(8,128)(2,1)}, u32[]{:S(2)}) copy-start(bf16[512,768]{1,0:T(8,128)(2,1)} %shard_map.57) | copy-start | bytes 2359300
  222.0 37.0 %collective-permute-start.11 = (f32[512,768]{1,0:T(8,128)S(1)}, f32[512,768]{1,0:T(8,128)S(1)}, u32[]{:S(2)}, u32[]{:S(2)}) collective-permute-start(f32[512,768]{1,0:T(8,128)S(1)} %multiply_add_fusion), channel_id=1, source_target_pairs={{0,1},{1,0},{2,3},{3,2},{4,5},{5,4},{6,7},{7,6},{8,9},{9,8},{10,11... | collective-permute-start | bytes 4718600 | tf_op jit(solution)/shard_map/ppermute | solution.py:24

commit v5 on v4

--- a/solution.py
+++ b/solution.py
@@ -127,21 +127,18 @@
     )
     half_rows = normed.shape[0]
     partner_normed = swap(normed, "tp")
+    w_partner = swap(w_out, "tp")
     flat_w = w_qkv.reshape(width, 3 * half_heads)
     qkv_own = jnp.dot(normed, flat_w, preferred_element_type=jnp.float32).astype(jnp.bfloat16)
     pair_own = qkv_own[:, half_heads:]
+
+    near_own = {sign: from_behind(pair_own, "orbit", -sign) for sign in (1, -1)}
+
     qkv_other = jnp.dot(partner_normed, flat_w, preferred_element_type=jnp.float32).astype(
         jnp.bfloat16
     )
     pair_other = qkv_other[:, half_heads:]
     queries = jnp.concatenate([qkv_own[:, :half_heads], qkv_other[:, :half_heads]], axis=0)
-
-    received = {}
-    for sign in (1, -1):
-        near = [from_behind(piece, "orbit", -sign) for piece in (pair_own, pair_other)]
-        far = [from_behind(piece, "orbit", -sign) for piece in near]
-        received[sign] = near
-        received[2 * sign] = far
 
     tp_index = lax.axis_index("tp")
     flags = adjacency[0]
@@ -150,45 +147,57 @@
     own_start = tp_index * per_chunk
     other_start = (1 - tp_index) * per_chunk
 
-    def chunk_bias(offsets):
+    def chunk_bias(offsets, start):
         rows_of = []
         for offset in offsets:
             row = flags[offset + REACH if offset < 0 else offset + REACH - 1]
-            rows_of.append(lax.dynamic_slice_in_dim(row, own_start, per_chunk))
-            rows_of.append(lax.dynamic_slice_in_dim(row, other_start, per_chunk))
+            rows_of.append(lax.dynamic_slice_in_dim(row, start, per_chunk))
         allowed = jnp.repeat(jnp.concatenate(rows_of), BLOCK) > 0
         return jnp.where(allowed, 0.0, -1e30).astype(jnp.float32)[None, :]
 
     carry = attend_stage(
         queries, [pair_own, pair_other], None, None, first=True, last=False, heads=heads
     )
-    carry = attend_stage(
-        queries, received[-1] + received[1], chunk_bias((-1, 1)), carry,
+    pair_other, carry = lax.optimization_barrier((pair_other, carry))
+    near_other = {sign: from_behind(pair_other, "orbit", -sign) for sign in (1, -1)}
+    far_own = {sign: from_behind(near_own[sign], "orbit", -sign) for sign in (1, -1)}
+    carry = attend_stage(
+        queries, [near_own[-1], near_own[1]], chunk_bias((-1, 1), own_start), carry,
         first=False, last=False, heads=heads,
     )
-    far_chunks = received[-2] + received[2]
-    far_bias = chunk_bias((-2, 2))
+    far_other = {sign: from_behind(near_other[sign], "orbit", -sign) for sign in (1, -1)}
+    carry = attend_stage(
+        queries, [near_other[-1], near_other[1]], chunk_bias((-1, 1), other_start), carry,
+        first=False, last=False, heads=heads,
+    )
+    carry = attend_stage(
+        queries, [far_own[-1], far_own[1]], chunk_bias((-2, 2), own_start), carry,
+        first=False, last=False, heads=heads,
+    )
+    last_chunks = [far_other[-1], far_other[1]]
+    last_bias = chunk_bias((-2, 2), other_start)
     context_other = attend_stage(
-        queries, far_chunks, far_bias, carry,
+        queries, last_chunks, last_bias, carry,
         first=False, last=True, heads=heads, row_block=1, rows=half_rows,
     )
+    context_partner = swap(context_other, "tp")
     context_own = attend_stage(
-        queries, far_chunks, far_bias, carry,
+        queries, last_chunks, last_bias, carry,
         first=False, last=True, heads=heads, row_block=0, rows=half_rows,
     )
+    context = jnp.concatenate([context_own, context_partner], axis=1)
+    w_local = jnp.concatenate([w_out, w_partner], axis=0)
 
     owner = lax.axis_index("cfg")
     half_width = width // 2
     weight_now = jnp.where(owner == 0, guide_scale, 1.0 - guide_scale).astype(jnp.float32)
-    w_mine = lax.dynamic_slice_in_dim(w_out, owner * half_width, half_width, 1)
-    w_theirs = lax.dynamic_slice_in_dim(w_out, (1 - owner) * half_width, half_width, 1)
-
-    def project(context):
-        theirs = weight_now * jnp.dot(context, w_theirs, preferred_element_type=jnp.float32)
-        mine = weight_now * jnp.dot(context, w_mine, preferred_element_type=jnp.float32)
-        return mine + swap(theirs, "cfg")
-
-    guided = project(context_own) + swap(project(context_other), "tp")
+    weight_other = jnp.where(owner == 0, 1.0 - guide_scale, guide_scale).astype(jnp.float32)
+    w_mine = lax.dynamic_slice_in_dim(w_local, owner * half_width, half_width, 1)
+    w_theirs = lax.dynamic_slice_in_dim(w_local, (1 - owner) * half_width, half_width, 1)
+    theirs = jnp.dot(context, w_theirs, preferred_element_type=jnp.float32).astype(jnp.bfloat16)
+    mine = jnp.dot(context, w_mine, preferred_element_type=jnp.float32).astype(jnp.bfloat16)
+    received = swap(theirs, "cfg")
+    guided = weight_now * mine.astype(jnp.float32) + weight_other * received.astype(jnp.float32)
     return guided.astype(jnp.bfloat16)[None]
 
 

time: 261 us -> 275 us (1.054)
  Pallas kernels: 66 us -> 74.6 us
  local copies, waits for them, and re-layouts: 15.7 us -> 22.2 us
  starting transfers between devices: 32.1 us -> 35.6 us
  waiting for transfers between devices: 118 us -> 115 us
    ppermute x4, waiting for transfers between devices: 42.9 us -> 11.1 us  [swap(): return lax.ppermute(array, axis, [(0, 1), (1, 0)])]
    ppermute x8, waiting for transfers between devices: 75 us -> 104 us  [from_behind(): lax.ppermute(array, axis, [(i, (i + by) % count) for i in range(count)])]
    pallas_call x4 -> x6, Pallas kernels: 66 us -> 74.6 us  [attend_stage(): pl.pallas_call(kernel, out_shape=out_shape, grid=(heads,), in_specs=in_sp...]
    ppermute x4, starting transfers between devices: 7 us -> 10.3 us  [swap(): return lax.ppermute(array, axis, [(0, 1), (1, 0)])]
    concatenate x0 -> x1, local copies, waits for them, and re-layouts: none -> 3.25 us  [per_device(): w_local = jnp.concatenate([w_out, w_partner], axis=0)]
    unnamed x21 -> x18, local copies, waits for them, and re-layouts: 13 us -> 14.5 us
    dot_general x4 -> x2, matrix products: 6.64 us -> 6.34 us  [the longest x1 3.3 us: per_device(): jnp.dot(context, w_theirs, preferred_element_type=jnp.float32)]
  transfers between devices with their start and end apart: 12 -> 12, of which waited for: 5 -> 6; matrix products, arithmetic and copies ran while one was open for 12% -> 14% of each run, Pallas kernels for 20% -> 27%
where the time goes in v5:
time: 275 us; the launch traced here: 274 us
  waiting for transfers between devices  115 us (42%)
  Pallas kernels  74.6 us (27%)
  starting transfers between devices  35.6 us (13%)
  local copies, waits for them, and re-layouts  22.2 us (8%)
  matrix products  19.1 us (7%)
  other arithmetic  7.19 us (3%)
    ppermute x8, waiting for transfers between devices, from_behind(): lax.ppermute(array, axis, [(i, (i + by) % count) for i in range(count)])  104 us
    pallas_call x6, Pallas kernels, attend_stage(): pl.pallas_call(kernel, out_shape=out_shape, grid=(heads,), in_specs=in_sp...  74.6 us
    ppermute x8, starting transfers between devices, from_behind(): lax.ppermute(array, axis, [(i, (i + by) % count) for i in range(count)])  25.3 us
    unnamed x18, local copies, waits for them, and re-layouts  14.5 us
    ppermute x4, waiting for transfers between devices, swap(): return lax.ppermute(array, axis, [(0, 1), (1, 0)])  11.1 us
    ppermute x4, starting transfers between devices, swap(): return lax.ppermute(array, axis, [(0, 1), (1, 0)])  10.3 us
    dot_general x1, matrix products, per_device(): jnp.dot(normed, flat_w, preferred_element_type=jnp.float32)  7.47 us
  transfers between devices with their start and end apart: 12, of which 6 were waited for; matrix products, arithmetic and copies ran while one was open for 14% of the time, Pallas kernels for 27%

profile of v5, /device:TPU:1, one launch (start us, length us, event | category | flops | bytes accessed | tf_op | source)
XLA Modules:
  0.0 273.8 jit_solution(9498371381885256918)
XLA Ops:
  4.6 3.6 %collective-permute-start = (bf16[512,1536]{1,0:T(8,128)(2,1)S(1)}, bf16[512,1536]{1,0:T(8,128)(2,1)}, u32[]{:S(2)}, u32[]{:S(2)}) collective-permute-start(bf16[512,1536]{1,0:T(8,128)(2,1)S(1)} %fusion.5), channel_id=1, source_target_pairs={{0,1},{1,0},{2,3},{3,2},{4,5},{5,4},{6,7},{7,6},{8,9},{9,8},{10,11... | collective-permute-start | bytes 4718600 | tf_op jit(solution)/shard_map/ppermute | solution.py:24
  8.2 10.3 %copy.6 = bf16[1536,3,768]{0,2,1:T(8,128)(2,1)} copy(bf16[1536,3,768]{2,0,1:T(8,128)(2,1)} %param.7) | data formatting | bytes 14155776 | tf_op args[2]
  18.5 7.5 %convolution_convert_fusion.1 = bf16[512,2304]{1,0:T(8,128)(2,1)S(1)} fusion(bf16[1536,2304]{0,1:T(8,128)(2,1)} %bitcast.43, bf16[1,1,512,1536]{3,2,1,0:T(8,128)(2,1)S(1)} %copy-done.5, f32[1536]{0:T(1024)S(1)} %get-tuple-element.38, f32[1536]{0:T(1024)S(1)} %get-tuple-element.37, f32[512]{0:T(512)S(1)} %add_rsqrt_fusion), kind=kOutput, calls=%fused_computation.1 | convolution fusion | flops 3628990464 | bytes 11024384 | tf_op jit(solution)/shard_map/dot_general | solution.py:132
  27.5 5.0 %collective-permute-start.7 = (bf16[512,1536]{1,0:T(8,128)(2,1)S(1)}, bf16[512,1536]{1,0:T(8,128)(2,1)}, u32[]{:S(2)}, u32[]{:S(2)}) collective-permute-start(bf16[512,1536]{1,0:T(8,128)(2,1)S(1)} %slice.53.refs_1_.refs_2_), channel_id=1, source_target_pairs={{0,62},{2,0},{4,2},{6,4},{8,6},{10,8},{12,10},{14,12},{16,14},{18,... | collective-permute-start | bytes 4718600 | tf_op jit(solution)/shard_map/ppermute | solution.py:20
  32.6 9.5 %collective-permute-done = bf16[512,1536]{1,0:T(8,128)(2,1)} collective-permute-done((bf16[512,1536]{1,0:T(8,128)(2,1)S(1)}, bf16[512,1536]{1,0:T(8,128)(2,1)}, u32[]{:S(2)}, u32[]{:S(2)}) %collective-permute-start) | collective-permute-done | bytes 1572896 | tf_op jit(solution)/shard_map/ppermute | solution.py:24
  42.0 5.3 %convolution_convert_fusion = bf16[512,2304]{1,0:T(8,128)(2,1)S(1)} fusion(bf16[512,1536]{1,0:T(8,128)(2,1)} %collective-permute-done, bf16[1536,2304]{0,1:T(8,128)(2,1)S(1)} %bitcast.44), kind=kOutput, calls=%fused_computation | convolution fusion | flops 3625058304 | bytes 11010048 | tf_op jit(solution)/shard_map/dot_general | solution.py:137
  50.0 13.5 %shard_map.55 = (f32[1024,768]{1,0:T(8,128)}, f32[1024,768]{1,0:T(8,128)}, f32[1024,768]{1,0:T(8,128)}) custom-call(bf16[1024,768]{1,0:T(8,128)(2,1)} %pad_maximum_fusion.refs_0_.refs_1_, bf16[512,1536]{1,0:T(8,128)(2,1)} %copy-done.2, bf16[512,1536]{1,0:T(8,128)(2,1)} %copy-done.2, bf16[512,1536]{1,0:T(8,128)(2,1)} %slice.52.refs_3_.refs_4_, ...), custom_call_target="tpu_custom_call" | custom-call | tf_op jit(solution)/shard_map/pallas_call | solution.py:108
  65.1 5.9 %collective-permute-start.3 = (bf16[512,1536]{1,0:T(8,128)(2,1)S(1)}, bf16[512,1536]{1,0:T(8,128)(2,1)}, u32[]{:S(2)}, u32[]{:S(2)}) collective-permute-start(bf16[512,1536]{1,0:T(8,128)(2,1)S(1)} %copy-done.3), channel_id=1, source_target_pairs={{0,62},{2,0},{4,2},{6,4},{8,6},{10,8},{12,10},{14,12},{16,14},{18,... | collective-permute-start | bytes 4718600 | tf_op jit(solution)/shard_map/ppermute | solution.py:20
  73.4 8.6 %collective-permute-done.5.refs_2_.refs_3_ = bf16[512,1536]{1,0:T(8,128)(2,1)} collective-permute-done((bf16[512,1536]{1,0:T(8,128)(2,1)S(1)}, bf16[512,1536]{1,0:T(8,128)(2,1)}, u32[]{:S(2)}, u32[]{:S(2)}) %collective-permute-start.5) | collective-permute-done | bytes 1572896 | tf_op jit(solution)/shard_map/ppermute | solution.py:20
  82.1 5.7 %collective-permute-start.8 = (bf16[512,1536]{1,0:T(8,128)(2,1)}, bf16[512,1536]{1,0:T(8,128)(2,1)}, u32[]{:S(2)}, u32[]{:S(2)}) collective-permute-start(bf16[512,1536]{1,0:T(8,128)(2,1)} %collective-permute-done.7.refs_4_.refs_5_), channel_id=1, source_target_pairs={{0,62},{2,0},{4,2},{6,4},{8,6},{10,8},{12,10},{14,12},{16,14},{18,... | collective-permute-start | bytes 4718600 | tf_op jit(solution)/shard_map/ppermute | solution.py:20
  87.8 28.0 %collective-permute-done.1.refs_2_.refs_3_ = bf16[512,1536]{1,0:T(8,128)(2,1)} collective-permute-done((bf16[512,1536]{1,0:T(8,128)(2,1)S(1)}, bf16[512,1536]{1,0:T(8,128)(2,1)}, u32[]{:S(2)}, u32[]{:S(2)}) %collective-permute-start.1) | collective-permute-done | bytes 1572896 | tf_op jit(solution)/shard_map/ppermute | solution.py:20
  115.8 5.7 %collective-permute-start.4 = (bf16[512,1536]{1,0:T(8,128)(2,1)}, bf16[512,1536]{1,0:T(8,128)(2,1)S(1)}, u32[]{:S(2)}, u32[]{:S(2)}) collective-permute-start(bf16[512,1536]{1,0:T(8,128)(2,1)} %collective-permute-done.3.refs_4_.refs_5_), channel_id=1, source_target_pairs={{0,62},{2,0},{4,2},{6,4},{8,6},{10,8},{12,10},{14,12},{16,14},{18,... | collective-permute-start | bytes 4718600 | tf_op jit(solution)/shard_map/ppermute | solution.py:20
  122.6 14.2 %shard_map.56 = (f32[1024,768]{1,0:T(8,128)}, f32[1024,768]{1,0:T(8,128)}, f32[1024,768]{1,0:T(8,128)}) custom-call(f32[1,1024]{1,0:T(1,128)} %bitcast.48, bf16[1024,768]{1,0:T(8,128)(2,1)} %pad_maximum_fusion.refs_0_.refs_1_, bf16[512,1536]{1,0:T(8,128)(2,1)} %collective-permute-done.5.refs_2_.refs_3_, ...), custom_call_target="tpu_custom_call" | custom-call | tf_op jit(solution)/shard_map/pallas_call | solution.py:108
  137.4 14.2 %shard_map.57 = (f32[1024,768]{1,0:T(8,128)}, f32[1024,768]{1,0:T(8,128)}, f32[1024,768]{1,0:T(8,128)}) custom-call(f32[1,1024]{1,0:T(1,128)} %bitcast.49, bf16[1024,768]{1,0:T(8,128)(2,1)} %pad_maximum_fusion.refs_0_.refs_1_, bf16[512,1536]{1,0:T(8,128)(2,1)} %collective-permute-done.1.refs_2_.refs_3_, ...), custom_call_target="tpu_custom_call" | custom-call | tf_op jit(solution)/shard_map/pallas_call | solution.py:108
  151.6 48.4 %collective-permute-done.6.refs_2_.refs_3_ = bf16[512,1536]{1,0:T(8,128)(2,1)} collective-permute-done((bf16[512,1536]{1,0:T(8,128)(2,1)}, bf16[512,1536]{1,0:T(8,128)(2,1)}, u32[]{:S(2)}, u32[]{:S(2)}) %collective-permute-start.6) | collective-permute-done | bytes 1572896 | tf_op jit(solution)/shard_map/ppermute | solution.py:20
  200.7 14.1 %shard_map.58 = (f32[1024,768]{1,0:T(8,128)}, f32[1024,768]{1,0:T(8,128)}, f32[1024,768]{1,0:T(8,128)}) custom-call(f32[1,1024]{1,0:T(1,128)} %bitcast.47, bf16[1024,768]{1,0:T(8,128)(2,1)} %pad_maximum_fusion.refs_0_.refs_1_, bf16[512,1536]{1,0:T(8,128)(2,1)} %collective-permute-done.6.refs_2_.refs_3_, ...), custom_call_target="tpu_custom_call" | custom-call | tf_op jit(solution)/shard_map/pallas_call | solution.py:108
  214.8 18.8 %collective-permute-done.2.refs_2_.refs_3_ = bf16[512,1536]{1,0:T(8,128)(2,1)S(1)} collective-permute-done((bf16[512,1536]{1,0:T(8,128)(2,1)}, bf16[512,1536]{1,0:T(8,128)(2,1)S(1)}, u32[]{:S(2)}, u32[]{:S(2)}) %collective-permute-start.2) | collective-permute-done | bytes 1572896 | tf_op jit(solution)/shard_map/ppermute | solution.py:20
  235.3 9.3 %shard_map.60 = bf16[512,768]{1,0:T(8,128)(2,1)} custom-call(f32[1,1024]{1,0:T(1,128)} %bitcast.45, bf16[1024,768]{1,0:T(8,128)(2,1)} %pad_maximum_fusion.refs_0_.refs_1_, bf16[512,1536]{1,0:T(8,128)(2,1)} %copy-done, bf16[512,1536]{1,0:T(8,128)(2,1)} %copy-done, bf16[512,1536]{1,0:T(8,128)(2,1)} %copy-done.1, bf16[512,1536]{1,0:T(8,128)(2,1)} %copy-done.1, ...), custom_call_target="tpu_custom_call" | custom-call | tf_op jit(solution)/shard_map/pallas_call | solution.py:108
  246.3 3.3 %constant_dynamic-update-slice_fusion.1 = bf16[1536,1536]{1,0:T(8,128)(2,1)} fusion(bf16[768,1536]{1,0:T(8,128)(2,1)} %param.8), kind=kLoop, calls=%fused_computation.28 | loop fusion | bytes 4718592
  249.5 3.3 %constant_dynamic-update-slice_fusion = bf16[1536,1536]{1,0:T(8,128)(2,1)} fusion(bf16[1536,1536]{1,0:T(8,128)(2,1)} %constant_dynamic-update-slice_fusion.1, bf16[768,1536]{1,0:T(8,128)(2,1)} %collective-permute-done.10), kind=kLoop, calls=%fused_computation.27 | loop fusion | bytes 4718592 | tf_op jit(solution)/shard_map/concatenate | solution.py:189
  252.8 9.4 %shard_map.59 = bf16[512,768]{1,0:T(8,128)(2,1)} custom-call(f32[1,1024]{1,0:T(1,128)} %bitcast.46, bf16[1024,768]{1,0:T(8,128)(2,1)} %pad_maximum_fusion.refs_0_.refs_1_, bf16[512,1536]{1,0:T(8,128)(2,1)} %copy-done, bf16[512,1536]{1,0:T(8,128)(2,1)} %copy-done, bf16[512,1536]{1,0:T(8,128)(2,1)} %copy-done.1, bf16[512,1536]{1,0:T(8,128)(2,1)} %copy-done.1, ...), custom_call_target="tpu_custom_call" | custom-call | tf_op jit(solution)/shard_map/pallas_call | solution.py:108
  263.8 3.3 %fusion.21 = bf16[512,768]{1,0:T(8,128)(2,1)S(1)} fusion(bf16[1536,1536]{1,0:T(8,128)(2,1)} %constant_dynamic-update-slice_fusion, s32[]{:T(128)S(6)} %select_n.95, bf16[512,768]{1,0:T(8,128)(2,1)S(1)} %collective-permute-done.9, bf16[512,768]{1,0:T(8,128)(2,1)} %shard_map.59), kind=kOutput, calls=%fused_computation.25 | convolution fusion | flops 1211498496 | bytes 4718596 | tf_op jit(solution)/shard_map/dot_general | solution.py:197
  267.1 2.5 collective-permute-start.11
  269.6 3.0 %fusion.18 = bf16[512,768]{1,0:T(8,128)(2,1)S(1)} fusion(bf16[1536,1536]{1,0:T(8,128)(2,1)} %constant_dynamic-update-slice_fusion, s32[]{:T(128)S(6)} %select_n.93, bf16[512,768]{1,0:T(8,128)(2,1)S(1)} %collective-permute-done.9, bf16[512,768]{1,0:T(8,128)(2,1)S(1)} %copy-done.6), kind=kOutput, calls=%fused_computation.24 | convolution fusion | flops 1211498496 | bytes 4718596 | tf_op jit(solution)/shard_map/dot_general | solution.py:198
  (50 shorter events, 21.4 us)
Async XLA Ops:
  4.6 13.9 %copy-start.5 = (bf16[1,1,512,1536]{3,2,1,0:T(8,128)(2,1)S(1)}, bf16[1,1,512,1536]{3,2,1,0:T(8,128)(2,1)}, u32[]{:S(2)}) copy-start(bf16[1,1,512,1536]{3,2,1,0:T(8,128)(2,1)} %param.5) | copy-start | bytes 4718596
  4.6 37.5 %collective-permute-start = (bf16[512,1536]{1,0:T(8,128)(2,1)S(1)}, bf16[512,1536]{1,0:T(8,128)(2,1)}, u32[]{:S(2)}, u32[]{:S(2)}) collective-permute-start(bf16[512,1536]{1,0:T(8,128)(2,1)S(1)} %fusion.5), channel_id=1, source_target_pairs={{0,1},{1,0},{2,3},{3,2},{4,5},{5,4},{6,7},{7,6},{8,9},{9,8},{10,11... | collective-permute-start | bytes 4718600 | tf_op jit(solution)/shard_map/ppermute | solution.py:24
  18.5 23.5 %copy-start.4 = (bf16[1536,3,768]{0,2,1:T(8,128)(2,1)S(1)}, bf16[1536,3,768]{0,2,1:T(8,128)(2,1)}, u32[]{:S(2)}) copy-start(bf16[1536,3,768]{0,2,1:T(8,128)(2,1)} %copy.6) | copy-start | bytes 21233668
  26.1 21.2 %copy-start.2 = (bf16[512,1536]{1,0:T(8,128)(2,1)}, bf16[512,1536]{1,0:T(8,128)(2,1)S(1)}, u32[]{:S(2)}) copy-start(bf16[512,1536]{1,0:T(8,128)(2,1)S(1)} %slice.53.refs_1_.refs_2_) | copy-start | bytes 4718596
  26.1 56.0 %collective-permute-start.5 = (bf16[512,1536]{1,0:T(8,128)(2,1)S(1)}, bf16[512,1536]{1,0:T(8,128)(2,1)}, u32[]{:S(2)}, u32[]{:S(2)}) collective-permute-start(bf16[512,1536]{1,0:T(8,128)(2,1)S(1)} %slice.53.refs_1_.refs_2_), channel_id=1, source_target_pairs={{0,2},{2,4},{4,6},{6,8},{8,10},{10,12},{12,14},{14,16},{16,18},{18... | collective-permute-start | bytes 4718600 | tf_op jit(solution)/shard_map/ppermute | solution.py:20
  27.5 54.6 %collective-permute-start.7 = (bf16[512,1536]{1,0:T(8,128)(2,1)S(1)}, bf16[512,1536]{1,0:T(8,128)(2,1)}, u32[]{:S(2)}, u32[]{:S(2)}) collective-permute-start(bf16[512,1536]{1,0:T(8,128)(2,1)S(1)} %slice.53.refs_1_.refs_2_), channel_id=1, source_target_pairs={{0,62},{2,0},{4,2},{6,4},{8,6},{10,8},{12,10},{14,12},{16,14},{18,... | collective-permute-start | bytes 4718600 | tf_op jit(solution)/shard_map/ppermute | solution.py:20
  50.0 13.5 %copy-start.3 = (bf16[512,1536]{1,0:T(8,128)(2,1)S(1)}, bf16[512,1536]{1,0:T(8,128)(2,1)}, u32[]{:S(2)}) copy-start(bf16[512,1536]{1,0:T(8,128)(2,1)} %slice.52.refs_3_.refs_4_) | copy-start | bytes 4718596
  50.0 71.5 %copy-start.7 = (s32[1,4,8]{2,1,0:T(4,128)S(1)}, s32[1,4,8]{2,1,0:T(4,128)}, u32[]{:S(2)}) copy-start(s32[1,4,8]{2,1,0:T(4,128)} %param.9) | copy-start | bytes 388
  63.4 52.4 %collective-permute-start.1 = (bf16[512,1536]{1,0:T(8,128)(2,1)S(1)}, bf16[512,1536]{1,0:T(8,128)(2,1)}, u32[]{:S(2)}, u32[]{:S(2)}) collective-permute-start(bf16[512,1536]{1,0:T(8,128)(2,1)S(1)} %copy-done.3), channel_id=1, source_target_pairs={{0,2},{2,4},{4,6},{6,8},{8,10},{10,12},{12,14},{14,16},{16,18},{18... | collective-permute-start | bytes 4718600 | tf_op jit(solution)/shard_map/ppermute | solution.py:20
  65.1 50.7 %collective-permute-start.3 = (bf16[512,1536]{1,0:T(8,128)(2,1)S(1)}, bf16[512,1536]{1,0:T(8,128)(2,1)}, u32[]{:S(2)}, u32[]{:S(2)}) collective-permute-start(bf16[512,1536]{1,0:T(8,128)(2,1)S(1)} %copy-done.3), channel_id=1, source_target_pairs={{0,62},{2,0},{4,2},{6,4},{8,6},{10,8},{12,10},{14,12},{16,14},{18,... | collective-permute-start | bytes 4718600 | tf_op jit(solution)/shard_map/ppermute | solution.py:20
  71.0 178.5 %collective-permute-start.10 = (bf16[768,1536]{1,0:T(8,128)(2,1)}, bf16[768,1536]{1,0:T(8,128)(2,1)}, u32[]{:S(2)}, u32[]{:S(2)}) collective-permute-start(bf16[768,1536]{1,0:T(8,128)(2,1)} %param.8), channel_id=1, source_target_pairs={{0,1},{1,0},{2,3},{3,2},{4,5},{5,4},{6,7},{7,6},{8,9},{9,8},{10,11... | collective-permute-start | bytes 7077896 | tf_op jit(solution)/shard_map/ppermute | solution.py:24
  82.1 118.0 %collective-permute-start.6 = (bf16[512,1536]{1,0:T(8,128)(2,1)}, bf16[512,1536]{1,0:T(8,128)(2,1)}, u32[]{:S(2)}, u32[]{:S(2)}) collective-permute-start(bf16[512,1536]{1,0:T(8,128)(2,1)} %collective-permute-done.5.refs_2_.refs_3_), channel_id=1, source_target_pairs={{0,2},{2,4},{4,6},{6,8},{8,10},{10,12},{12,14},{14,16},{16,18},{18... | collective-permute-start | bytes 4718600 | tf_op jit(solution)/shard_map/ppermute | solution.py:20
  82.1 118.0 %collective-permute-start.8 = (bf16[512,1536]{1,0:T(8,128)(2,1)}, bf16[512,1536]{1,0:T(8,128)(2,1)}, u32[]{:S(2)}, u32[]{:S(2)}) collective-permute-start(bf16[512,1536]{1,0:T(8,128)(2,1)} %collective-permute-done.7.refs_4_.refs_5_), channel_id=1, source_target_pairs={{0,62},{2,0},{4,2},{6,4},{8,6},{10,8},{12,10},{14,12},{16,14},{18,... | collective-permute-start | bytes 4718600 | tf_op jit(solution)/shard_map/ppermute | solution.py:20
  115.8 117.9 %collective-permute-start.2 = (bf16[512,1536]{1,0:T(8,128)(2,1)}, bf16[512,1536]{1,0:T(8,128)(2,1)S(1)}, u32[]{:S(2)}, u32[]{:S(2)}) collective-permute-start(bf16[512,1536]{1,0:T(8,128)(2,1)} %collective-permute-done.1.refs_2_.refs_3_), channel_id=1, source_target_pairs={{0,2},{2,4},{4,6},{6,8},{8,10},{10,12},{12,14},{14,16},{16,18},{18... | collective-permute-start | bytes 4718600 | tf_op jit(solution)/shard_map/ppermute | solution.py:20
  115.8 117.9 %collective-permute-start.4 = (bf16[512,1536]{1,0:T(8,128)(2,1)}, bf16[512,1536]{1,0:T(8,128)(2,1)S(1)}, u32[]{:S(2)}, u32[]{:S(2)}) collective-permute-start(bf16[512,1536]{1,0:T(8,128)(2,1)} %collective-permute-done.3.refs_4_.refs_5_), channel_id=1, source_target_pairs={{0,62},{2,0},{4,2},{6,4},{8,6},{10,8},{12,10},{14,12},{16,14},{18,... | collective-permute-start | bytes 4718600 | tf_op jit(solution)/shard_map/ppermute | solution.py:20
  233.7 1.2 copy-start
  233.7 1.6 copy-start.1
  244.5 19.3 %collective-permute-start.9 = (bf16[512,768]{1,0:T(8,128)(2,1)}, bf16[512,768]{1,0:T(8,128)(2,1)S(1)}, u32[]{:S(2)}, u32[]{:S(2)}) collective-permute-start(bf16[512,768]{1,0:T(8,128)(2,1)} %shard_map.60), channel_id=1, source_target_pairs={{0,1},{1,0},{2,3},{3,2},{4,5},{5,4},{6,7},{7,6},{8,9},{9,8},{10,11... | collective-permute-start | bytes 2359304 | tf_op jit(solution)/shard_map/ppermute | solution.py:24
  262.2 7.4 %copy-start.6 = (bf16[512,768]{1,0:T(8,128)(2,1)S(1)}, bf16[512,768]{1,0:T(8,128)(2,1)}, u32[]{:S(2)}) copy-start(bf16[512,768]{1,0:T(8,128)(2,1)} %shard_map.59) | copy-start | bytes 2359300
  267.1 5.5 %collective-permute-start.11 = (bf16[512,768]{1,0:T(8,128)(2,1)S(1)}, bf16[512,768]{1,0:T(8,128)(2,1)S(1)}, u32[]{:S(2)}, u32[]{:S(2)}) collective-permute-start(bf16[512,768]{1,0:T(8,128)(2,1)S(1)} %fusion.21), channel_id=1, source_target_pairs={{0,64},{64,0},{1,65},{65,1},{2,66},{66,2},{3,67},{67,3},{4,68},{68... | collective-permute-start | bytes 2359304 | tf_op jit(solution)/shard_map/ppermute | solution.py:24

commit v6 on v5

--- a/solution.py
+++ b/solution.py
@@ -6,6 +6,7 @@
 from jax.experimental import pallas as pl
 from jax.experimental.pallas import tpu as pltpu
 from jax.sharding import PartitionSpec as P
+
 
 HEAD_DIM = 128
 REACH = 2
@@ -115,7 +116,7 @@
     )(*operands)
 
 
-def per_device(tokens, modulation, w_qkv, w_out, adjacency):
+def per_device_body(tokens, modulation, w_qkv, w_out, adjacency):
     inputs = tokens[0, 0].astype(jnp.float32)
     width = inputs.shape[1]
     half_heads = w_qkv.shape[2]
@@ -127,7 +128,6 @@
     )
     half_rows = normed.shape[0]
     partner_normed = swap(normed, "tp")
-    w_partner = swap(w_out, "tp")
     flat_w = w_qkv.reshape(width, 3 * half_heads)
     qkv_own = jnp.dot(normed, flat_w, preferred_element_type=jnp.float32).astype(jnp.bfloat16)
     pair_own = qkv_own[:, half_heads:]
@@ -180,30 +180,31 @@
         queries, last_chunks, last_bias, carry,
         first=False, last=True, heads=heads, row_block=1, rows=half_rows,
     )
-    context_partner = swap(context_other, "tp")
+    owner = lax.axis_index("cfg")
+    half_width = width // 2
+    weight_now = jnp.where(owner == 0, guide_scale, 1.0 - guide_scale).astype(jnp.float32)
+    w_mine = lax.dynamic_slice_in_dim(w_out, owner * half_width, half_width, 1)
+    w_theirs = lax.dynamic_slice_in_dim(w_out, (1 - owner) * half_width, half_width, 1)
+
+    def project(context):
+        theirs = weight_now * jnp.dot(context, w_theirs, preferred_element_type=jnp.float32)
+        mine = weight_now * jnp.dot(context, w_mine, preferred_element_type=jnp.float32)
+        return mine + swap(theirs, "cfg")
+
+    to_partner = project(context_other).astype(jnp.bfloat16)
+    to_partner, carry = lax.optimization_barrier((to_partner, carry))
+    from_partner = swap(to_partner, "tp")
     context_own = attend_stage(
         queries, last_chunks, last_bias, carry,
         first=False, last=True, heads=heads, row_block=0, rows=half_rows,
     )
-    context = jnp.concatenate([context_own, context_partner], axis=1)
-    w_local = jnp.concatenate([w_out, w_partner], axis=0)
-
-    owner = lax.axis_index("cfg")
-    half_width = width // 2
-    weight_now = jnp.where(owner == 0, guide_scale, 1.0 - guide_scale).astype(jnp.float32)
-    weight_other = jnp.where(owner == 0, 1.0 - guide_scale, guide_scale).astype(jnp.float32)
-    w_mine = lax.dynamic_slice_in_dim(w_local, owner * half_width, half_width, 1)
-    w_theirs = lax.dynamic_slice_in_dim(w_local, (1 - owner) * half_width, half_width, 1)
-    theirs = jnp.dot(context, w_theirs, preferred_element_type=jnp.float32).astype(jnp.bfloat16)
-    mine = jnp.dot(context, w_mine, preferred_element_type=jnp.float32).astype(jnp.bfloat16)
-    received = swap(theirs, "cfg")
-    guided = weight_now * mine.astype(jnp.float32) + weight_other * received.astype(jnp.float32)
+    guided = project(context_own) + from_partner.astype(jnp.float32)
     return guided.astype(jnp.bfloat16)[None]
 
 
 def solution(mesh):
     return jax.shard_map(
-        per_device,
+        per_device_body,
         mesh=mesh,
         in_specs=(
             P("cfg", "orbit", "tp", None),

time: 275 us -> 238 us (0.87)
  waiting for transfers between devices: 115 us -> 84 us
  local copies, waits for them, and re-layouts: 22.2 us -> 17 us
  starting transfers between devices: 35.6 us -> 32.4 us
    ppermute x8, waiting for transfers between devices: 104 us -> 55 us  [from_behind(): lax.ppermute(array, axis, [(i, (i + by) % count) for i in range(count)])]
    ppermute x4, waiting for transfers between devices: 11.1 us -> 29 us  [swap(): return lax.ppermute(array, axis, [(0, 1), (1, 0)])]
    unnamed x18 -> x15, local copies, waits for them, and re-layouts: 14.5 us -> 10.3 us
    concatenate x1 -> x0, local copies, waits for them, and re-layouts: 3.25 us -> none  [per_device(): w_local = jnp.concatenate([w_out, w_partner], axis=0)]
    ppermute x4, starting transfers between devices: 10.3 us -> 7.29 us  [swap(): return lax.ppermute(array, axis, [(0, 1), (1, 0)])]
    dot_general x4 -> x6, matrix products: 19.1 us -> 19.7 us  [the longest x1 7.59 us: per_device_body(): jnp.dot(normed, flat_w, preferred_element_type=jnp.float32)]
  transfers between devices with their start and end apart: 12 -> 12, of which waited for: 6 -> 6; matrix products, arithmetic and copies ran while one was open for 14% -> 13% of each run, Pallas kernels for 27% -> 24%
where the time goes in v6:
time: 238 us; the launch traced here: 236 us
  waiting for transfers between devices  84 us (35%)
  Pallas kernels  74.3 us (31%)
  starting transfers between devices  32.4 us (14%)
  matrix products  19.7 us (8%)
  local copies, waits for them, and re-layouts  17 us (7%)
  other arithmetic  8.84 us (4%)
    pallas_call x6, Pallas kernels, attend_stage(): pl.pallas_call(kernel, out_shape=out_shape, grid=(heads,), in_specs=in_sp...  74.3 us
    ppermute x8, waiting for transfers between devices, from_behind(): lax.ppermute(array, axis, [(i, (i + by) % count) for i in range(count)])  55 us
    ppermute x4, waiting for transfers between devices, swap(): return lax.ppermute(array, axis, [(0, 1), (1, 0)])  29 us
    ppermute x8, starting transfers between devices, from_behind(): lax.ppermute(array, axis, [(i, (i + by) % count) for i in range(count)])  25.2 us
    unnamed x15, local copies, waits for them, and re-layouts  10.3 us
    dot_general x1, matrix products, per_device_body(): jnp.dot(normed, flat_w, preferred_element_type=jnp.float32)  7.59 us
    ppermute x4, starting transfers between devices, swap(): return lax.ppermute(array, axis, [(0, 1), (1, 0)])  7.29 us
    dot_general x1, matrix products, per_device_body(): jnp.dot(partner_normed, flat_w, preferred_element_type=jnp.float32)  5.29 us
  transfers between devices with their start and end apart: 12, of which 6 were waited for; matrix products, arithmetic and copies ran while one was open for 13% of the time, Pallas kernels for 24%

profile of v6, /device:TPU:1, one launch (start us, length us, event | category | flops | bytes accessed | tf_op | source)
XLA Modules:
  0.0 236.3 jit_solution(4364201447007894976)
XLA Ops:
  0.9 1.9 fusion.2
  4.5 3.6 %collective-permute-start = (bf16[512,1536]{1,0:T(8,128)(2,1)}, bf16[512,1536]{1,0:T(8,128)(2,1)}, u32[]{:S(2)}, u32[]{:S(2)}) collective-permute-start(bf16[512,1536]{1,0:T(8,128)(2,1)} %fusion.5), channel_id=1, source_target_pairs={{0,1},{1,0},{2,3},{3,2},{4,5},{5,4},{6,7},{7,6},{8,9},{9,8},{10,11... | collective-permute-start | bytes 4718600 | tf_op jit(solution)/shard_map/ppermute | solution.py:25
  8.1 10.3 %copy.6 = bf16[1536,3,768]{0,2,1:T(8,128)(2,1)} copy(bf16[1536,3,768]{2,0,1:T(8,128)(2,1)} %param.7) | data formatting | bytes 14155776 | tf_op args[2]
  18.4 7.6 %convolution_convert_fusion.1 = bf16[512,2304]{1,0:T(8,128)(2,1)S(1)} fusion(bf16[1536,2304]{0,1:T(8,128)(2,1)} %bitcast.47, bf16[1,1,512,1536]{3,2,1,0:T(8,128)(2,1)} %param.5, f32[1536]{0:T(1024)S(1)} %get-tuple-element.46, f32[1536]{0:T(1024)S(1)} %get-tuple-element.45, f32[512]{0:T(512)S(1)} %add_rsqrt_fusion), kind=kOutput, calls=%fused_computation.1 | convolution fusion | flops 3628990464 | bytes 11024384 | tf_op jit(solution)/shard_map/dot_general | solution.py:132
  28.7 4.9 %collective-permute-start.7 = (bf16[512,1536]{1,0:T(8,128)(2,1)}, bf16[512,1536]{1,0:T(8,128)(2,1)}, u32[]{:S(2)}, u32[]{:S(2)}) collective-permute-start(bf16[512,1536]{1,0:T(8,128)(2,1)} %slice.53.refs_1_.refs_2_), channel_id=1, source_target_pairs={{0,62},{2,0},{4,2},{6,4},{8,6},{10,8},{12,10},{14,12},{16,14},{18,... | collective-permute-start | bytes 4718600 | tf_op jit(solution)/shard_map/ppermute | solution.py:21
  33.7 8.4 %collective-permute-done = bf16[512,1536]{1,0:T(8,128)(2,1)} collective-permute-done((bf16[512,1536]{1,0:T(8,128)(2,1)}, bf16[512,1536]{1,0:T(8,128)(2,1)}, u32[]{:S(2)}, u32[]{:S(2)}) %collective-permute-start) | collective-permute-done | bytes 1572896 | tf_op jit(solution)/shard_map/ppermute | solution.py:25
  42.1 5.3 %convolution_convert_fusion = bf16[512,2304]{1,0:T(8,128)(2,1)S(1)} fusion(bf16[512,1536]{1,0:T(8,128)(2,1)} %collective-permute-done, bf16[1536,2304]{0,1:T(8,128)(2,1)S(1)} %bitcast.48), kind=kOutput, calls=%fused_computation | convolution fusion | flops 3625058304 | bytes 11010048 | tf_op jit(solution)/shard_map/dot_general | solution.py:137
  51.1 13.3 %shard_map.55 = (f32[1024,768]{1,0:T(8,128)}, f32[1024,768]{1,0:T(8,128)}, f32[1024,768]{1,0:T(8,128)}) custom-call(bf16[1024,768]{1,0:T(8,128)(2,1)} %pad_maximum_fusion.refs_0_.refs_1_, bf16[512,1536]{1,0:T(8,128)(2,1)} %slice.53.refs_1_.refs_2_, bf16[512,1536]{1,0:T(8,128)(2,1)} %slice.53.refs_1_.refs_2_, bf16[512,1536]{1,0:T(8,128)(2,1)} %slice.52.refs_3_.refs_4_, ...), custom_call_target="tpu_custom_call" | custom-call | tf_op jit(solution)/shard_map/pallas_call | solution.py:109
  66.0 5.9 %collective-permute-start.3 = (bf16[512,1536]{1,0:T(8,128)(2,1)}, bf16[512,1536]{1,0:T(8,128)(2,1)}, u32[]{:S(2)}, u32[]{:S(2)}) collective-permute-start(bf16[512,1536]{1,0:T(8,128)(2,1)} %slice.52.refs_3_.refs_4_), channel_id=1, source_target_pairs={{0,62},{2,0},{4,2},{6,4},{8,6},{10,8},{12,10},{14,12},{16,14},{18,... | collective-permute-start | bytes 4718600 | tf_op jit(solution)/shard_map/ppermute | solution.py:21
  71.9 10.2 %collective-permute-done.5.refs_2_.refs_3_ = bf16[512,1536]{1,0:T(8,128)(2,1)} collective-permute-done((bf16[512,1536]{1,0:T(8,128)(2,1)}, bf16[512,1536]{1,0:T(8,128)(2,1)}, u32[]{:S(2)}, u32[]{:S(2)}) %collective-permute-start.5) | collective-permute-done | bytes 1572896 | tf_op jit(solution)/shard_map/ppermute | solution.py:21
  82.1 5.7 %collective-permute-start.8 = (bf16[512,1536]{1,0:T(8,128)(2,1)}, bf16[512,1536]{1,0:T(8,128)(2,1)}, u32[]{:S(2)}, u32[]{:S(2)}) collective-permute-start(bf16[512,1536]{1,0:T(8,128)(2,1)} %collective-permute-done.7.refs_4_.refs_5_), channel_id=1, source_target_pairs={{0,62},{2,0},{4,2},{6,4},{8,6},{10,8},{12,10},{14,12},{16,14},{18,... | collective-permute-start | bytes 4718600 | tf_op jit(solution)/shard_map/ppermute | solution.py:21
  87.8 28.0 %collective-permute-done.1.refs_2_.refs_3_ = bf16[512,1536]{1,0:T(8,128)(2,1)} collective-permute-done((bf16[512,1536]{1,0:T(8,128)(2,1)}, bf16[512,1536]{1,0:T(8,128)(2,1)}, u32[]{:S(2)}, u32[]{:S(2)}) %collective-permute-start.1) | collective-permute-done | bytes 1572896 | tf_op jit(solution)/shard_map/ppermute | solution.py:21
  115.8 5.7 %collective-permute-start.4 = (bf16[512,1536]{1,0:T(8,128)(2,1)}, bf16[512,1536]{1,0:T(8,128)(2,1)}, u32[]{:S(2)}, u32[]{:S(2)}) collective-permute-start(bf16[512,1536]{1,0:T(8,128)(2,1)} %collective-permute-done.3.refs_4_.refs_5_), channel_id=1, source_target_pairs={{0,62},{2,0},{4,2},{6,4},{8,6},{10,8},{12,10},{14,12},{16,14},{18,... | collective-permute-start | bytes 4718600 | tf_op jit(solution)/shard_map/ppermute | solution.py:21
  122.7 14.2 %shard_map.56 = (f32[1024,768]{1,0:T(8,128)}, f32[1024,768]{1,0:T(8,128)}, f32[1024,768]{1,0:T(8,128)}) custom-call(f32[1,1024]{1,0:T(1,128)} %bitcast.52, bf16[1024,768]{1,0:T(8,128)(2,1)} %pad_maximum_fusion.refs_0_.refs_1_, bf16[512,1536]{1,0:T(8,128)(2,1)} %collective-permute-done.5.refs_2_.refs_3_, ...), custom_call_target="tpu_custom_call" | custom-call | tf_op jit(solution)/shard_map/pallas_call | solution.py:109
  137.5 14.2 %shard_map.57 = (f32[1024,768]{1,0:T(8,128)}, f32[1024,768]{1,0:T(8,128)}, f32[1024,768]{1,0:T(8,128)}) custom-call(f32[1,1024]{1,0:T(1,128)} %bitcast.53, bf16[1024,768]{1,0:T(8,128)(2,1)} %pad_maximum_fusion.refs_0_.refs_1_, bf16[512,1536]{1,0:T(8,128)(2,1)} %collective-permute-done.1.refs_2_.refs_3_, ...), custom_call_target="tpu_custom_call" | custom-call | tf_op jit(solution)/shard_map/pallas_call | solution.py:109
  152.3 14.1 %shard_map.58 = (f32[1024,768]{1,0:T(8,128)}, f32[1024,768]{1,0:T(8,128)}, f32[1024,768]{1,0:T(8,128)}) custom-call(f32[1,1024]{1,0:T(1,128)} %bitcast.51, bf16[1024,768]{1,0:T(8,128)(2,1)} %pad_maximum_fusion.refs_0_.refs_1_, bf16[512,1536]{1,0:T(8,128)(2,1)} %collective-permute-done.6.refs_2_.refs_3_, ...), custom_call_target="tpu_custom_call" | custom-call | tf_op jit(solution)/shard_map/pallas_call | solution.py:109
  166.5 16.8 %collective-permute-done.2.refs_2_.refs_3_ = bf16[512,1536]{1,0:T(8,128)(2,1)} collective-permute-done((bf16[512,1536]{1,0:T(8,128)(2,1)}, bf16[512,1536]{1,0:T(8,128)(2,1)}, u32[]{:S(2)}, u32[]{:S(2)}) %collective-permute-start.2) | collective-permute-done | bytes 1572896 | tf_op jit(solution)/shard_map/ppermute | solution.py:21
  183.9 9.3 %shard_map.59 = bf16[512,768]{1,0:T(8,128)(2,1)} custom-call(f32[1,1024]{1,0:T(1,128)} %bitcast.49, bf16[1024,768]{1,0:T(8,128)(2,1)} %pad_maximum_fusion.refs_0_.refs_1_, bf16[512,1536]{1,0:T(8,128)(2,1)} %collective-permute-done.2.refs_2_.refs_3_, bf16[512,1536]{1,0:T(8,128)(2,1)} %collective-permute-done.2.refs_2_.refs_3_, ...), custom_call_target="tpu_custom_call" | custom-call | tf_op jit(solution)/shard_map/pallas_call | solution.py:109
  193.2 3.2 %convolution_multiply_fusion.1 = f32[512,768]{1,0:T(8,128)} fusion(bf16[512,768]{1,0:T(8,128)(2,1)} %shard_map.59, bf16[768,1536]{1,0:T(8,128)(2,1)S(1)} %copy-done, s32[]{:T(128)S(6)} %select_n.91, f32[]{:T(128)S(6)} %select_n.79), kind=kOutput, calls=%fused_computation.21 | convolution fusion | flops 604372992 | bytes 3538952 | tf_op jit(solution)/shard_map/dot_general | solution.py:190
  198.7 2.6 %collective-permute-done.9 = f32[512,768]{1,0:T(8,128)} collective-permute-done((f32[512,768]{1,0:T(8,128)}, f32[512,768]{1,0:T(8,128)}, u32[]{:S(2)}, u32[]{:S(2)}) %collective-permute-start.9) | collective-permute-done | bytes 1572896 | tf_op jit(solution)/shard_map/ppermute | solution.py:25
  203.0 9.3 %shard_map.60 = bf16[512,768]{1,0:T(8,128)(2,1)} custom-call(f32[1,1024]{1,0:T(1,128)} %bitcast.50, bf16[1024,768]{1,0:T(8,128)(2,1)} %pad_maximum_fusion.refs_0_.refs_1_, bf16[512,1536]{1,0:T(8,128)(2,1)} %collective-permute-done.2.refs_2_.refs_3_, bf16[512,1536]{1,0:T(8,128)(2,1)} %collective-permute-done.2.refs_2_.refs_3_, ...), custom_call_target="tpu_custom_call" | custom-call | tf_op jit(solution)/shard_map/pallas_call | solution.py:109
  212.2 2.0 convolution_multiply_fusion
  214.7 1.7 collective-permute-start.11
  217.2 17.9 %collective-permute-done.11 = bf16[512,768]{1,0:T(8,128)(2,1)S(1)} collective-permute-done((bf16[512,768]{1,0:T(8,128)(2,1)S(1)}, bf16[512,768]{1,0:T(8,128)(2,1)S(1)}, u32[]{:S(2)}, u32[]{:S(2)}) %collective-permute-start.11) | collective-permute-done | bytes 786464 | tf_op jit(solution)/shard_map/ppermute | solution.py:25
  (50 shorter events, 20.2 us)
Async XLA Ops:
  0.0 193.2 %copy-start = (bf16[768,1536]{1,0:T(8,128)(2,1)S(1)}, bf16[768,1536]{1,0:T(8,128)(2,1)}, u32[]{:S(2)}) copy-start(bf16[768,1536]{1,0:T(8,128)(2,1)} %param.8) | copy-start | bytes 7077892
  0.0 2.8 %copy-start.2 = (bf16[1,1,512,1536]{3,2,1,0:T(8,128)(2,1)S(1)}, bf16[1,1,512,1536]{3,2,1,0:T(8,128)(2,1)}, u32[]{:S(2)}) copy-start(bf16[1,1,512,1536]{3,2,1,0:T(8,128)(2,1)} %param.5) | copy-start | bytes 4718596
  4.5 37.6 %collective-permute-start = (bf16[512,1536]{1,0:T(8,128)(2,1)}, bf16[512,1536]{1,0:T(8,128)(2,1)}, u32[]{:S(2)}, u32[]{:S(2)}) collective-permute-start(bf16[512,1536]{1,0:T(8,128)(2,1)} %fusion.5), channel_id=1, source_target_pairs={{0,1},{1,0},{2,3},{3,2},{4,5},{5,4},{6,7},{7,6},{8,9},{9,8},{10,11... | collective-permute-start | bytes 4718600 | tf_op jit(solution)/shard_map/ppermute | solution.py:25
  18.4 23.7 %copy-start.1 = (bf16[1536,3,768]{0,2,1:T(8,128)(2,1)S(1)}, bf16[1536,3,768]{0,2,1:T(8,128)(2,1)}, u32[]{:S(2)}) copy-start(bf16[1536,3,768]{0,2,1:T(8,128)(2,1)} %copy.6) | copy-start | bytes 21233668
  26.0 7.7 %copy-start.3 = (bf16[512,2304]{1,0:T(8,128)(2,1)}, bf16[512,2304]{1,0:T(8,128)(2,1)S(1)}, u32[]{:S(2)}) copy-start(bf16[512,2304]{1,0:T(8,128)(2,1)S(1)} %convolution_convert_fusion.1) | copy-start | bytes 7077892
  27.4 54.7 %collective-permute-start.5 = (bf16[512,1536]{1,0:T(8,128)(2,1)}, bf16[512,1536]{1,0:T(8,128)(2,1)}, u32[]{:S(2)}, u32[]{:S(2)}) collective-permute-start(bf16[512,1536]{1,0:T(8,128)(2,1)} %slice.53.refs_1_.refs_2_), channel_id=1, source_target_pairs={{0,2},{2,4},{4,6},{6,8},{8,10},{10,12},{12,14},{14,16},{16,18},{18... | collective-permute-start | bytes 4718600 | tf_op jit(solution)/shard_map/ppermute | solution.py:21
  28.7 53.4 %collective-permute-start.7 = (bf16[512,1536]{1,0:T(8,128)(2,1)}, bf16[512,1536]{1,0:T(8,128)(2,1)}, u32[]{:S(2)}, u32[]{:S(2)}) collective-permute-start(bf16[512,1536]{1,0:T(8,128)(2,1)} %slice.53.refs_1_.refs_2_), channel_id=1, source_target_pairs={{0,62},{2,0},{4,2},{6,4},{8,6},{10,8},{12,10},{14,12},{16,14},{18,... | collective-permute-start | bytes 4718600 | tf_op jit(solution)/shard_map/ppermute | solution.py:21
  47.4 1.1 slice-start
  51.1 70.5 %copy-start.6 = (s32[1,4,8]{2,1,0:T(4,128)S(1)}, s32[1,4,8]{2,1,0:T(4,128)}, u32[]{:S(2)}) copy-start(s32[1,4,8]{2,1,0:T(4,128)} %param.9) | copy-start | bytes 388
  64.4 51.4 %collective-permute-start.1 = (bf16[512,1536]{1,0:T(8,128)(2,1)}, bf16[512,1536]{1,0:T(8,128)(2,1)}, u32[]{:S(2)}, u32[]{:S(2)}) collective-permute-start(bf16[512,1536]{1,0:T(8,128)(2,1)} %slice.52.refs_3_.refs_4_), channel_id=1, source_target_pairs={{0,2},{2,4},{4,6},{6,8},{8,10},{10,12},{12,14},{14,16},{16,18},{18... | collective-permute-start | bytes 4718600 | tf_op jit(solution)/shard_map/ppermute | solution.py:21
  66.0 49.8 %collective-permute-start.3 = (bf16[512,1536]{1,0:T(8,128)(2,1)}, bf16[512,1536]{1,0:T(8,128)(2,1)}, u32[]{:S(2)}, u32[]{:S(2)}) collective-permute-start(bf16[512,1536]{1,0:T(8,128)(2,1)} %slice.52.refs_3_.refs_4_), channel_id=1, source_target_pairs={{0,62},{2,0},{4,2},{6,4},{8,6},{10,8},{12,10},{14,12},{16,14},{18,... | collective-permute-start | bytes 4718600 | tf_op jit(solution)/shard_map/ppermute | solution.py:21
  82.1 69.5 %collective-permute-start.6 = (bf16[512,1536]{1,0:T(8,128)(2,1)}, bf16[512,1536]{1,0:T(8,128)(2,1)}, u32[]{:S(2)}, u32[]{:S(2)}) collective-permute-start(bf16[512,1536]{1,0:T(8,128)(2,1)} %collective-permute-done.5.refs_2_.refs_3_), channel_id=1, source_target_pairs={{0,2},{2,4},{4,6},{6,8},{8,10},{10,12},{12,14},{14,16},{16,18},{18... | collective-permute-start | bytes 4718600 | tf_op jit(solution)/shard_map/ppermute | solution.py:21
  82.1 69.5 %collective-permute-start.8 = (bf16[512,1536]{1,0:T(8,128)(2,1)}, bf16[512,1536]{1,0:T(8,128)(2,1)}, u32[]{:S(2)}, u32[]{:S(2)}) collective-permute-start(bf16[512,1536]{1,0:T(8,128)(2,1)} %collective-permute-done.7.refs_4_.refs_5_), channel_id=1, source_target_pairs={{0,62},{2,0},{4,2},{6,4},{8,6},{10,8},{12,10},{14,12},{16,14},{18,... | collective-permute-start | bytes 4718600 | tf_op jit(solution)/shard_map/ppermute | solution.py:21
  115.8 67.4 %collective-permute-start.2 = (bf16[512,1536]{1,0:T(8,128)(2,1)}, bf16[512,1536]{1,0:T(8,128)(2,1)}, u32[]{:S(2)}, u32[]{:S(2)}) collective-permute-start(bf16[512,1536]{1,0:T(8,128)(2,1)} %collective-permute-done.1.refs_2_.refs_3_), channel_id=1, source_target_pairs={{0,2},{2,4},{4,6},{6,8},{8,10},{10,12},{12,14},{14,16},{16,18},{18... | collective-permute-start | bytes 4718600 | tf_op jit(solution)/shard_map/ppermute | solution.py:21
  115.8 67.4 %collective-permute-start.4 = (bf16[512,1536]{1,0:T(8,128)(2,1)}, bf16[512,1536]{1,0:T(8,128)(2,1)}, u32[]{:S(2)}, u32[]{:S(2)}) collective-permute-start(bf16[512,1536]{1,0:T(8,128)(2,1)} %collective-permute-done.3.refs_4_.refs_5_), channel_id=1, source_target_pairs={{0,62},{2,0},{4,2},{6,4},{8,6},{10,8},{12,10},{14,12},{16,14},{18,... | collective-permute-start | bytes 4718600 | tf_op jit(solution)/shard_map/ppermute | solution.py:21
  193.2 4.8 %copy-start.5 = (bf16[512,768]{1,0:T(8,128)(2,1)S(1)}, bf16[512,768]{1,0:T(8,128)(2,1)}, u32[]{:S(2)}) copy-start(bf16[512,768]{1,0:T(8,128)(2,1)} %shard_map.59) | copy-start | bytes 2359300
  196.4 4.9 %collective-permute-start.9 = (f32[512,768]{1,0:T(8,128)}, f32[512,768]{1,0:T(8,128)}, u32[]{:S(2)}, u32[]{:S(2)}) collective-permute-start(f32[512,768]{1,0:T(8,128)} %convolution_multiply_fusion.1), channel_id=1, source_target_pairs={{0,64},{64,0},{1,65},{65,1},{2,66},{66,2},{3,67},{67,3},{4,68},{68... | collective-permute-start | bytes 4718600 | tf_op jit(solution)/shard_map/ppermute | solution.py:25
  212.2 4.2 %copy-start.4 = (bf16[512,768]{1,0:T(8,128)(2,1)S(1)}, bf16[512,768]{1,0:T(8,128)(2,1)}, u32[]{:S(2)}) copy-start(bf16[512,768]{1,0:T(8,128)(2,1)} %shard_map.60) | copy-start | bytes 2359300
  214.2 20.9 %collective-permute-start.10 = (f32[512,768]{1,0:T(8,128)S(1)}, f32[512,768]{1,0:T(8,128)S(1)}, u32[]{:S(2)}, u32[]{:S(2)}) collective-permute-start(f32[512,768]{1,0:T(8,128)S(1)} %convolution_multiply_fusion), channel_id=1, source_target_pairs={{0,64},{64,0},{1,65},{65,1},{2,66},{66,2},{3,67},{67,3},{4,68},{68... | collective-permute-start | bytes 4718600 | tf_op jit(solution)/shard_map/ppermute | solution.py:25
  214.7 20.5 %collective-permute-start.11 = (bf16[512,768]{1,0:T(8,128)(2,1)S(1)}, bf16[512,768]{1,0:T(8,128)(2,1)S(1)}, u32[]{:S(2)}, u32[]{:S(2)}) collective-permute-start(bf16[512,768]{1,0:T(8,128)(2,1)S(1)} %add_convert_fusion.1), channel_id=1, source_target_pairs={{0,1},{1,0},{2,3},{3,2},{4,5},{5,4},{6,7},{7,6},{8,9},{9,8},{10,11... | collective-permute-start | bytes 2359304 | tf_op jit(solution)/shard_map/ppermute | solution.py:25

commit v7 on v6

--- a/solution.py
+++ b/solution.py
@@ -128,16 +128,24 @@
     )
     half_rows = normed.shape[0]
     partner_normed = swap(normed, "tp")
+    near_own = {sign: from_behind(normed, "orbit", -sign) for sign in (1, -1)}
     flat_w = w_qkv.reshape(width, 3 * half_heads)
+    kv_w = w_qkv[:, 1:, :].reshape(width, 2 * half_heads)
+    near_other = {sign: from_behind(partner_normed, "orbit", -sign) for sign in (1, -1)}
     qkv_own = jnp.dot(normed, flat_w, preferred_element_type=jnp.float32).astype(jnp.bfloat16)
     pair_own = qkv_own[:, half_heads:]
-
-    near_own = {sign: from_behind(pair_own, "orbit", -sign) for sign in (1, -1)}
-
     qkv_other = jnp.dot(partner_normed, flat_w, preferred_element_type=jnp.float32).astype(
         jnp.bfloat16
     )
     pair_other = qkv_other[:, half_heads:]
+
+    def project_pair(rows):
+        return jnp.dot(rows, kv_w, preferred_element_type=jnp.float32).astype(jnp.bfloat16)
+
+    near_own = {sign: project_pair(near_own[sign]) for sign in (1, -1)}
+    far_own = {sign: from_behind(near_own[sign], "orbit", -sign) for sign in (1, -1)}
+    near_other = {sign: project_pair(near_other[sign]) for sign in (1, -1)}
+    far_other = {sign: from_behind(near_other[sign], "orbit", -sign) for sign in (1, -1)}
     queries = jnp.concatenate([qkv_own[:, :half_heads], qkv_other[:, :half_heads]], axis=0)
 
     tp_index = lax.axis_index("tp")
@@ -158,14 +166,10 @@
     carry = attend_stage(
         queries, [pair_own, pair_other], None, None, first=True, last=False, heads=heads
     )
-    pair_other, carry = lax.optimization_barrier((pair_other, carry))
-    near_other = {sign: from_behind(pair_other, "orbit", -sign) for sign in (1, -1)}
-    far_own = {sign: from_behind(near_own[sign], "orbit", -sign) for sign in (1, -1)}
     carry = attend_stage(
         queries, [near_own[-1], near_own[1]], chunk_bias((-1, 1), own_start), carry,
         first=False, last=False, heads=heads,
     )
-    far_other = {sign: from_behind(near_other[sign], "orbit", -sign) for sign in (1, -1)}
     carry = attend_stage(
         queries, [near_other[-1], near_other[1]], chunk_bias((-1, 1), other_start), carry,
         first=False, last=False, heads=heads,

time: 238 us -> 256 us (1.076)
  matrix products: 19.7 us -> 44 us
  waiting for transfers between devices: 84 us -> 72.7 us
  local copies, waits for them, and re-layouts: 17 us -> 20.7 us
    dot_general x0 -> x4, matrix products: none -> 21 us  [project_pair(): jnp.dot(rows, kv_w, preferred_element_type=jnp.float32).astype(jnp.bfloat16)]
    ppermute x8, waiting for transfers between devices: 55 us -> 43.7 us  [from_behind(): lax.ppermute(array, axis, [(i, (i + by) % count) for i in range(count)])]
    slice x0 -> x1, local copies, waits for them, and re-layouts: none -> 4.81 us  [per_device_body(): kv_w = w_qkv[:, 1:, :].reshape(width, 2 * half_heads)]
  transfers between devices with their start and end apart: 12 -> 12, of which waited for: 6 -> 5; matrix products, arithmetic and copies ran while one was open for 13% -> 24% of each run, Pallas kernels for 24% -> 22%
where the time goes in v7:
time: 256 us; the launch traced here: 255 us
  Pallas kernels  74.4 us (29%)
  waiting for transfers between devices  72.7 us (28%)
  matrix products  44 us (17%)
  starting transfers between devices  34.1 us (13%)
  local copies, waits for them, and re-layouts  20.7 us (8%)
  other arithmetic  8.93 us (3%)
    pallas_call x6, Pallas kernels, attend_stage(): pl.pallas_call(kernel, out_shape=out_shape, grid=(heads,), in_specs=in_sp...  74.4 us
    ppermute x8, waiting for transfers between devices, from_behind(): lax.ppermute(array, axis, [(i, (i + by) % count) for i in range(count)])  43.7 us
    ppermute x4, waiting for transfers between devices, swap(): return lax.ppermute(array, axis, [(0, 1), (1, 0)])  29.1 us
    ppermute x8, starting transfers between devices, from_behind(): lax.ppermute(array, axis, [(i, (i + by) % count) for i in range(count)])  25.1 us
    dot_general x4, matrix products, project_pair(): jnp.dot(rows, kv_w, preferred_element_type=jnp.float32).astype(jnp.bfloat16)  21 us
    unnamed x15, local copies, waits for them, and re-layouts  10.3 us
    ppermute x4, starting transfers between devices, swap(): return lax.ppermute(array, axis, [(0, 1), (1, 0)])  8.99 us
    dot_general x1, matrix products, per_device_body(): jnp.dot(normed, flat_w, preferred_element_type=jnp.float32)  8.94 us
  transfers between devices with their start and end apart: 12, of which 5 were waited for; matrix products, arithmetic and copies ran while one was open for 24% of the time, Pallas kernels for 22%

profile of v7, /device:TPU:1, one launch (start us, length us, event | category | flops | bytes accessed | tf_op | source)
XLA Modules:
  0.0 255.0 jit_solution(5988583578324770524)
XLA Ops:
  4.5 3.6 %collective-permute-start = (bf16[512,1536]{1,0:T(8,128)(2,1)}, bf16[512,1536]{1,0:T(8,128)(2,1)}, u32[]{:S(2)}, u32[]{:S(2)}) collective-permute-start(bf16[512,1536]{1,0:T(8,128)(2,1)} %fusion.5), channel_id=1, source_target_pairs={{0,1},{1,0},{2,3},{3,2},{4,5},{5,4},{6,7},{7,6},{8,9},{9,8},{10,11... | collective-permute-start | bytes 4718600 | tf_op jit(solution)/shard_map/ppermute | solution.py:25
  9.4 4.9 %collective-permute-start.7 = (bf16[512,1536]{1,0:T(8,128)(2,1)}, bf16[512,1536]{1,0:T(8,128)(2,1)}, u32[]{:S(2)}, u32[]{:S(2)}) collective-permute-start(bf16[512,1536]{1,0:T(8,128)(2,1)} %fusion.5), channel_id=1, source_target_pairs={{0,62},{2,0},{4,2},{6,4},{8,6},{10,8},{12,10},{14,12},{16,14},{18,... | collective-permute-start | bytes 4718600 | tf_op jit(solution)/shard_map/ppermute | solution.py:21
  14.3 10.3 %copy.6 = bf16[1536,3,768]{0,2,1:T(8,128)(2,1)} copy(bf16[1536,3,768]{2,0,1:T(8,128)(2,1)} %param.7) | data formatting | bytes 14155776 | tf_op args[2]
  24.7 8.9 %convolution_convert_fusion.1 = bf16[512,2304]{1,0:T(8,128)(2,1)} fusion(bf16[1536,2304]{0,1:T(8,128)(2,1)} %bitcast.56, bf16[1,1,512,1536]{3,2,1,0:T(8,128)(2,1)} %param.5, f32[1536]{0:T(1024)S(1)} %get-tuple-element.38, f32[1536]{0:T(1024)S(1)} %get-tuple-element.37, f32[512]{0:T(512)S(1)} %add_rsqrt_fusion), kind=kOutput, calls=%fused_computation.1 | convolution fusion | flops 3628990464 | bytes 11024384 | tf_op jit(solution)/shard_map/dot_general | solution.py:135
  33.6 8.5 %collective-permute-done = bf16[512,1536]{1,0:T(8,128)(2,1)} collective-permute-done((bf16[512,1536]{1,0:T(8,128)(2,1)}, bf16[512,1536]{1,0:T(8,128)(2,1)}, u32[]{:S(2)}, u32[]{:S(2)}) %collective-permute-start) | collective-permute-done | bytes 1572896 | tf_op jit(solution)/shard_map/ppermute | solution.py:25
  43.8 4.8 %slice.56 = bf16[1536,2,768]{0,2,1:T(8,128)(2,1)} slice(bf16[1536,3,768]{0,2,1:T(8,128)(2,1)} %copy.6), slice={[0:1536], [1:3], [0:768]} | slice | bytes 9437184 | tf_op jit(solution)/shard_map/slice | solution.py:133
  48.7 5.9 %collective-permute-start.3 = (bf16[512,1536]{1,0:T(8,128)(2,1)}, bf16[512,1536]{1,0:T(8,128)(2,1)S(1)}, u32[]{:S(2)}, u32[]{:S(2)}) collective-permute-start(bf16[512,1536]{1,0:T(8,128)(2,1)} %collective-permute-done), channel_id=1, source_target_pairs={{0,62},{2,0},{4,2},{6,4},{8,6},{10,8},{12,10},{14,12},{16,14},{18,... | collective-permute-start | bytes 4718600 | tf_op jit(solution)/shard_map/ppermute | solution.py:21
  54.5 27.7 %collective-permute-done.5 = bf16[512,1536]{1,0:T(8,128)(2,1)} collective-permute-done((bf16[512,1536]{1,0:T(8,128)(2,1)}, bf16[512,1536]{1,0:T(8,128)(2,1)}, u32[]{:S(2)}, u32[]{:S(2)}) %collective-permute-start.5) | collective-permute-done | bytes 1572896 | tf_op jit(solution)/shard_map/ppermute | solution.py:21
  82.2 6.8 %convolution_convert_fusion.3.refs_2_.refs_3_ = bf16[512,1536]{1,0:T(8,128)(2,1)} fusion(bf16[512,1536]{1,0:T(8,128)(2,1)} %collective-permute-done.5, bf16[1536,1536]{0,1:T(8,128)(2,1)} %bitcast.58), kind=kOutput, calls=%fused_computation.14 | convolution fusion | flops 2416705536 | bytes 7864320 | tf_op jit(solution)/shard_map/dot_general | solution.py:143
  89.0 5.2 %convolution_convert_fusion.2.refs_4_.refs_5_ = bf16[512,1536]{1,0:T(8,128)(2,1)} fusion(bf16[512,1536]{1,0:T(8,128)(2,1)} %collective-permute-done.7, bf16[1536,1536]{0,1:T(8,128)(2,1)S(1)} %bitcast.59), kind=kOutput, calls=%fused_computation.13 | convolution fusion | flops 2416705536 | bytes 7864320 | tf_op jit(solution)/shard_map/dot_general | solution.py:143
  94.2 5.7 %collective-permute-start.8 = (bf16[512,1536]{1,0:T(8,128)(2,1)}, bf16[512,1536]{1,0:T(8,128)(2,1)}, u32[]{:S(2)}, u32[]{:S(2)}) collective-permute-start(bf16[512,1536]{1,0:T(8,128)(2,1)} %convolution_convert_fusion.2.refs_4_.refs_5_), channel_id=1, source_target_pairs={{0,62},{2,0},{4,2},{6,4},{8,6},{10,8},{12,10},{14,12},{16,14},{18,... | collective-permute-start | bytes 4718600 | tf_op jit(solution)/shard_map/ppermute | solution.py:21
  99.9 16.0 %collective-permute-done.1 = bf16[512,1536]{1,0:T(8,128)(2,1)} collective-permute-done((bf16[512,1536]{1,0:T(8,128)(2,1)}, bf16[512,1536]{1,0:T(8,128)(2,1)}, u32[]{:S(2)}, u32[]{:S(2)}) %collective-permute-start.1) | collective-permute-done | bytes 1572896 | tf_op jit(solution)/shard_map/ppermute | solution.py:21
  115.9 5.2 %convolution_convert_fusion.5.refs_2_.refs_3_ = bf16[512,1536]{1,0:T(8,128)(2,1)} fusion(bf16[512,1536]{1,0:T(8,128)(2,1)} %collective-permute-done.1, bf16[1536,1536]{0,1:T(8,128)(2,1)S(1)} %bitcast.60), kind=kOutput, calls=%fused_computation.16 | convolution fusion | flops 2416705536 | bytes 7864320 | tf_op jit(solution)/shard_map/dot_general | solution.py:143
  121.1 3.8 %convolution_convert_fusion.4.refs_4_.refs_5_ = bf16[512,1536]{1,0:T(8,128)(2,1)} fusion(bf16[512,1536]{1,0:T(8,128)(2,1)S(1)} %collective-permute-done.3, bf16[1536,1536]{0,1:T(8,128)(2,1)S(1)} %bitcast.61), kind=kOutput, calls=%fused_computation.15 | convolution fusion | flops 2416705536 | bytes 7864320 | tf_op jit(solution)/shard_map/dot_general | solution.py:143
  124.9 5.7 %collective-permute-start.4 = (bf16[512,1536]{1,0:T(8,128)(2,1)}, bf16[512,1536]{1,0:T(8,128)(2,1)}, u32[]{:S(2)}, u32[]{:S(2)}) collective-permute-start(bf16[512,1536]{1,0:T(8,128)(2,1)} %convolution_convert_fusion.4.refs_4_.refs_5_), channel_id=1, source_target_pairs={{0,62},{2,0},{4,2},{6,4},{8,6},{10,8},{12,10},{14,12},{16,14},{18,... | collective-permute-start | bytes 4718600 | tf_op jit(solution)/shard_map/ppermute | solution.py:21
  132.3 7.3 %convolution_convert_fusion = bf16[512,2304]{1,0:T(8,128)(2,1)S(1)} fusion(bf16[512,1536]{1,0:T(8,128)(2,1)} %collective-permute-done, bf16[1536,2304]{0,1:T(8,128)(2,1)} %bitcast.57), kind=kOutput, calls=%fused_computation | convolution fusion | flops 3625058304 | bytes 11010048 | tf_op jit(solution)/shard_map/dot_general | solution.py:137
  142.4 13.3 %shard_map.55 = (f32[1024,768]{1,0:T(8,128)}, f32[1024,768]{1,0:T(8,128)}, f32[1024,768]{1,0:T(8,128)}) custom-call(bf16[1024,768]{1,0:T(8,128)(2,1)} %pad_maximum_fusion.refs_0_.refs_1_, bf16[512,1536]{1,0:T(8,128)(2,1)} %slice.57.refs_1_.refs_2_, bf16[512,1536]{1,0:T(8,128)(2,1)} %slice.57.refs_1_.refs_2_, bf16[512,1536]{1,0:T(8,128)(2,1)} %slice.58.refs_3_.refs_4_, ...), custom_call_target="tpu_custom_call" | custom-call | tf_op jit(solution)/shard_map/pallas_call | solution.py:109
  156.4 14.2 %shard_map.56 = (f32[1024,768]{1,0:T(8,128)}, f32[1024,768]{1,0:T(8,128)}, f32[1024,768]{1,0:T(8,128)}) custom-call(f32[1,1024]{1,0:T(1,128)} %bitcast.65, bf16[1024,768]{1,0:T(8,128)(2,1)} %pad_maximum_fusion.refs_0_.refs_1_, bf16[512,1536]{1,0:T(8,128)(2,1)} %convolution_convert_fusion.3.refs_2_.refs_3_, ...), custom_call_target="tpu_custom_call" | custom-call | tf_op jit(solution)/shard_map/pallas_call | solution.py:109
  171.2 14.1 %shard_map.57 = (f32[1024,768]{1,0:T(8,128)}, f32[1024,768]{1,0:T(8,128)}, f32[1024,768]{1,0:T(8,128)}) custom-call(f32[1,1024]{1,0:T(1,128)} %bitcast.66, bf16[1024,768]{1,0:T(8,128)(2,1)} %pad_maximum_fusion.refs_0_.refs_1_, bf16[512,1536]{1,0:T(8,128)(2,1)} %convolution_convert_fusion.5.refs_2_.refs_3_, ...), custom_call_target="tpu_custom_call" | custom-call | tf_op jit(solution)/shard_map/pallas_call | solution.py:109
  186.0 14.2 %shard_map.58 = (f32[1024,768]{1,0:T(8,128)}, f32[1024,768]{1,0:T(8,128)}, f32[1024,768]{1,0:T(8,128)}) custom-call(f32[1,1024]{1,0:T(1,128)} %bitcast.64, bf16[1024,768]{1,0:T(8,128)(2,1)} %pad_maximum_fusion.refs_0_.refs_1_, bf16[512,1536]{1,0:T(8,128)(2,1)} %collective-permute-done.6.refs_2_.refs_3_, ...), custom_call_target="tpu_custom_call" | custom-call | tf_op jit(solution)/shard_map/pallas_call | solution.py:109
  200.9 9.3 %shard_map.59 = bf16[512,768]{1,0:T(8,128)(2,1)} custom-call(f32[1,1024]{1,0:T(1,128)} %bitcast.62, bf16[1024,768]{1,0:T(8,128)(2,1)} %pad_maximum_fusion.refs_0_.refs_1_, bf16[512,1536]{1,0:T(8,128)(2,1)} %collective-permute-done.2.refs_2_.refs_3_, bf16[512,1536]{1,0:T(8,128)(2,1)} %collective-permute-done.2.refs_2_.refs_3_, ...), custom_call_target="tpu_custom_call" | custom-call | tf_op jit(solution)/shard_map/pallas_call | solution.py:109
  213.3 3.2 %collective-permute-start.9 = (f32[512,768]{1,0:T(8,128)}, f32[512,768]{1,0:T(8,128)}, u32[]{:S(2)}, u32[]{:S(2)}) collective-permute-start(f32[512,768]{1,0:T(8,128)} %convolution_multiply_fusion.1), channel_id=1, source_target_pairs={{0,64},{64,0},{1,65},{65,1},{2,66},{66,2},{3,67},{67,3},{4,68},{68... | collective-permute-start | bytes 4718600 | tf_op jit(solution)/shard_map/ppermute | solution.py:25
  221.6 9.3 %shard_map.60 = bf16[512,768]{1,0:T(8,128)(2,1)} custom-call(f32[1,1024]{1,0:T(1,128)} %bitcast.63, bf16[1024,768]{1,0:T(8,128)(2,1)} %pad_maximum_fusion.refs_0_.refs_1_, bf16[512,1536]{1,0:T(8,128)(2,1)} %collective-permute-done.2.refs_2_.refs_3_, bf16[512,1536]{1,0:T(8,128)(2,1)} %collective-permute-done.2.refs_2_.refs_3_, ...), custom_call_target="tpu_custom_call" | custom-call | tf_op jit(solution)/shard_map/pallas_call | solution.py:109
  235.9 17.9 %collective-permute-done.11 = bf16[512,768]{1,0:T(8,128)(2,1)S(1)} collective-permute-done((bf16[512,768]{1,0:T(8,128)(2,1)S(1)}, bf16[512,768]{1,0:T(8,128)(2,1)S(1)}, u32[]{:S(2)}, u32[]{:S(2)}) %collective-permute-start.11) | collective-permute-done | bytes 786464 | tf_op jit(solution)/shard_map/ppermute | solution.py:25
  (55 shorter events, 29.0 us)
Async XLA Ops:
  0.0 210.2 %copy-start = (bf16[768,1536]{1,0:T(8,128)(2,1)S(1)}, bf16[768,1536]{1,0:T(8,128)(2,1)}, u32[]{:S(2)}) copy-start(bf16[768,1536]{1,0:T(8,128)(2,1)} %param.8) | copy-start | bytes 7077892
  0.0 2.8 %copy-start.1 = (bf16[1,1,512,1536]{3,2,1,0:T(8,128)(2,1)S(1)}, bf16[1,1,512,1536]{3,2,1,0:T(8,128)(2,1)}, u32[]{:S(2)}) copy-start(bf16[1,1,512,1536]{3,2,1,0:T(8,128)(2,1)} %param.5) | copy-start | bytes 4718596
  4.5 37.6 %collective-permute-start = (bf16[512,1536]{1,0:T(8,128)(2,1)}, bf16[512,1536]{1,0:T(8,128)(2,1)}, u32[]{:S(2)}, u32[]{:S(2)}) collective-permute-start(bf16[512,1536]{1,0:T(8,128)(2,1)} %fusion.5), channel_id=1, source_target_pairs={{0,1},{1,0},{2,3},{3,2},{4,5},{5,4},{6,7},{7,6},{8,9},{9,8},{10,11... | collective-permute-start | bytes 4718600 | tf_op jit(solution)/shard_map/ppermute | solution.py:25
  8.1 74.1 %collective-permute-start.5 = (bf16[512,1536]{1,0:T(8,128)(2,1)}, bf16[512,1536]{1,0:T(8,128)(2,1)}, u32[]{:S(2)}, u32[]{:S(2)}) collective-permute-start(bf16[512,1536]{1,0:T(8,128)(2,1)} %fusion.5), channel_id=1, source_target_pairs={{0,2},{2,4},{4,6},{6,8},{8,10},{10,12},{12,14},{14,16},{16,18},{18... | collective-permute-start | bytes 4718600 | tf_op jit(solution)/shard_map/ppermute | solution.py:21
  9.4 79.6 %collective-permute-start.7 = (bf16[512,1536]{1,0:T(8,128)(2,1)}, bf16[512,1536]{1,0:T(8,128)(2,1)}, u32[]{:S(2)}, u32[]{:S(2)}) collective-permute-start(bf16[512,1536]{1,0:T(8,128)(2,1)} %fusion.5), channel_id=1, source_target_pairs={{0,62},{2,0},{4,2},{6,4},{8,6},{10,8},{12,10},{14,12},{16,14},{18,... | collective-permute-start | bytes 4718600 | tf_op jit(solution)/shard_map/ppermute | solution.py:21
  24.6 19.1 %copy-start.6 = (s32[1,4,8]{2,1,0:T(4,128)S(1)}, s32[1,4,8]{2,1,0:T(4,128)}, u32[]{:S(2)}) copy-start(s32[1,4,8]{2,1,0:T(4,128)} %param.9) | copy-start | bytes 388
  42.1 73.8 %collective-permute-start.1 = (bf16[512,1536]{1,0:T(8,128)(2,1)}, bf16[512,1536]{1,0:T(8,128)(2,1)}, u32[]{:S(2)}, u32[]{:S(2)}) collective-permute-start(bf16[512,1536]{1,0:T(8,128)(2,1)} %collective-permute-done), channel_id=1, source_target_pairs={{0,2},{2,4},{4,6},{6,8},{8,10},{10,12},{12,14},{14,16},{16,18},{18... | collective-permute-start | bytes 4718600 | tf_op jit(solution)/shard_map/ppermute | solution.py:21
  48.7 72.4 %collective-permute-start.3 = (bf16[512,1536]{1,0:T(8,128)(2,1)}, bf16[512,1536]{1,0:T(8,128)(2,1)S(1)}, u32[]{:S(2)}, u32[]{:S(2)}) collective-permute-start(bf16[512,1536]{1,0:T(8,128)(2,1)} %collective-permute-done), channel_id=1, source_target_pairs={{0,62},{2,0},{4,2},{6,4},{8,6},{10,8},{12,10},{14,12},{16,14},{18,... | collective-permute-start | bytes 4718600 | tf_op jit(solution)/shard_map/ppermute | solution.py:21
  82.2 6.8 %copy-start.2 = (bf16[1536,2,768]{0,2,1:T(8,128)(2,1)S(1)}, bf16[1536,2,768]{0,2,1:T(8,128)(2,1)}, u32[]{:S(2)}) copy-start(bf16[1536,2,768]{0,2,1:T(8,128)(2,1)} %slice.56) | copy-start | bytes 14155780
  89.0 96.3 %collective-permute-start.6 = (bf16[512,1536]{1,0:T(8,128)(2,1)}, bf16[512,1536]{1,0:T(8,128)(2,1)}, u32[]{:S(2)}, u32[]{:S(2)}) collective-permute-start(bf16[512,1536]{1,0:T(8,128)(2,1)} %convolution_convert_fusion.3.refs_2_.refs_3_), channel_id=1, source_target_pairs={{0,2},{2,4},{4,6},{6,8},{8,10},{10,12},{12,14},{14,16},{16,18},{18... | collective-permute-start | bytes 4718600 | tf_op jit(solution)/shard_map/ppermute | solution.py:21
  94.2 91.1 %collective-permute-start.8 = (bf16[512,1536]{1,0:T(8,128)(2,1)}, bf16[512,1536]{1,0:T(8,128)(2,1)}, u32[]{:S(2)}, u32[]{:S(2)}) collective-permute-start(bf16[512,1536]{1,0:T(8,128)(2,1)} %convolution_convert_fusion.2.refs_4_.refs_5_), channel_id=1, source_target_pairs={{0,62},{2,0},{4,2},{6,4},{8,6},{10,8},{12,10},{14,12},{16,14},{18,... | collective-permute-start | bytes 4718600 | tf_op jit(solution)/shard_map/ppermute | solution.py:21
  121.1 79.1 %collective-permute-start.2 = (bf16[512,1536]{1,0:T(8,128)(2,1)}, bf16[512,1536]{1,0:T(8,128)(2,1)}, u32[]{:S(2)}, u32[]{:S(2)}) collective-permute-start(bf16[512,1536]{1,0:T(8,128)(2,1)} %convolution_convert_fusion.5.refs_2_.refs_3_), channel_id=1, source_target_pairs={{0,2},{2,4},{4,6},{6,8},{8,10},{10,12},{12,14},{14,16},{16,18},{18... | collective-permute-start | bytes 4718600 | tf_op jit(solution)/shard_map/ppermute | solution.py:21
  121.1 9.5 %copy-start.3 = (bf16[512,2304]{1,0:T(8,128)(2,1)S(1)}, bf16[512,2304]{1,0:T(8,128)(2,1)}, u32[]{:S(2)}) copy-start(bf16[512,2304]{1,0:T(8,128)(2,1)} %convolution_convert_fusion.1) | copy-start | bytes 7077892
  124.9 75.3 %collective-permute-start.4 = (bf16[512,1536]{1,0:T(8,128)(2,1)}, bf16[512,1536]{1,0:T(8,128)(2,1)}, u32[]{:S(2)}, u32[]{:S(2)}) collective-permute-start(bf16[512,1536]{1,0:T(8,128)(2,1)} %convolution_convert_fusion.4.refs_4_.refs_5_), channel_id=1, source_target_pairs={{0,62},{2,0},{4,2},{6,4},{8,6},{10,8},{12,10},{14,12},{16,14},{18,... | collective-permute-start | bytes 4718600 | tf_op jit(solution)/shard_map/ppermute | solution.py:21
  139.7 1.4 slice-start
  210.2 6.4 %copy-start.5 = (bf16[512,768]{1,0:T(8,128)(2,1)S(1)}, bf16[512,768]{1,0:T(8,128)(2,1)}, u32[]{:S(2)}) copy-start(bf16[512,768]{1,0:T(8,128)(2,1)} %shard_map.59) | copy-start | bytes 2359300
  213.3 6.6 %collective-permute-start.9 = (f32[512,768]{1,0:T(8,128)}, f32[512,768]{1,0:T(8,128)}, u32[]{:S(2)}, u32[]{:S(2)}) collective-permute-start(f32[512,768]{1,0:T(8,128)} %convolution_multiply_fusion.1), channel_id=1, source_target_pairs={{0,64},{64,0},{1,65},{65,1},{2,66},{66,2},{3,67},{67,3},{4,68},{68... | collective-permute-start | bytes 4718600 | tf_op jit(solution)/shard_map/ppermute | solution.py:25
  230.9 4.2 %copy-start.4 = (bf16[512,768]{1,0:T(8,128)(2,1)S(1)}, bf16[512,768]{1,0:T(8,128)(2,1)}, u32[]{:S(2)}) copy-start(bf16[512,768]{1,0:T(8,128)(2,1)} %shard_map.60) | copy-start | bytes 2359300
  232.9 20.9 %collective-permute-start.10 = (f32[512,768]{1,0:T(8,128)S(1)}, f32[512,768]{1,0:T(8,128)S(1)}, u32[]{:S(2)}, u32[]{:S(2)}) collective-permute-start(f32[512,768]{1,0:T(8,128)S(1)} %convolution_multiply_fusion), channel_id=1, source_target_pairs={{0,64},{64,0},{1,65},{65,1},{2,66},{66,2},{3,67},{67,3},{4,68},{68... | collective-permute-start | bytes 4718600 | tf_op jit(solution)/shard_map/ppermute | solution.py:25
  233.3 20.5 %collective-permute-start.11 = (bf16[512,768]{1,0:T(8,128)(2,1)S(1)}, bf16[512,768]{1,0:T(8,128)(2,1)S(1)}, u32[]{:S(2)}, u32[]{:S(2)}) collective-permute-start(bf16[512,768]{1,0:T(8,128)(2,1)S(1)} %add_convert_fusion.1), channel_id=1, source_target_pairs={{0,1},{1,0},{2,3},{3,2},{4,5},{5,4},{6,7},{7,6},{8,9},{9,8},{10,11... | collective-permute-start | bytes 2359304 | tf_op jit(solution)/shard_map/ppermute | solution.py:25

commit v8 on v6

--- a/solution.py
+++ b/solution.py
@@ -128,30 +128,33 @@
     )
     half_rows = normed.shape[0]
     partner_normed = swap(normed, "tp")
-    flat_w = w_qkv.reshape(width, 3 * half_heads)
-    qkv_own = jnp.dot(normed, flat_w, preferred_element_type=jnp.float32).astype(jnp.bfloat16)
-    pair_own = qkv_own[:, half_heads:]
-
-    near_own = {sign: from_behind(pair_own, "orbit", -sign) for sign in (1, -1)}
-
-    qkv_other = jnp.dot(partner_normed, flat_w, preferred_element_type=jnp.float32).astype(
+    kv_w = w_qkv[:, 1:, :].reshape(width, 2 * half_heads)
+    q_w = w_qkv[:, 0, :]
+    pair_own = jnp.dot(normed, kv_w, preferred_element_type=jnp.float32).astype(jnp.bfloat16)
+
+    piece_rows = half_rows // 2
+    own_pieces = [pair_own[:piece_rows], pair_own[piece_rows:]]
+    near = {sign: [from_behind(piece, "orbit", -sign) for piece in own_pieces] for sign in (1, -1)}
+
+    pair_other = jnp.dot(partner_normed, kv_w, preferred_element_type=jnp.float32).astype(
         jnp.bfloat16
     )
-    pair_other = qkv_other[:, half_heads:]
-    queries = jnp.concatenate([qkv_own[:, :half_heads], qkv_other[:, :half_heads]], axis=0)
+    both_rows = jnp.concatenate([normed, partner_normed], axis=0)
+    queries = jnp.dot(both_rows, q_w, preferred_element_type=jnp.float32).astype(jnp.bfloat16)
 
     tp_index = lax.axis_index("tp")
     flags = adjacency[0]
     blocks = flags.shape[1]
-    per_chunk = blocks // 2
-    own_start = tp_index * per_chunk
-    other_start = (1 - tp_index) * per_chunk
-
-    def chunk_bias(offsets, start):
+    per_piece = blocks // 4
+    own_start = tp_index * 2 * per_piece
+    other_start = (1 - tp_index) * 2 * per_piece
+    starts = [own_start, own_start + per_piece, other_start, other_start + per_piece]
+
+    def chunk_bias(offsets, piece):
         rows_of = []
         for offset in offsets:
             row = flags[offset + REACH if offset < 0 else offset + REACH - 1]
-            rows_of.append(lax.dynamic_slice_in_dim(row, start, per_chunk))
+            rows_of.append(lax.dynamic_slice_in_dim(row, starts[piece], per_piece))
         allowed = jnp.repeat(jnp.concatenate(rows_of), BLOCK) > 0
         return jnp.where(allowed, 0.0, -1e30).astype(jnp.float32)[None, :]
 
@@ -159,27 +162,42 @@
         queries, [pair_own, pair_other], None, None, first=True, last=False, heads=heads
     )
     pair_other, carry = lax.optimization_barrier((pair_other, carry))
-    near_other = {sign: from_behind(pair_other, "orbit", -sign) for sign in (1, -1)}
-    far_own = {sign: from_behind(near_own[sign], "orbit", -sign) for sign in (1, -1)}
-    carry = attend_stage(
-        queries, [near_own[-1], near_own[1]], chunk_bias((-1, 1), own_start), carry,
-        first=False, last=False, heads=heads,
-    )
-    far_other = {sign: from_behind(near_other[sign], "orbit", -sign) for sign in (1, -1)}
-    carry = attend_stage(
-        queries, [near_other[-1], near_other[1]], chunk_bias((-1, 1), other_start), carry,
-        first=False, last=False, heads=heads,
-    )
-    carry = attend_stage(
-        queries, [far_own[-1], far_own[1]], chunk_bias((-2, 2), own_start), carry,
-        first=False, last=False, heads=heads,
-    )
-    last_chunks = [far_other[-1], far_other[1]]
-    last_bias = chunk_bias((-2, 2), other_start)
+    for sign in (1, -1):
+        near[sign] += [from_behind(pair_other[:piece_rows], "orbit", -sign),
+                       from_behind(pair_other[piece_rows:], "orbit", -sign)]
+    far = {sign: [from_behind(piece, "orbit", -sign) for piece in near[sign]] for sign in (1, -1)}
+
+    def near_stage(pieces_of, carry):
+        chunks = []
+        biases = []
+        for piece in pieces_of:
+            chunks += [near[-1][piece], near[1][piece]]
+            biases.append(chunk_bias((-1, 1), piece))
+        return attend_stage(
+            queries, chunks, jnp.concatenate(biases, axis=1), carry,
+            first=False, last=False, heads=heads,
+        )
+
+    def far_chunks(pieces_of):
+        chunks = []
+        biases = []
+        for piece in pieces_of:
+            chunks += [far[-1][piece], far[1][piece]]
+            biases.append(chunk_bias((-2, 2), piece))
+        return chunks, jnp.concatenate(biases, axis=1)
+
+    carry = near_stage([0, 1], carry)
+    carry = near_stage([2, 3], carry)
+    chunks, bias = far_chunks([0, 1])
+    carry = attend_stage(queries, chunks, bias, carry, first=False, last=False, heads=heads)
+    chunks, bias = far_chunks([2])
+    carry = attend_stage(queries, chunks, bias, carry, first=False, last=False, heads=heads)
+    last_chunks, last_bias = far_chunks([3])
     context_other = attend_stage(
         queries, last_chunks, last_bias, carry,
         first=False, last=True, heads=heads, row_block=1, rows=half_rows,
     )
+
     owner = lax.axis_index("cfg")
     half_width = width // 2
     weight_now = jnp.where(owner == 0, guide_scale, 1.0 - guide_scale).astype(jnp.float32)

time: 238 us -> 280 us (1.18)
  starting transfers between devices: 32.4 us -> 54.1 us
  Pallas kernels: 74.3 us -> 88.3 us
  matrix products: 19.7 us -> 25.2 us
    ppermute x8 -> x16, starting transfers between devices: 25.2 us -> 40.5 us  [from_behind(): lax.ppermute(array, axis, [(i, (i + by) % count) for i in range(count)])]
    pallas_call x6 -> x7, Pallas kernels: 74.3 us -> 88.3 us  [attend_stage(): pl.pallas_call(kernel, out_shape=out_shape, grid=(heads,), in_specs=in_sp...]
    ppermute x4, waiting for transfers between devices: 29 us -> 20.5 us  [swap(): return lax.ppermute(array, axis, [(0, 1), (1, 0)])]
    ppermute x8 -> x16, waiting for transfers between devices: 55 us -> 62.9 us  [from_behind(): lax.ppermute(array, axis, [(i, (i + by) % count) for i in range(count)])]
    ppermute x4, starting transfers between devices: 7.29 us -> 13.6 us  [swap(): return lax.ppermute(array, axis, [(0, 1), (1, 0)])]
    dot_general x2 -> x3, matrix products: 12.9 us -> 18.5 us  [the longest x1 6.64 us: per_device_body(): jnp.dot(partner_normed, kv_w, preferred_element_type=jnp.float32)]
    slice x5 -> x3, local copies, waits for them, and re-layouts: 3.85 us -> 8.42 us  [the longest x1 4.82 us: per_device_body(): kv_w = w_qkv[:, 1:, :].reshape(width, 2 * half_heads)]
    unnamed x15 -> x17, local copies, waits for them, and re-layouts: 10.3 us -> 7.94 us
  transfers between devices with their start and end apart: 12 -> 20, of which waited for: 6 -> 5; matrix products, arithmetic and copies ran while one was open for 13% -> 14% of each run, Pallas kernels for 24% -> 26%
where the time goes in v8:
time: 280 us; the launch traced here: 279 us
  Pallas kernels  88.3 us (32%)
  waiting for transfers between devices  83.5 us (30%)
  starting transfers between devices  54.1 us (19%)
  matrix products  25.2 us (9%)
  local copies, waits for them, and re-layouts  18.3 us (7%)
  other arithmetic  9.67 us (3%)
    pallas_call x7, Pallas kernels, attend_stage(): pl.pallas_call(kernel, out_shape=out_shape, grid=(heads,), in_specs=in_sp...  88.3 us
    ppermute x16, waiting for transfers between devices, from_behind(): lax.ppermute(array, axis, [(i, (i + by) % count) for i in range(count)])  62.9 us
    ppermute x16, starting transfers between devices, from_behind(): lax.ppermute(array, axis, [(i, (i + by) % count) for i in range(count)])  40.5 us
    ppermute x4, waiting for transfers between devices, swap(): return lax.ppermute(array, axis, [(0, 1), (1, 0)])  20.5 us
    ppermute x4, starting transfers between devices, swap(): return lax.ppermute(array, axis, [(0, 1), (1, 0)])  13.6 us
    unnamed x17, local copies, waits for them, and re-layouts  7.94 us
    dot_general x1, matrix products, per_device_body(): jnp.dot(partner_normed, kv_w, preferred_element_type=jnp.float32)  6.64 us
    dot_general x1, matrix products, per_device_body(): jnp.dot(both_rows, q_w, preferred_element_type=jnp.float32)  6.36 us
  transfers between devices with their start and end apart: 20, of which 5 were waited for; matrix products, arithmetic and copies ran while one was open for 14% of the time, Pallas kernels for 26%

profile of v8, /device:TPU:1, one launch (start us, length us, event | category | flops | bytes accessed | tf_op | source)
XLA Modules:
  0.0 279.2 jit_solution(4571835338727769113)
XLA Ops:
  8.1 4.8 %slice.61 = bf16[1536,2,768]{2,0,1:T(8,128)(2,1)} slice(bf16[1536,3,768]{2,0,1:T(8,128)(2,1)} %param.7), slice={[0:1536], [1:3], [0:768]} | slice | bytes 9437184 | tf_op jit(solution)/shard_map/slice | solution.py:131
  12.9 6.7 %copy.7 = bf16[1536,2,768]{0,2,1:T(8,128)(2,1)} copy(bf16[1536,2,768]{2,0,1:T(8,128)(2,1)} %slice.61) | data formatting | bytes 9437184
  19.5 5.5 %convolution_convert_fusion.refs_1_.refs_2_ = bf16[512,1536]{1,0:T(8,128)(2,1)S(1)} fusion(bf16[1536,1536]{0,1:T(8,128)(2,1)} %bitcast.72, bf16[1,1,512,1536]{3,2,1,0:T(8,128)(2,1)} %param.5, f32[1536]{0:T(1024)S(1)} %get-tuple-element.52, f32[1536]{0:T(1024)S(1)} %get-tuple-element.51, f32[512]{0:T(512)S(1)} %add_rsqrt_fusion), kind=kOutput, calls=%fused_computation.15 | convolution fusion | flops 2420637696 | bytes 7878656 | tf_op jit(solution)/shard_map/dot_general | solution.py:133
  28.7 4.9 %collective-permute-start.11 = (bf16[256,1536]{1,0:T(8,128)(2,1)}, bf16[256,1536]{1,0:T(8,128)(2,1)}, u32[]{:S(2)}, u32[]{:S(2)}) collective-permute-start(bf16[256,1536]{1,0:T(8,128)(2,1)} %get-tuple-element.54), channel_id=1, source_target_pairs={{0,62},{2,0},{4,2},{6,4},{8,6},{10,8},{12,10},{14,12},{16,14},{18,... | collective-permute-start | bytes 2359304 | tf_op jit(solution)/shard_map/ppermute | solution.py:21
  33.7 5.7 %collective-permute-start.15 = (bf16[256,1536]{1,0:T(8,128)(2,1)}, bf16[256,1536]{1,0:T(8,128)(2,1)}, u32[]{:S(2)}, u32[]{:S(2)}) collective-permute-start(bf16[256,1536]{1,0:T(8,128)(2,1)} %get-tuple-element.53), channel_id=1, source_target_pairs={{0,62},{2,0},{4,2},{6,4},{8,6},{10,8},{12,10},{14,12},{16,14},{18,... | collective-permute-start | bytes 2359304 | tf_op jit(solution)/shard_map/ppermute | solution.py:21
  39.3 25.8 %collective-permute-done.9.refs_2_.refs_3_ = bf16[256,1536]{1,0:T(8,128)(2,1)S(1)} collective-permute-done((bf16[256,1536]{1,0:T(8,128)(2,1)}, bf16[256,1536]{1,0:T(8,128)(2,1)S(1)}, u32[]{:S(2)}, u32[]{:S(2)}) %collective-permute-start.9) | collective-permute-done | bytes 786464 | tf_op jit(solution)/shard_map/ppermute | solution.py:21
  65.2 5.7 %collective-permute-start.12 = (bf16[256,1536]{1,0:T(8,128)(2,1)}, bf16[256,1536]{1,0:T(8,128)(2,1)}, u32[]{:S(2)}, u32[]{:S(2)}) collective-permute-start(bf16[256,1536]{1,0:T(8,128)(2,1)} %collective-permute-done.11.refs_4_.refs_5_), channel_id=1, source_target_pairs={{0,62},{2,0},{4,2},{6,4},{8,6},{10,8},{12,10},{14,12},{16,14},{18,... | collective-permute-start | bytes 2359304 | tf_op jit(solution)/shard_map/ppermute | solution.py:21
  70.9 11.3 %collective-permute-done.13.refs_6_.refs_7_ = bf16[256,1536]{1,0:T(8,128)(2,1)} collective-permute-done((bf16[256,1536]{1,0:T(8,128)(2,1)}, bf16[256,1536]{1,0:T(8,128)(2,1)}, u32[]{:S(2)}, u32[]{:S(2)}) %collective-permute-start.13) | collective-permute-done | bytes 786464 | tf_op jit(solution)/shard_map/ppermute | solution.py:21
  82.1 6.6 %convolution_convert_fusion.1.refs_3_.refs_4_ = bf16[512,1536]{1,0:T(8,128)(2,1)} fusion(bf16[512,1536]{1,0:T(8,128)(2,1)} %collective-permute-done, bf16[1536,1536]{0,1:T(8,128)(2,1)} %bitcast.73), kind=kOutput, calls=%fused_computation.16 | convolution fusion | flops 2416705536 | bytes 7864320 | tf_op jit(solution)/shard_map/dot_general | solution.py:139
  88.8 6.4 %fusion.15.refs_0_.refs_1_ = bf16[1024,768]{1,0:T(8,128)(2,1)} fusion(bf16[1536,3,768]{2,0,1:T(8,128)(2,1)} %param.7, bf16[512,1536]{1,0:T(8,128)(2,1)} %collective-permute-done, bf16[512,1536]{1,0:T(8,128)(2,1)} %fusion.5), kind=kOutput, calls=%fused_computation.19 | convolution fusion | flops 2422996992 | bytes 7077888 | tf_op jit(solution)/shard_map/dot_general | solution.py:143
  95.1 13.4 %shard_map.55 = (f32[1024,768]{1,0:T(8,128)}, f32[1024,768]{1,0:T(8,128)}, f32[1024,768]{1,0:T(8,128)}) custom-call(bf16[1024,768]{1,0:T(8,128)(2,1)} %fusion.15.refs_0_.refs_1_, bf16[512,1536]{1,0:T(8,128)(2,1)} %copy-done.1, bf16[512,1536]{1,0:T(8,128)(2,1)} %copy-done.1, bf16[512,1536]{1,0:T(8,128)(2,1)} %convolution_convert_fusion.1.refs_3_.refs_4_, ...), custom_call_target="tpu_custom_call" | custom-call | tf_op jit(solution)/shard_map/pallas_call | solution.py:109
  110.9 5.7 %collective-permute-start.3 = (bf16[256,1536]{1,0:T(8,128)(2,1)}, bf16[256,1536]{1,0:T(8,128)(2,1)}, u32[]{:S(2)}, u32[]{:S(2)}) collective-permute-start(bf16[256,1536]{1,0:T(8,128)(2,1)} %get-tuple-element.56), channel_id=1, source_target_pairs={{0,62},{2,0},{4,2},{6,4},{8,6},{10,8},{12,10},{14,12},{16,14},{18,... | collective-permute-start | bytes 2359304 | tf_op jit(solution)/shard_map/ppermute | solution.py:21
  116.7 5.7 %collective-permute-start.7 = (bf16[256,1536]{1,0:T(8,128)(2,1)S(1)}, bf16[256,1536]{1,0:T(8,128)(2,1)}, u32[]{:S(2)}, u32[]{:S(2)}) collective-permute-start(bf16[256,1536]{1,0:T(8,128)(2,1)S(1)} %get-tuple-element.55), channel_id=1, source_target_pairs={{0,62},{2,0},{4,2},{6,4},{8,6},{10,8},{12,10},{14,12},{16,14},{18,... | collective-permute-start | bytes 2359304 | tf_op jit(solution)/shard_map/ppermute | solution.py:21
  122.9 25.8 %collective-permute-done.5.refs_2_.refs_3_ = bf16[256,1536]{1,0:T(8,128)(2,1)} collective-permute-done((bf16[256,1536]{1,0:T(8,128)(2,1)S(1)}, bf16[256,1536]{1,0:T(8,128)(2,1)}, u32[]{:S(2)}, u32[]{:S(2)}) %collective-permute-start.5) | collective-permute-done | bytes 786464 | tf_op jit(solution)/shard_map/ppermute | solution.py:21
  148.8 5.7 %collective-permute-start.8 = (bf16[256,1536]{1,0:T(8,128)(2,1)}, bf16[256,1536]{1,0:T(8,128)(2,1)}, u32[]{:S(2)}, u32[]{:S(2)}) collective-permute-start(bf16[256,1536]{1,0:T(8,128)(2,1)} %collective-permute-done.7.refs_4_.refs_5_), channel_id=1, source_target_pairs={{0,62},{2,0},{4,2},{6,4},{8,6},{10,8},{12,10},{14,12},{16,14},{18,... | collective-permute-start | bytes 2359304 | tf_op jit(solution)/shard_map/ppermute | solution.py:21
  154.4 5.7 %collective-permute-start.4 = (bf16[256,1536]{1,0:T(8,128)(2,1)}, bf16[256,1536]{1,0:T(8,128)(2,1)}, u32[]{:S(2)}, u32[]{:S(2)}) collective-permute-start(bf16[256,1536]{1,0:T(8,128)(2,1)} %collective-permute-done.3.refs_8_.refs_9_), channel_id=1, source_target_pairs={{0,62},{2,0},{4,2},{6,4},{8,6},{10,8},{12,10},{14,12},{16,14},{18,... | collective-permute-start | bytes 2359304 | tf_op jit(solution)/shard_map/ppermute | solution.py:21
  162.7 16.0 %shard_map.56 = (f32[1024,768]{1,0:T(8,128)}, f32[1024,768]{1,0:T(8,128)}, f32[1024,768]{1,0:T(8,128)}) custom-call(f32[1,1024]{1,0:T(1,128)} %pad_maximum_fusion.2.refs_0_, bf16[1024,768]{1,0:T(8,128)(2,1)} %fusion.15.refs_0_.refs_1_, bf16[256,1536]{1,0:T(8,128)(2,1)} %copy-done.4, bf16[256,1536]{1,0:T(8,128)(2,1)} %copy-done.4, ...), custom_call_target="tpu_custom_call" | custom-call | tf_op jit(solution)/shard_map/pallas_call | solution.py:109
  178.7 16.0 %shard_map.57 = (f32[1024,768]{1,0:T(8,128)}, f32[1024,768]{1,0:T(8,128)}, f32[1024,768]{1,0:T(8,128)}) custom-call(f32[1,1024]{1,0:T(1,128)} %pad_maximum_fusion.1.refs_0_, bf16[1024,768]{1,0:T(8,128)(2,1)} %fusion.15.refs_0_.refs_1_, bf16[256,1536]{1,0:T(8,128)(2,1)} %collective-permute-done.5.refs_2_.refs_3_, ...), custom_call_target="tpu_custom_call" | custom-call | tf_op jit(solution)/shard_map/pallas_call | solution.py:109
  194.7 16.0 %shard_map.58 = (f32[1024,768]{1,0:T(8,128)}, f32[1024,768]{1,0:T(8,128)}, f32[1024,768]{1,0:T(8,128)}) custom-call(f32[1,1024]{1,0:T(1,128)} %pad_maximum_fusion.refs_0_, bf16[1024,768]{1,0:T(8,128)(2,1)} %fusion.15.refs_0_.refs_1_, bf16[256,1536]{1,0:T(8,128)(2,1)} %collective-permute-done.10.refs_2_.refs_3_, ...), custom_call_target="tpu_custom_call" | custom-call | tf_op jit(solution)/shard_map/pallas_call | solution.py:109
  211.4 11.8 %shard_map.59 = (f32[1024,768]{1,0:T(8,128)}, f32[1024,768]{1,0:T(8,128)}, f32[1024,768]{1,0:T(8,128)}) custom-call(f32[1,512]{1,0:T(1,128)} %bitcast.82, bf16[1024,768]{1,0:T(8,128)(2,1)} %fusion.15.refs_0_.refs_1_, bf16[256,1536]{1,0:T(8,128)(2,1)} %collective-permute-done.6.refs_2_.refs_3_, bf16[256,1536]{1,0:T(8,128)(2,1)} %collective-permute-done.6.refs_2_.refs_3_, ...), custom_call_target="tpu_custom_call" | custom-call | tf_op jit(solution)/shard_map/pallas_call | solution.py:109
  224.1 7.5 %shard_map.60 = bf16[512,768]{1,0:T(8,128)(2,1)} custom-call(f32[1,512]{1,0:T(1,128)} %bitcast.74, bf16[1024,768]{1,0:T(8,128)(2,1)} %fusion.15.refs_0_.refs_1_, bf16[256,1536]{1,0:T(8,128)(2,1)} %copy-done.2, bf16[256,1536]{1,0:T(8,128)(2,1)} %copy-done.2, bf16[256,1536]{1,0:T(8,128)(2,1)} %collective-permute-done.4.refs_4_.refs_5_, ...), custom_call_target="tpu_custom_call" | custom-call | tf_op jit(solution)/shard_map/pallas_call | solution.py:109
  234.7 7.8 %collective-permute-start.17 = (f32[512,768]{1,0:T(8,128)}, f32[512,768]{1,0:T(8,128)}, u32[]{:S(2)}, u32[]{:S(2)}) collective-permute-start(f32[512,768]{1,0:T(8,128)} %convolution_multiply_fusion.1), channel_id=1, source_target_pairs={{0,64},{64,0},{1,65},{65,1},{2,66},{66,2},{3,67},{67,3},{4,68},{68... | collective-permute-start | bytes 4718600 | tf_op jit(solution)/shard_map/ppermute | solution.py:25
  247.6 7.5 %shard_map.61 = bf16[512,768]{1,0:T(8,128)(2,1)} custom-call(f32[1,512]{1,0:T(1,128)} %bitcast.75, bf16[1024,768]{1,0:T(8,128)(2,1)} %fusion.15.refs_0_.refs_1_, bf16[256,1536]{1,0:T(8,128)(2,1)} %copy-done.2, bf16[256,1536]{1,0:T(8,128)(2,1)} %copy-done.2, bf16[256,1536]{1,0:T(8,128)(2,1)} %collective-permute-done.4.refs_4_.refs_5_, ...), custom_call_target="tpu_custom_call" | custom-call | tf_op jit(solution)/shard_map/pallas_call | solution.py:109
  260.1 17.9 %collective-permute-done.19 = bf16[512,768]{1,0:T(8,128)(2,1)S(1)} collective-permute-done((bf16[512,768]{1,0:T(8,128)(2,1)S(1)}, bf16[512,768]{1,0:T(8,128)(2,1)S(1)}, u32[]{:S(2)}, u32[]{:S(2)}) %collective-permute-start.19) | collective-permute-done | bytes 786464 | tf_op jit(solution)/shard_map/ppermute | solution.py:25
  (78 shorter events, 33.0 us)
Async XLA Ops:
  0.0 231.6 %copy-start = (bf16[768,1536]{1,0:T(8,128)(2,1)S(1)}, bf16[768,1536]{1,0:T(8,128)(2,1)}, u32[]{:S(2)}) copy-start(bf16[768,1536]{1,0:T(8,128)(2,1)} %param.8) | copy-start | bytes 7077892
  4.5 77.6 %collective-permute-start = (bf16[512,1536]{1,0:T(8,128)(2,1)}, bf16[512,1536]{1,0:T(8,128)(2,1)}, u32[]{:S(2)}, u32[]{:S(2)}) collective-permute-start(bf16[512,1536]{1,0:T(8,128)(2,1)} %fusion.5), channel_id=1, source_target_pairs={{0,1},{1,0},{2,3},{3,2},{4,5},{5,4},{6,7},{7,6},{8,9},{9,8},{10,11... | collective-permute-start | bytes 4718600 | tf_op jit(solution)/shard_map/ppermute | solution.py:25
  27.4 37.8 %collective-permute-start.9 = (bf16[256,1536]{1,0:T(8,128)(2,1)}, bf16[256,1536]{1,0:T(8,128)(2,1)S(1)}, u32[]{:S(2)}, u32[]{:S(2)}) collective-permute-start(bf16[256,1536]{1,0:T(8,128)(2,1)} %get-tuple-element.54), channel_id=1, source_target_pairs={{0,2},{2,4},{4,6},{6,8},{8,10},{10,12},{12,14},{14,16},{16,18},{18... | collective-permute-start | bytes 2359304 | tf_op jit(solution)/shard_map/ppermute | solution.py:21
  28.7 36.5 %collective-permute-start.11 = (bf16[256,1536]{1,0:T(8,128)(2,1)}, bf16[256,1536]{1,0:T(8,128)(2,1)}, u32[]{:S(2)}, u32[]{:S(2)}) collective-permute-start(bf16[256,1536]{1,0:T(8,128)(2,1)} %get-tuple-element.54), channel_id=1, source_target_pairs={{0,62},{2,0},{4,2},{6,4},{8,6},{10,8},{12,10},{14,12},{16,14},{18,... | collective-permute-start | bytes 2359304 | tf_op jit(solution)/shard_map/ppermute | solution.py:21
  33.7 48.5 %collective-permute-start.13 = (bf16[256,1536]{1,0:T(8,128)(2,1)}, bf16[256,1536]{1,0:T(8,128)(2,1)}, u32[]{:S(2)}, u32[]{:S(2)}) collective-permute-start(bf16[256,1536]{1,0:T(8,128)(2,1)} %get-tuple-element.53), channel_id=1, source_target_pairs={{0,2},{2,4},{4,6},{6,8},{8,10},{10,12},{12,14},{14,16},{16,18},{18... | collective-permute-start | bytes 2359304 | tf_op jit(solution)/shard_map/ppermute | solution.py:21
  33.7 77.3 %collective-permute-start.15 = (bf16[256,1536]{1,0:T(8,128)(2,1)}, bf16[256,1536]{1,0:T(8,128)(2,1)}, u32[]{:S(2)}, u32[]{:S(2)}) collective-permute-start(bf16[256,1536]{1,0:T(8,128)(2,1)} %get-tuple-element.53), channel_id=1, source_target_pairs={{0,62},{2,0},{4,2},{6,4},{8,6},{10,8},{12,10},{14,12},{16,14},{18,... | collective-permute-start | bytes 2359304 | tf_op jit(solution)/shard_map/ppermute | solution.py:21
  65.2 23.6 %copy-start.4 = (bf16[256,1536]{1,0:T(8,128)(2,1)}, bf16[256,1536]{1,0:T(8,128)(2,1)S(1)}, u32[]{:S(2)}) copy-start(bf16[256,1536]{1,0:T(8,128)(2,1)S(1)} %collective-permute-done.9.refs_2_.refs_3_) | copy-start | bytes 2359300
  65.2 51.5 %collective-permute-start.10 = (bf16[256,1536]{1,0:T(8,128)(2,1)S(1)}, bf16[256,1536]{1,0:T(8,128)(2,1)}, u32[]{:S(2)}, u32[]{:S(2)}) collective-permute-start(bf16[256,1536]{1,0:T(8,128)(2,1)S(1)} %collective-permute-done.9.refs_2_.refs_3_), channel_id=1, source_target_pairs={{0,2},{2,4},{4,6},{6,8},{8,10},{10,12},{12,14},{14,16},{16,18},{18... | collective-permute-start | bytes 2359304 | tf_op jit(solution)/shard_map/ppermute | solution.py:21
  65.2 51.5 %collective-permute-start.12 = (bf16[256,1536]{1,0:T(8,128)(2,1)}, bf16[256,1536]{1,0:T(8,128)(2,1)}, u32[]{:S(2)}, u32[]{:S(2)}) collective-permute-start(bf16[256,1536]{1,0:T(8,128)(2,1)} %collective-permute-done.11.refs_4_.refs_5_), channel_id=1, source_target_pairs={{0,62},{2,0},{4,2},{6,4},{8,6},{10,8},{12,10},{14,12},{16,14},{18,... | collective-permute-start | bytes 2359304 | tf_op jit(solution)/shard_map/ppermute | solution.py:21
  82.1 40.7 %collective-permute-start.14 = (bf16[256,1536]{1,0:T(8,128)(2,1)}, bf16[256,1536]{1,0:T(8,128)(2,1)}, u32[]{:S(2)}, u32[]{:S(2)}) collective-permute-start(bf16[256,1536]{1,0:T(8,128)(2,1)} %collective-permute-done.13.refs_6_.refs_7_), channel_id=1, source_target_pairs={{0,2},{2,4},{4,6},{6,8},{8,10},{10,12},{12,14},{14,16},{16,18},{18... | collective-permute-start | bytes 2359304 | tf_op jit(solution)/shard_map/ppermute | solution.py:21
  108.6 13.8 %copy-start.7 = (s32[1,4,8]{2,1,0:T(4,128)S(1)}, s32[1,4,8]{2,1,0:T(4,128)}, u32[]{:S(2)}) copy-start(s32[1,4,8]{2,1,0:T(4,128)} %param.9) | copy-start | bytes 388
  110.9 43.5 %collective-permute-start.1 = (bf16[256,1536]{1,0:T(8,128)(2,1)}, bf16[256,1536]{1,0:T(8,128)(2,1)}, u32[]{:S(2)}, u32[]{:S(2)}) collective-permute-start(bf16[256,1536]{1,0:T(8,128)(2,1)} %get-tuple-element.56), channel_id=1, source_target_pairs={{0,2},{2,4},{4,6},{6,8},{8,10},{10,12},{12,14},{14,16},{16,18},{18... | collective-permute-start | bytes 2359304 | tf_op jit(solution)/shard_map/ppermute | solution.py:21
  110.9 43.5 %collective-permute-start.3 = (bf16[256,1536]{1,0:T(8,128)(2,1)}, bf16[256,1536]{1,0:T(8,128)(2,1)}, u32[]{:S(2)}, u32[]{:S(2)}) collective-permute-start(bf16[256,1536]{1,0:T(8,128)(2,1)} %get-tuple-element.56), channel_id=1, source_target_pairs={{0,62},{2,0},{4,2},{6,4},{8,6},{10,8},{12,10},{14,12},{16,14},{18,... | collective-permute-start | bytes 2359304 | tf_op jit(solution)/shard_map/ppermute | solution.py:21
  116.7 32.1 %collective-permute-start.5 = (bf16[256,1536]{1,0:T(8,128)(2,1)S(1)}, bf16[256,1536]{1,0:T(8,128)(2,1)}, u32[]{:S(2)}, u32[]{:S(2)}) collective-permute-start(bf16[256,1536]{1,0:T(8,128)(2,1)S(1)} %get-tuple-element.55), channel_id=1, source_target_pairs={{0,2},{2,4},{4,6},{6,8},{8,10},{10,12},{12,14},{14,16},{16,18},{18... | collective-permute-start | bytes 2359304 | tf_op jit(solution)/shard_map/ppermute | solution.py:21
  116.7 32.1 %collective-permute-start.7 = (bf16[256,1536]{1,0:T(8,128)(2,1)S(1)}, bf16[256,1536]{1,0:T(8,128)(2,1)}, u32[]{:S(2)}, u32[]{:S(2)}) collective-permute-start(bf16[256,1536]{1,0:T(8,128)(2,1)S(1)} %get-tuple-element.55), channel_id=1, source_target_pairs={{0,62},{2,0},{4,2},{6,4},{8,6},{10,8},{12,10},{14,12},{16,14},{18,... | collective-permute-start | bytes 2359304 | tf_op jit(solution)/shard_map/ppermute | solution.py:21
  122.9 71.8 %collective-permute-start.16 = (bf16[256,1536]{1,0:T(8,128)(2,1)}, bf16[256,1536]{1,0:T(8,128)(2,1)}, u32[]{:S(2)}, u32[]{:S(2)}) collective-permute-start(bf16[256,1536]{1,0:T(8,128)(2,1)} %collective-permute-done.15.refs_8_.refs_9_), channel_id=1, source_target_pairs={{0,62},{2,0},{4,2},{6,4},{8,6},{10,8},{12,10},{14,12},{16,14},{18,... | collective-permute-start | bytes 2359304 | tf_op jit(solution)/shard_map/ppermute | solution.py:21
  148.7 62.0 %collective-permute-start.6 = (bf16[256,1536]{1,0:T(8,128)(2,1)}, bf16[256,1536]{1,0:T(8,128)(2,1)}, u32[]{:S(2)}, u32[]{:S(2)}) collective-permute-start(bf16[256,1536]{1,0:T(8,128)(2,1)} %collective-permute-done.5.refs_2_.refs_3_), channel_id=1, source_target_pairs={{0,2},{2,4},{4,6},{6,8},{8,10},{10,12},{12,14},{14,16},{16,18},{18... | collective-permute-start | bytes 2359304 | tf_op jit(solution)/shard_map/ppermute | solution.py:21
  148.8 62.0 %collective-permute-start.8 = (bf16[256,1536]{1,0:T(8,128)(2,1)}, bf16[256,1536]{1,0:T(8,128)(2,1)}, u32[]{:S(2)}, u32[]{:S(2)}) collective-permute-start(bf16[256,1536]{1,0:T(8,128)(2,1)} %collective-permute-done.7.refs_4_.refs_5_), channel_id=1, source_target_pairs={{0,62},{2,0},{4,2},{6,4},{8,6},{10,8},{12,10},{14,12},{16,14},{18,... | collective-permute-start | bytes 2359304 | tf_op jit(solution)/shard_map/ppermute | solution.py:21
  154.4 68.8 %collective-permute-start.2 = (bf16[256,1536]{1,0:T(8,128)(2,1)}, bf16[256,1536]{1,0:T(8,128)(2,1)S(1)}, u32[]{:S(2)}, u32[]{:S(2)}) collective-permute-start(bf16[256,1536]{1,0:T(8,128)(2,1)} %collective-permute-done.1.refs_6_.refs_7_), channel_id=1, source_target_pairs={{0,2},{2,4},{4,6},{6,8},{8,10},{10,12},{12,14},{14,16},{16,18},{18... | collective-permute-start | bytes 2359304 | tf_op jit(solution)/shard_map/ppermute | solution.py:21
  154.4 68.8 %collective-permute-start.4 = (bf16[256,1536]{1,0:T(8,128)(2,1)}, bf16[256,1536]{1,0:T(8,128)(2,1)}, u32[]{:S(2)}, u32[]{:S(2)}) collective-permute-start(bf16[256,1536]{1,0:T(8,128)(2,1)} %collective-permute-done.3.refs_8_.refs_9_), channel_id=1, source_target_pairs={{0,62},{2,0},{4,2},{6,4},{8,6},{10,8},{12,10},{14,12},{16,14},{18,... | collective-permute-start | bytes 2359304 | tf_op jit(solution)/shard_map/ppermute | solution.py:21
  231.6 11.0 %copy-start.6 = (bf16[512,768]{1,0:T(8,128)(2,1)S(1)}, bf16[512,768]{1,0:T(8,128)(2,1)}, u32[]{:S(2)}) copy-start(bf16[512,768]{1,0:T(8,128)(2,1)} %shard_map.60) | copy-start | bytes 2359300
  234.7 11.2 %collective-permute-start.17 = (f32[512,768]{1,0:T(8,128)}, f32[512,768]{1,0:T(8,128)}, u32[]{:S(2)}, u32[]{:S(2)}) collective-permute-start(f32[512,768]{1,0:T(8,128)} %convolution_multiply_fusion.1), channel_id=1, source_target_pairs={{0,64},{64,0},{1,65},{65,1},{2,66},{66,2},{3,67},{67,3},{4,68},{68... | collective-permute-start | bytes 4718600 | tf_op jit(solution)/shard_map/ppermute | solution.py:25
  257.1 20.9 %collective-permute-start.18 = (f32[512,768]{1,0:T(8,128)S(1)}, f32[512,768]{1,0:T(8,128)S(1)}, u32[]{:S(2)}, u32[]{:S(2)}) collective-permute-start(f32[512,768]{1,0:T(8,128)S(1)} %convolution_multiply_fusion), channel_id=1, source_target_pairs={{0,64},{64,0},{1,65},{65,1},{2,66},{66,2},{3,67},{67,3},{4,68},{68... | collective-permute-start | bytes 4718600 | tf_op jit(solution)/shard_map/ppermute | solution.py:25
  257.5 20.5 %collective-permute-start.19 = (bf16[512,768]{1,0:T(8,128)(2,1)S(1)}, bf16[512,768]{1,0:T(8,128)(2,1)S(1)}, u32[]{:S(2)}, u32[]{:S(2)}) collective-permute-start(bf16[512,768]{1,0:T(8,128)(2,1)S(1)} %add_convert_fusion.1), channel_id=1, source_target_pairs={{0,1},{1,0},{2,3},{3,2},{4,5},{5,4},{6,7},{7,6},{8,9},{9,8},{10,11... | collective-permute-start | bytes 2359304 | tf_op jit(solution)/shard_map/ppermute | solution.py:25
  (4 other events, 9.0 us)

commit v9 on v6

--- a/solution.py
+++ b/solution.py
@@ -128,17 +128,18 @@
     )
     half_rows = normed.shape[0]
     partner_normed = swap(normed, "tp")
-    flat_w = w_qkv.reshape(width, 3 * half_heads)
-    qkv_own = jnp.dot(normed, flat_w, preferred_element_type=jnp.float32).astype(jnp.bfloat16)
-    pair_own = qkv_own[:, half_heads:]
-
+    kv_w = w_qkv[:, 1:, :].reshape(width, 2 * half_heads)
+    q_w = w_qkv[:, 0, :]
+    pair_own = jnp.dot(normed, kv_w, preferred_element_type=jnp.float32).astype(jnp.bfloat16)
+
+    pair_own, partner_normed = lax.optimization_barrier((pair_own, partner_normed))
     near_own = {sign: from_behind(pair_own, "orbit", -sign) for sign in (1, -1)}
 
-    qkv_other = jnp.dot(partner_normed, flat_w, preferred_element_type=jnp.float32).astype(
+    pair_other = jnp.dot(partner_normed, kv_w, preferred_element_type=jnp.float32).astype(
         jnp.bfloat16
     )
-    pair_other = qkv_other[:, half_heads:]
-    queries = jnp.concatenate([qkv_own[:, :half_heads], qkv_other[:, :half_heads]], axis=0)
+    both_rows = jnp.concatenate([normed, partner_normed], axis=0)
+    queries = jnp.dot(both_rows, q_w, preferred_element_type=jnp.float32).astype(jnp.bfloat16)
 
     tp_index = lax.axis_index("tp")
     flags = adjacency[0]

time: 238 us -> 251 us (1.055)
  waiting for transfers between devices: 84 us -> 94.9 us
  matrix products: 19.7 us -> 25.1 us
  local copies, waits for them, and re-layouts: 17 us -> 14.4 us
    ppermute x4, waiting for transfers between devices: 29 us -> 35.6 us  [swap(): return lax.ppermute(array, axis, [(0, 1), (1, 0)])]
    dot_general x2 -> x3, matrix products: 12.9 us -> 18.3 us  [the longest x1 6.72 us: per_device_body(): jnp.dot(normed, kv_w, preferred_element_type=jnp.float32)]
    ppermute x8, waiting for transfers between devices: 55 us -> 59.3 us  [from_behind(): lax.ppermute(array, axis, [(i, (i + by) % count) for i in range(count)])]
    unnamed x15, local copies, waits for them, and re-layouts: 10.3 us -> 6.74 us
  transfers between devices with their start and end apart: 12 -> 12, of which waited for: 6 -> 6; matrix products, arithmetic and copies ran while one was open for 13% -> 9% of each run, Pallas kernels for 24% -> 22%
where the time goes in v9:
time: 251 us; the launch traced here: 250 us
  waiting for transfers between devices  94.9 us (38%)
  Pallas kernels  74.3 us (30%)
  starting transfers between devices  33.1 us (13%)
  matrix products  25.1 us (10%)
  local copies, waits for them, and re-layouts  14.4 us (6%)
  other arithmetic  7.57 us (3%)
    pallas_call x6, Pallas kernels, attend_stage(): pl.pallas_call(kernel, out_shape=out_shape, grid=(heads,), in_specs=in_sp...  74.3 us
    ppermute x8, waiting for transfers between devices, from_behind(): lax.ppermute(array, axis, [(i, (i + by) % count) for i in range(count)])  59.3 us
    ppermute x4, waiting for transfers between devices, swap(): return lax.ppermute(array, axis, [(0, 1), (1, 0)])  35.6 us
    ppermute x8, starting transfers between devices, from_behind(): lax.ppermute(array, axis, [(i, (i + by) % count) for i in range(count)])  24.5 us
    ppermute x4, starting transfers between devices, swap(): return lax.ppermute(array, axis, [(0, 1), (1, 0)])  8.57 us
    unnamed x15, local copies, waits for them, and re-layouts  6.74 us
    dot_general x1, matrix products, per_device_body(): jnp.dot(normed, kv_w, preferred_element_type=jnp.float32)  6.72 us
    dot_general x1, matrix products, per_device_body(): jnp.dot(both_rows, q_w, preferred_element_type=jnp.float32)  6.39 us
  transfers between devices with their start and end apart: 12, of which 6 were waited for; matrix products, arithmetic and copies ran while one was open for 9% of the time, Pallas kernels for 22%

profile of v9, /device:TPU:1, one launch (start us, length us, event | category | flops | bytes accessed | tf_op | source)
XLA Modules:
  0.0 249.5 jit_solution(2170353876456507430)
XLA Ops:
  4.5 3.6 %collective-permute-start = (bf16[512,1536]{1,0:T(8,128)(2,1)}, bf16[512,1536]{1,0:T(8,128)(2,1)}, u32[]{:S(2)}, u32[]{:S(2)}) collective-permute-start(bf16[512,1536]{1,0:T(8,128)(2,1)} %fusion.5), channel_id=1, source_target_pairs={{0,1},{1,0},{2,3},{3,2},{4,5},{5,4},{6,7},{7,6},{8,9},{9,8},{10,11... | collective-permute-start | bytes 4718600 | tf_op jit(solution)/shard_map/ppermute | solution.py:25
  8.1 4.9 %slice.38 = bf16[1536,2,768]{2,0,1:T(8,128)(2,1)} slice(bf16[1536,3,768]{2,0,1:T(8,128)(2,1)} %param.7), slice={[0:1536], [1:3], [0:768]} | slice | bytes 9437184 | tf_op jit(solution)/shard_map/slice | solution.py:131
  12.9 6.7 %copy.7 = bf16[1536,2,768]{0,2,1:T(8,128)(2,1)} copy(bf16[1536,2,768]{2,0,1:T(8,128)(2,1)} %slice.38) | data formatting | bytes 9437184
  19.7 6.7 %convolution_convert_fusion.1.refs_1_.refs_2_ = bf16[512,1536]{1,0:T(8,128)(2,1)} fusion(bf16[1536,1536]{0,1:T(8,128)(2,1)} %bitcast.52, bf16[1,1,512,1536]{3,2,1,0:T(8,128)(2,1)} %param.5, f32[1536]{0:T(1024)S(1)} %get-tuple-element.50, f32[1536]{0:T(1024)S(1)} %get-tuple-element.49, f32[512]{0:T(512)S(1)} %add_rsqrt_fusion), kind=kOutput, calls=%fused_computation.16 | convolution fusion | flops 2420637696 | bytes 7878656 | tf_op jit(solution)/shard_map/dot_general | solution.py:133
  26.4 15.7 %collective-permute-done = bf16[512,1536]{1,0:T(8,128)(2,1)} collective-permute-done((bf16[512,1536]{1,0:T(8,128)(2,1)}, bf16[512,1536]{1,0:T(8,128)(2,1)}, u32[]{:S(2)}, u32[]{:S(2)}) %collective-permute-start) | collective-permute-done | bytes 1572896 | tf_op jit(solution)/shard_map/ppermute | solution.py:25
  42.1 6.4 %fusion.15.refs_0_.refs_1_ = bf16[1024,768]{1,0:T(8,128)(2,1)} fusion(bf16[1536,3,768]{2,0,1:T(8,128)(2,1)} %param.7, bf16[512,1536]{1,0:T(8,128)(2,1)} %collective-permute-done, bf16[512,1536]{1,0:T(8,128)(2,1)} %fusion.5), kind=kOutput, calls=%fused_computation.19 | convolution fusion | flops 2422996992 | bytes 7077888 | tf_op jit(solution)/shard_map/dot_general | solution.py:142
  48.5 5.2 %convolution_convert_fusion.refs_3_.refs_4_ = bf16[512,1536]{1,0:T(8,128)(2,1)} fusion(bf16[512,1536]{1,0:T(8,128)(2,1)} %collective-permute-done, bf16[1536,1536]{0,1:T(8,128)(2,1)S(1)} %bitcast.55), kind=kOutput, calls=%fused_computation.15 | convolution fusion | flops 2416705536 | bytes 7864320 | tf_op jit(solution)/shard_map/dot_general | solution.py:138
  55.3 5.9 %collective-permute-start.7 = (bf16[512,1536]{1,0:T(8,128)(2,1)}, bf16[512,1536]{1,0:T(8,128)(2,1)}, u32[]{:S(2)}, u32[]{:S(2)}) collective-permute-start(bf16[512,1536]{1,0:T(8,128)(2,1)} %convolution_convert_fusion.1.refs_1_.refs_2_), channel_id=1, source_target_pairs={{0,62},{2,0},{4,2},{6,4},{8,6},{10,8},{12,10},{14,12},{16,14},{18,... | collective-permute-start | bytes 4718600 | tf_op jit(solution)/shard_map/ppermute | solution.py:21
  61.2 13.3 %shard_map.55 = (f32[1024,768]{1,0:T(8,128)}, f32[1024,768]{1,0:T(8,128)}, f32[1024,768]{1,0:T(8,128)}) custom-call(bf16[1024,768]{1,0:T(8,128)(2,1)} %fusion.15.refs_0_.refs_1_, bf16[512,1536]{1,0:T(8,128)(2,1)} %convolution_convert_fusion.1.refs_1_.refs_2_, bf16[512,1536]{1,0:T(8,128)(2,1)} %convolution_convert_fusion.1.refs_1_.refs_2_, ...), custom_call_target="tpu_custom_call" | custom-call | tf_op jit(solution)/shard_map/pallas_call | solution.py:109
  74.5 5.7 %collective-permute-start.3 = (bf16[512,1536]{1,0:T(8,128)(2,1)}, bf16[512,1536]{1,0:T(8,128)(2,1)}, u32[]{:S(2)}, u32[]{:S(2)}) collective-permute-start(bf16[512,1536]{1,0:T(8,128)(2,1)} %convolution_convert_fusion.refs_3_.refs_4_), channel_id=1, source_target_pairs={{0,62},{2,0},{4,2},{6,4},{8,6},{10,8},{12,10},{14,12},{16,14},{18,... | collective-permute-start | bytes 4718600 | tf_op jit(solution)/shard_map/ppermute | solution.py:21
  80.2 14.5 %collective-permute-done.5.refs_2_.refs_3_ = bf16[512,1536]{1,0:T(8,128)(2,1)} collective-permute-done((bf16[512,1536]{1,0:T(8,128)(2,1)}, bf16[512,1536]{1,0:T(8,128)(2,1)}, u32[]{:S(2)}, u32[]{:S(2)}) %collective-permute-start.5) | collective-permute-done | bytes 1572896 | tf_op jit(solution)/shard_map/ppermute | solution.py:21
  94.8 5.7 %collective-permute-start.8 = (bf16[512,1536]{1,0:T(8,128)(2,1)}, bf16[512,1536]{1,0:T(8,128)(2,1)}, u32[]{:S(2)}, u32[]{:S(2)}) collective-permute-start(bf16[512,1536]{1,0:T(8,128)(2,1)} %collective-permute-done.7.refs_4_.refs_5_), channel_id=1, source_target_pairs={{0,62},{2,0},{4,2},{6,4},{8,6},{10,8},{12,10},{14,12},{16,14},{18,... | collective-permute-start | bytes 4718600 | tf_op jit(solution)/shard_map/ppermute | solution.py:21
  100.4 28.0 %collective-permute-done.1.refs_2_.refs_3_ = bf16[512,1536]{1,0:T(8,128)(2,1)} collective-permute-done((bf16[512,1536]{1,0:T(8,128)(2,1)}, bf16[512,1536]{1,0:T(8,128)(2,1)}, u32[]{:S(2)}, u32[]{:S(2)}) %collective-permute-start.1) | collective-permute-done | bytes 1572896 | tf_op jit(solution)/shard_map/ppermute | solution.py:21
  128.5 5.7 %collective-permute-start.4 = (bf16[512,1536]{1,0:T(8,128)(2,1)}, bf16[512,1536]{1,0:T(8,128)(2,1)}, u32[]{:S(2)}, u32[]{:S(2)}) collective-permute-start(bf16[512,1536]{1,0:T(8,128)(2,1)} %collective-permute-done.3.refs_4_.refs_5_), channel_id=1, source_target_pairs={{0,62},{2,0},{4,2},{6,4},{8,6},{10,8},{12,10},{14,12},{16,14},{18,... | collective-permute-start | bytes 4718600 | tf_op jit(solution)/shard_map/ppermute | solution.py:21
  135.3 14.2 %shard_map.56 = (f32[1024,768]{1,0:T(8,128)}, f32[1024,768]{1,0:T(8,128)}, f32[1024,768]{1,0:T(8,128)}) custom-call(f32[1,1024]{1,0:T(1,128)} %bitcast.59, bf16[1024,768]{1,0:T(8,128)(2,1)} %fusion.15.refs_0_.refs_1_, bf16[512,1536]{1,0:T(8,128)(2,1)} %collective-permute-done.5.refs_2_.refs_3_, bf16[512,1536]{1,0:T(8,128)(2,1)} %collective-permute-done.5.refs_2_.refs_3_, ...), custom_call_target="tpu_custom_call" | custom-call | tf_op jit(solution)/shard_map/pallas_call | solution.py:109
  150.1 14.2 %shard_map.57 = (f32[1024,768]{1,0:T(8,128)}, f32[1024,768]{1,0:T(8,128)}, f32[1024,768]{1,0:T(8,128)}) custom-call(f32[1,1024]{1,0:T(1,128)} %bitcast.60, bf16[1024,768]{1,0:T(8,128)(2,1)} %fusion.15.refs_0_.refs_1_, bf16[512,1536]{1,0:T(8,128)(2,1)} %collective-permute-done.1.refs_2_.refs_3_, bf16[512,1536]{1,0:T(8,128)(2,1)} %collective-permute-done.1.refs_2_.refs_3_, ...), custom_call_target="tpu_custom_call" | custom-call | tf_op jit(solution)/shard_map/pallas_call | solution.py:109
  165.0 14.1 %shard_map.58 = (f32[1024,768]{1,0:T(8,128)}, f32[1024,768]{1,0:T(8,128)}, f32[1024,768]{1,0:T(8,128)}) custom-call(f32[1,1024]{1,0:T(1,128)} %bitcast.58, bf16[1024,768]{1,0:T(8,128)(2,1)} %fusion.15.refs_0_.refs_1_, bf16[512,1536]{1,0:T(8,128)(2,1)} %collective-permute-done.6.refs_2_.refs_3_, bf16[512,1536]{1,0:T(8,128)(2,1)} %collective-permute-done.6.refs_2_.refs_3_, ...), custom_call_target="tpu_custom_call" | custom-call | tf_op jit(solution)/shard_map/pallas_call | solution.py:109
  179.1 16.8 %collective-permute-done.2.refs_2_.refs_3_ = bf16[512,1536]{1,0:T(8,128)(2,1)} collective-permute-done((bf16[512,1536]{1,0:T(8,128)(2,1)}, bf16[512,1536]{1,0:T(8,128)(2,1)}, u32[]{:S(2)}, u32[]{:S(2)}) %collective-permute-start.2) | collective-permute-done | bytes 1572896 | tf_op jit(solution)/shard_map/ppermute | solution.py:21
  196.5 9.3 %shard_map.59 = bf16[512,768]{1,0:T(8,128)(2,1)} custom-call(f32[1,1024]{1,0:T(1,128)} %bitcast.56, bf16[1024,768]{1,0:T(8,128)(2,1)} %fusion.15.refs_0_.refs_1_, bf16[512,1536]{1,0:T(8,128)(2,1)} %collective-permute-done.2.refs_2_.refs_3_, bf16[512,1536]{1,0:T(8,128)(2,1)} %collective-permute-done.2.refs_2_.refs_3_, ...), custom_call_target="tpu_custom_call" | custom-call | tf_op jit(solution)/shard_map/pallas_call | solution.py:109
  205.8 3.2 %convolution_multiply_fusion.1 = f32[512,768]{1,0:T(8,128)} fusion(bf16[512,768]{1,0:T(8,128)(2,1)} %shard_map.59, bf16[768,1536]{1,0:T(8,128)(2,1)S(1)} %copy-done, s32[]{:T(128)S(6)} %select_n.91, f32[]{:T(128)S(6)} %select_n.79), kind=kOutput, calls=%fused_computation.27 | convolution fusion | flops 604372992 | bytes 3538952 | tf_op jit(solution)/shard_map/dot_general | solution.py:191
  211.9 2.6 %collective-permute-done.9 = f32[512,768]{1,0:T(8,128)} collective-permute-done((f32[512,768]{1,0:T(8,128)}, f32[512,768]{1,0:T(8,128)}, u32[]{:S(2)}, u32[]{:S(2)}) %collective-permute-start.9) | collective-permute-done | bytes 1572896 | tf_op jit(solution)/shard_map/ppermute | solution.py:25
  216.1 9.3 %shard_map.60 = bf16[512,768]{1,0:T(8,128)(2,1)} custom-call(f32[1,1024]{1,0:T(1,128)} %bitcast.57, bf16[1024,768]{1,0:T(8,128)(2,1)} %fusion.15.refs_0_.refs_1_, bf16[512,1536]{1,0:T(8,128)(2,1)} %collective-permute-done.2.refs_2_.refs_3_, bf16[512,1536]{1,0:T(8,128)(2,1)} %collective-permute-done.2.refs_2_.refs_3_, ...), custom_call_target="tpu_custom_call" | custom-call | tf_op jit(solution)/shard_map/pallas_call | solution.py:109
  227.9 2.4 collective-permute-start.11
  231.1 17.3 %collective-permute-done.11 = bf16[512,768]{1,0:T(8,128)(2,1)S(1)} collective-permute-done((bf16[512,768]{1,0:T(8,128)(2,1)S(1)}, bf16[512,768]{1,0:T(8,128)(2,1)S(1)}, u32[]{:S(2)}, u32[]{:S(2)}) %collective-permute-start.11) | collective-permute-done | bytes 786464 | tf_op jit(solution)/shard_map/ppermute | solution.py:25
  (47 shorter events, 18.2 us)
Async XLA Ops:
  0.0 205.8 %copy-start = (bf16[768,1536]{1,0:T(8,128)(2,1)S(1)}, bf16[768,1536]{1,0:T(8,128)(2,1)}, u32[]{:S(2)}) copy-start(bf16[768,1536]{1,0:T(8,128)(2,1)} %param.8) | copy-start | bytes 7077892
  0.0 2.8 %copy-start.1 = (bf16[1,1,512,1536]{3,2,1,0:T(8,128)(2,1)S(1)}, bf16[1,1,512,1536]{3,2,1,0:T(8,128)(2,1)}, u32[]{:S(2)}) copy-start(bf16[1,1,512,1536]{3,2,1,0:T(8,128)(2,1)} %param.5) | copy-start | bytes 4718596
  4.5 37.6 %collective-permute-start = (bf16[512,1536]{1,0:T(8,128)(2,1)}, bf16[512,1536]{1,0:T(8,128)(2,1)}, u32[]{:S(2)}, u32[]{:S(2)}) collective-permute-start(bf16[512,1536]{1,0:T(8,128)(2,1)} %fusion.5), channel_id=1, source_target_pairs={{0,1},{1,0},{2,3},{3,2},{4,5},{5,4},{6,7},{7,6},{8,9},{9,8},{10,11... | collective-permute-start | bytes 4718600 | tf_op jit(solution)/shard_map/ppermute | solution.py:25
  19.7 28.8 %slice-start = ((s8[4718592]{0:T(1024)(128)(4,1)}), s8[524288]{0:T(1024)(128)(4,1)S(1)}, s32[]{:S(2)}) async-start(s8[4718592]{0:T(1024)(128)(4,1)} %bitcast.53), calls=%async_computation | async-start | bytes 1048576
  26.4 22.1 %slice-start.1 = ((s8[4718592]{0:T(1024)(128)(4,1)}), s8[4194304]{0:T(1024)(128)(4,1)S(1)}, s32[]{:S(2)}) async-start(s8[4718592]{0:T(1024)(128)(4,1)} %bitcast.53), calls=%async_computation.1 | async-start | bytes 8388608
  53.7 80.4 %copy-start.4 = (s32[1,4,8]{2,1,0:T(4,128)S(1)}, s32[1,4,8]{2,1,0:T(4,128)}, u32[]{:S(2)}) copy-start(s32[1,4,8]{2,1,0:T(4,128)} %param.9) | copy-start | bytes 388
  53.7 41.0 %collective-permute-start.5 = (bf16[512,1536]{1,0:T(8,128)(2,1)}, bf16[512,1536]{1,0:T(8,128)(2,1)}, u32[]{:S(2)}, u32[]{:S(2)}) collective-permute-start(bf16[512,1536]{1,0:T(8,128)(2,1)} %convolution_convert_fusion.1.refs_1_.refs_2_), channel_id=1, source_target_pairs={{0,2},{2,4},{4,6},{6,8},{8,10},{10,12},{12,14},{14,16},{16,18},{18... | collective-permute-start | bytes 4718600 | tf_op jit(solution)/shard_map/ppermute | solution.py:21
  55.3 39.4 %collective-permute-start.7 = (bf16[512,1536]{1,0:T(8,128)(2,1)}, bf16[512,1536]{1,0:T(8,128)(2,1)}, u32[]{:S(2)}, u32[]{:S(2)}) collective-permute-start(bf16[512,1536]{1,0:T(8,128)(2,1)} %convolution_convert_fusion.1.refs_1_.refs_2_), channel_id=1, source_target_pairs={{0,62},{2,0},{4,2},{6,4},{8,6},{10,8},{12,10},{14,12},{16,14},{18,... | collective-permute-start | bytes 4718600 | tf_op jit(solution)/shard_map/ppermute | solution.py:21
  74.5 53.9 %collective-permute-start.1 = (bf16[512,1536]{1,0:T(8,128)(2,1)}, bf16[512,1536]{1,0:T(8,128)(2,1)}, u32[]{:S(2)}, u32[]{:S(2)}) collective-permute-start(bf16[512,1536]{1,0:T(8,128)(2,1)} %convolution_convert_fusion.refs_3_.refs_4_), channel_id=1, source_target_pairs={{0,2},{2,4},{4,6},{6,8},{8,10},{10,12},{12,14},{14,16},{16,18},{18... | collective-permute-start | bytes 4718600 | tf_op jit(solution)/shard_map/ppermute | solution.py:21
  74.5 53.9 %collective-permute-start.3 = (bf16[512,1536]{1,0:T(8,128)(2,1)}, bf16[512,1536]{1,0:T(8,128)(2,1)}, u32[]{:S(2)}, u32[]{:S(2)}) collective-permute-start(bf16[512,1536]{1,0:T(8,128)(2,1)} %convolution_convert_fusion.refs_3_.refs_4_), channel_id=1, source_target_pairs={{0,62},{2,0},{4,2},{6,4},{8,6},{10,8},{12,10},{14,12},{16,14},{18,... | collective-permute-start | bytes 4718600 | tf_op jit(solution)/shard_map/ppermute | solution.py:21
  94.8 69.5 %collective-permute-start.6 = (bf16[512,1536]{1,0:T(8,128)(2,1)}, bf16[512,1536]{1,0:T(8,128)(2,1)}, u32[]{:S(2)}, u32[]{:S(2)}) collective-permute-start(bf16[512,1536]{1,0:T(8,128)(2,1)} %collective-permute-done.5.refs_2_.refs_3_), channel_id=1, source_target_pairs={{0,2},{2,4},{4,6},{6,8},{8,10},{10,12},{12,14},{14,16},{16,18},{18... | collective-permute-start | bytes 4718600 | tf_op jit(solution)/shard_map/ppermute | solution.py:21
  94.8 69.5 %collective-permute-start.8 = (bf16[512,1536]{1,0:T(8,128)(2,1)}, bf16[512,1536]{1,0:T(8,128)(2,1)}, u32[]{:S(2)}, u32[]{:S(2)}) collective-permute-start(bf16[512,1536]{1,0:T(8,128)(2,1)} %collective-permute-done.7.refs_4_.refs_5_), channel_id=1, source_target_pairs={{0,62},{2,0},{4,2},{6,4},{8,6},{10,8},{12,10},{14,12},{16,14},{18,... | collective-permute-start | bytes 4718600 | tf_op jit(solution)/shard_map/ppermute | solution.py:21
  128.5 67.4 %collective-permute-start.2 = (bf16[512,1536]{1,0:T(8,128)(2,1)}, bf16[512,1536]{1,0:T(8,128)(2,1)}, u32[]{:S(2)}, u32[]{:S(2)}) collective-permute-start(bf16[512,1536]{1,0:T(8,128)(2,1)} %collective-permute-done.1.refs_2_.refs_3_), channel_id=1, source_target_pairs={{0,2},{2,4},{4,6},{6,8},{8,10},{10,12},{12,14},{14,16},{16,18},{18... | collective-permute-start | bytes 4718600 | tf_op jit(solution)/shard_map/ppermute | solution.py:21
  128.5 67.4 %collective-permute-start.4 = (bf16[512,1536]{1,0:T(8,128)(2,1)}, bf16[512,1536]{1,0:T(8,128)(2,1)}, u32[]{:S(2)}, u32[]{:S(2)}) collective-permute-start(bf16[512,1536]{1,0:T(8,128)(2,1)} %collective-permute-done.3.refs_4_.refs_5_), channel_id=1, source_target_pairs={{0,62},{2,0},{4,2},{6,4},{8,6},{10,8},{12,10},{14,12},{16,14},{18,... | collective-permute-start | bytes 4718600 | tf_op jit(solution)/shard_map/ppermute | solution.py:21
  205.8 5.3 %copy-start.3 = (bf16[512,768]{1,0:T(8,128)(2,1)S(1)}, bf16[512,768]{1,0:T(8,128)(2,1)}, u32[]{:S(2)}) copy-start(bf16[512,768]{1,0:T(8,128)(2,1)} %shard_map.59) | copy-start | bytes 2359300
  209.0 5.5 %collective-permute-start.9 = (f32[512,768]{1,0:T(8,128)}, f32[512,768]{1,0:T(8,128)}, u32[]{:S(2)}, u32[]{:S(2)}) collective-permute-start(f32[512,768]{1,0:T(8,128)} %convolution_multiply_fusion.1), channel_id=1, source_target_pairs={{0,64},{64,0},{1,65},{65,1},{2,66},{66,2},{3,67},{67,3},{4,68},{68... | collective-permute-start | bytes 4718600 | tf_op jit(solution)/shard_map/ppermute | solution.py:25
  225.4 4.9 %copy-start.2 = (bf16[512,768]{1,0:T(8,128)(2,1)S(1)}, bf16[512,768]{1,0:T(8,128)(2,1)}, u32[]{:S(2)}) copy-start(bf16[512,768]{1,0:T(8,128)(2,1)} %shard_map.60) | copy-start | bytes 2359300
  227.4 20.9 %collective-permute-start.10 = (f32[512,768]{1,0:T(8,128)S(1)}, f32[512,768]{1,0:T(8,128)S(1)}, u32[]{:S(2)}, u32[]{:S(2)}) collective-permute-start(f32[512,768]{1,0:T(8,128)S(1)} %convolution_multiply_fusion), channel_id=1, source_target_pairs={{0,64},{64,0},{1,65},{65,1},{2,66},{66,2},{3,67},{67,3},{4,68},{68... | collective-permute-start | bytes 4718600 | tf_op jit(solution)/shard_map/ppermute | solution.py:25
  227.9 20.5 %collective-permute-start.11 = (bf16[512,768]{1,0:T(8,128)(2,1)S(1)}, bf16[512,768]{1,0:T(8,128)(2,1)S(1)}, u32[]{:S(2)}, u32[]{:S(2)}) collective-permute-start(bf16[512,768]{1,0:T(8,128)(2,1)S(1)} %add_convert_fusion.1), channel_id=1, source_target_pairs={{0,1},{1,0},{2,3},{3,2},{4,5},{5,4},{6,7},{7,6},{8,9},{9,8},{10,11... | collective-permute-start | bytes 2359304 | tf_op jit(solution)/shard_map/ppermute | solution.py:25

commit v10 on v9

--- a/solution.py
+++ b/solution.py
@@ -132,7 +132,6 @@
     q_w = w_qkv[:, 0, :]
     pair_own = jnp.dot(normed, kv_w, preferred_element_type=jnp.float32).astype(jnp.bfloat16)
 
-    pair_own, partner_normed = lax.optimization_barrier((pair_own, partner_normed))
     near_own = {sign: from_behind(pair_own, "orbit", -sign) for sign in (1, -1)}
 
     pair_other = jnp.dot(partner_normed, kv_w, preferred_element_type=jnp.float32).astype(
@@ -148,11 +147,11 @@
     own_start = tp_index * per_chunk
     other_start = (1 - tp_index) * per_chunk
 
-    def chunk_bias(offsets, start):
+    def chunk_bias(offsets, start, count):
         rows_of = []
         for offset in offsets:
             row = flags[offset + REACH if offset < 0 else offset + REACH - 1]
-            rows_of.append(lax.dynamic_slice_in_dim(row, start, per_chunk))
+            rows_of.append(lax.dynamic_slice_in_dim(row, start, count))
         allowed = jnp.repeat(jnp.concatenate(rows_of), BLOCK) > 0
         return jnp.where(allowed, 0.0, -1e30).astype(jnp.float32)[None, :]
 
@@ -160,27 +159,45 @@
         queries, [pair_own, pair_other], None, None, first=True, last=False, heads=heads
     )
     pair_other, carry = lax.optimization_barrier((pair_other, carry))
-    near_other = {sign: from_behind(pair_other, "orbit", -sign) for sign in (1, -1)}
+    piece_rows = half_rows // 2
+    piece_blocks = per_chunk // 2
+    other_pieces = [pair_other[:piece_rows], pair_other[piece_rows:]]
+    near_other = {
+        sign: [from_behind(piece, "orbit", -sign) for piece in other_pieces] for sign in (1, -1)
+    }
     far_own = {sign: from_behind(near_own[sign], "orbit", -sign) for sign in (1, -1)}
     carry = attend_stage(
-        queries, [near_own[-1], near_own[1]], chunk_bias((-1, 1), own_start), carry,
+        queries, [near_own[-1], near_own[1]], chunk_bias((-1, 1), own_start, per_chunk), carry,
         first=False, last=False, heads=heads,
     )
-    far_other = {sign: from_behind(near_other[sign], "orbit", -sign) for sign in (1, -1)}
-    carry = attend_stage(
-        queries, [near_other[-1], near_other[1]], chunk_bias((-1, 1), other_start), carry,
+    far_other = {
+        sign: [from_behind(piece, "orbit", -sign) for piece in near_other[sign]] for sign in (1, -1)
+    }
+    near_bias = jnp.concatenate(
+        [chunk_bias((-1, 1), other_start + k * piece_blocks, piece_blocks) for k in range(2)],
+        axis=1,
+    )
+    carry = attend_stage(
+        queries,
+        [near_other[-1][0], near_other[1][0], near_other[-1][1], near_other[1][1]],
+        near_bias, carry, first=False, last=False, heads=heads,
+    )
+    carry = attend_stage(
+        queries, [far_own[-1], far_own[1]], chunk_bias((-2, 2), own_start, per_chunk), carry,
         first=False, last=False, heads=heads,
     )
     carry = attend_stage(
-        queries, [far_own[-1], far_own[1]], chunk_bias((-2, 2), own_start), carry,
+        queries, [far_other[-1][0], far_other[1][0]],
+        chunk_bias((-2, 2), other_start, piece_blocks), carry,
         first=False, last=False, heads=heads,
     )
-    last_chunks = [far_other[-1], far_other[1]]
-    last_bias = chunk_bias((-2, 2), other_start)
+    last_chunks = [far_other[-1][1], far_other[1][1]]
+    last_bias = chunk_bias((-2, 2), other_start + piece_blocks, piece_blocks)
     context_other = attend_stage(
         queries, last_chunks, last_bias, carry,
         first=False, last=True, heads=heads, row_block=1, rows=half_rows,
     )
+
     owner = lax.axis_index("cfg")
     half_width = width // 2
     weight_now = jnp.where(owner == 0, guide_scale, 1.0 - guide_scale).astype(jnp.float32)

time: 251 us -> 272 us (1.084)
  Pallas kernels: 74.3 us -> 84.4 us
  starting transfers between devices: 33.1 us -> 39 us
    pallas_call x6 -> x7, Pallas kernels: 74.3 us -> 84.4 us  [attend_stage(): pl.pallas_call(kernel, out_shape=out_shape, grid=(heads,), in_specs=in_sp...]
    ppermute x8 -> x12, waiting for transfers between devices: 59.3 us -> 66.9 us  [from_behind(): lax.ppermute(array, axis, [(i, (i + by) % count) for i in range(count)])]
    ppermute x8 -> x12, starting transfers between devices: 24.5 us -> 30.6 us  [from_behind(): lax.ppermute(array, axis, [(i, (i + by) % count) for i in range(count)])]
    ppermute x4, waiting for transfers between devices: 35.6 us -> 30 us  [swap(): return lax.ppermute(array, axis, [(0, 1), (1, 0)])]
  transfers between devices with their start and end apart: 12 -> 16, of which waited for: 6 -> 6; matrix products, arithmetic and copies ran while one was open for 9% -> 14% of each run, Pallas kernels for 22% -> 26%
where the time goes in v10:
time: 272 us; the launch traced here: 271 us
  waiting for transfers between devices  96.9 us (36%)
  Pallas kernels  84.4 us (31%)
  starting transfers between devices  39 us (14%)
  matrix products  25.1 us (9%)
  local copies, waits for them, and re-layouts  17.1 us (6%)
  other arithmetic  8.33 us (3%)
    pallas_call x7, Pallas kernels, attend_stage(): pl.pallas_call(kernel, out_shape=out_shape, grid=(heads,), in_specs=in_sp...  84.4 us
    ppermute x12, waiting for transfers between devices, from_behind(): lax.ppermute(array, axis, [(i, (i + by) % count) for i in range(count)])  66.9 us
    ppermute x12, starting transfers between devices, from_behind(): lax.ppermute(array, axis, [(i, (i + by) % count) for i in range(count)])  30.6 us
    ppermute x4, waiting for transfers between devices, swap(): return lax.ppermute(array, axis, [(0, 1), (1, 0)])  30 us
    ppermute x4, starting transfers between devices, swap(): return lax.ppermute(array, axis, [(0, 1), (1, 0)])  8.41 us
    dot_general x1, matrix products, per_device_body(): jnp.dot(normed, kv_w, preferred_element_type=jnp.float32)  6.86 us
    unnamed x15, local copies, waits for them, and re-layouts  6.78 us
    dot_general x1, matrix products, per_device_body(): jnp.dot(both_rows, q_w, preferred_element_type=jnp.float32)  6.36 us
  transfers between devices with their start and end apart: 16, of which 6 were waited for; matrix products, arithmetic and copies ran while one was open for 14% of the time, Pallas kernels for 26%

profile of v10, /device:TPU:1, one launch (start us, length us, event | category | flops | bytes accessed | tf_op | source)
XLA Modules:
  0.0 271.0 jit_solution(14933773105819998934)
XLA Ops:
  4.5 3.6 %collective-permute-start = (bf16[512,1536]{1,0:T(8,128)(2,1)}, bf16[512,1536]{1,0:T(8,128)(2,1)}, u32[]{:S(2)}, u32[]{:S(2)}) collective-permute-start(bf16[512,1536]{1,0:T(8,128)(2,1)} %fusion.5), channel_id=1, source_target_pairs={{0,1},{1,0},{2,3},{3,2},{4,5},{5,4},{6,7},{7,6},{8,9},{9,8},{10,11... | collective-permute-start | bytes 4718600 | tf_op jit(solution)/shard_map/ppermute | solution.py:25
  8.1 4.8 %slice.49 = bf16[1536,2,768]{2,0,1:T(8,128)(2,1)} slice(bf16[1536,3,768]{2,0,1:T(8,128)(2,1)} %param.7), slice={[0:1536], [1:3], [0:768]} | slice | bytes 9437184 | tf_op jit(solution)/shard_map/slice | solution.py:131
  12.9 6.6 %copy.7 = bf16[1536,2,768]{0,2,1:T(8,128)(2,1)} copy(bf16[1536,2,768]{2,0,1:T(8,128)(2,1)} %slice.49) | data formatting | bytes 9437184
  19.5 6.9 %convolution_convert_fusion.refs_1_.refs_2_ = bf16[512,1536]{1,0:T(8,128)(2,1)} fusion(bf16[1536,1536]{0,1:T(8,128)(2,1)} %bitcast.62, bf16[1,1,512,1536]{3,2,1,0:T(8,128)(2,1)} %param.5, f32[1536]{0:T(1024)S(1)} %get-tuple-element.52, f32[1536]{0:T(1024)S(1)} %get-tuple-element.51, f32[512]{0:T(512)S(1)} %add_rsqrt_fusion), kind=kOutput, calls=%fused_computation.15 | convolution fusion | flops 2420637696 | bytes 7878656 | tf_op jit(solution)/shard_map/dot_general | solution.py:133
  26.4 6.2 %collective-permute-start.11 = (bf16[512,1536]{1,0:T(8,128)(2,1)}, bf16[512,1536]{1,0:T(8,128)(2,1)}, u32[]{:S(2)}, u32[]{:S(2)}) collective-permute-start(bf16[512,1536]{1,0:T(8,128)(2,1)} %convolution_convert_fusion.refs_1_.refs_2_), channel_id=1, source_target_pairs={{0,62},{2,0},{4,2},{6,4},{8,6},{10,8},{12,10},{14,12},{16,14},{18,... | collective-permute-start | bytes 4718600 | tf_op jit(solution)/shard_map/ppermute | solution.py:21
  32.6 9.5 %collective-permute-done = bf16[512,1536]{1,0:T(8,128)(2,1)} collective-permute-done((bf16[512,1536]{1,0:T(8,128)(2,1)}, bf16[512,1536]{1,0:T(8,128)(2,1)}, u32[]{:S(2)}, u32[]{:S(2)}) %collective-permute-start) | collective-permute-done | bytes 1572896 | tf_op jit(solution)/shard_map/ppermute | solution.py:25
  42.1 5.2 %convolution_convert_fusion.1.refs_3_.refs_4_ = bf16[512,1536]{1,0:T(8,128)(2,1)} fusion(bf16[512,1536]{1,0:T(8,128)(2,1)} %collective-permute-done, bf16[1536,1536]{0,1:T(8,128)(2,1)S(1)} %bitcast.63), kind=kOutput, calls=%fused_computation.16 | convolution fusion | flops 2416705536 | bytes 7864320 | tf_op jit(solution)/shard_map/dot_general | solution.py:137
  47.3 6.4 %fusion.15.refs_0_.refs_1_ = bf16[1024,768]{1,0:T(8,128)(2,1)} fusion(bf16[1536,3,768]{2,0,1:T(8,128)(2,1)} %param.7, bf16[512,1536]{1,0:T(8,128)(2,1)} %collective-permute-done, bf16[512,1536]{1,0:T(8,128)(2,1)} %fusion.5), kind=kOutput, calls=%fused_computation.19 | convolution fusion | flops 2422996992 | bytes 7077888 | tf_op jit(solution)/shard_map/dot_general | solution.py:141
  53.6 13.4 %shard_map.55 = (f32[1024,768]{1,0:T(8,128)}, f32[1024,768]{1,0:T(8,128)}, f32[1024,768]{1,0:T(8,128)}) custom-call(bf16[1024,768]{1,0:T(8,128)(2,1)} %fusion.15.refs_0_.refs_1_, bf16[512,1536]{1,0:T(8,128)(2,1)} %convolution_convert_fusion.refs_1_.refs_2_, bf16[512,1536]{1,0:T(8,128)(2,1)} %convolution_convert_fusion.refs_1_.refs_2_, ...), custom_call_target="tpu_custom_call" | custom-call | tf_op jit(solution)/shard_map/pallas_call | solution.py:109
  71.0 11.2 %collective-permute-done.9.refs_2_.refs_3_ = bf16[512,1536]{1,0:T(8,128)(2,1)} collective-permute-done((bf16[512,1536]{1,0:T(8,128)(2,1)}, bf16[512,1536]{1,0:T(8,128)(2,1)}, u32[]{:S(2)}, u32[]{:S(2)}) %collective-permute-start.9) | collective-permute-done | bytes 1572896 | tf_op jit(solution)/shard_map/ppermute | solution.py:21
  82.1 5.7 %collective-permute-start.12 = (bf16[512,1536]{1,0:T(8,128)(2,1)}, bf16[512,1536]{1,0:T(8,128)(2,1)}, u32[]{:S(2)}, u32[]{:S(2)}) collective-permute-start(bf16[512,1536]{1,0:T(8,128)(2,1)} %collective-permute-done.11.refs_4_.refs_5_), channel_id=1, source_target_pairs={{0,62},{2,0},{4,2},{6,4},{8,6},{10,8},{12,10},{14,12},{16,14},{18,... | collective-permute-start | bytes 4718600 | tf_op jit(solution)/shard_map/ppermute | solution.py:21
  87.8 5.7 %collective-permute-start.7 = (bf16[256,1536]{1,0:T(8,128)(2,1)}, bf16[256,1536]{1,0:T(8,128)(2,1)}, u32[]{:S(2)}, u32[]{:S(2)}) collective-permute-start(bf16[256,1536]{1,0:T(8,128)(2,1)} %get-tuple-element.53), channel_id=1, source_target_pairs={{0,62},{2,0},{4,2},{6,4},{8,6},{10,8},{12,10},{14,12},{16,14},{18,... | collective-permute-start | bytes 2359304 | tf_op jit(solution)/shard_map/ppermute | solution.py:21
  93.5 5.5 %collective-permute-done.1.refs_6_.refs_7_ = bf16[256,1536]{1,0:T(8,128)(2,1)} collective-permute-done((bf16[256,1536]{1,0:T(8,128)(2,1)S(1)}, bf16[256,1536]{1,0:T(8,128)(2,1)}, u32[]{:S(2)}, u32[]{:S(2)}) %collective-permute-start.1) | collective-permute-done | bytes 786464 | tf_op jit(solution)/shard_map/ppermute | solution.py:21
  99.3 50.2 %collective-permute-done.5.refs_2_.refs_3_ = bf16[256,1536]{1,0:T(8,128)(2,1)} collective-permute-done((bf16[256,1536]{1,0:T(8,128)(2,1)}, bf16[256,1536]{1,0:T(8,128)(2,1)}, u32[]{:S(2)}, u32[]{:S(2)}) %collective-permute-start.5) | collective-permute-done | bytes 786464 | tf_op jit(solution)/shard_map/ppermute | solution.py:21
  149.6 5.7 %collective-permute-start.8 = (bf16[256,1536]{1,0:T(8,128)(2,1)}, bf16[256,1536]{1,0:T(8,128)(2,1)}, u32[]{:S(2)}, u32[]{:S(2)}) collective-permute-start(bf16[256,1536]{1,0:T(8,128)(2,1)} %collective-permute-done.7.refs_4_.refs_5_), channel_id=1, source_target_pairs={{0,62},{2,0},{4,2},{6,4},{8,6},{10,8},{12,10},{14,12},{16,14},{18,... | collective-permute-start | bytes 2359304 | tf_op jit(solution)/shard_map/ppermute | solution.py:21
  155.3 5.7 %collective-permute-start.4 = (bf16[256,1536]{1,0:T(8,128)(2,1)}, bf16[256,1536]{1,0:T(8,128)(2,1)}, u32[]{:S(2)}, u32[]{:S(2)}) collective-permute-start(bf16[256,1536]{1,0:T(8,128)(2,1)} %collective-permute-done.3.refs_8_.refs_9_), channel_id=1, source_target_pairs={{0,62},{2,0},{4,2},{6,4},{8,6},{10,8},{12,10},{14,12},{16,14},{18,... | collective-permute-start | bytes 2359304 | tf_op jit(solution)/shard_map/ppermute | solution.py:21
  162.8 14.1 %shard_map.56 = (f32[1024,768]{1,0:T(8,128)}, f32[1024,768]{1,0:T(8,128)}, f32[1024,768]{1,0:T(8,128)}) custom-call(f32[1,1024]{1,0:T(1,128)} %bitcast.67, bf16[1024,768]{1,0:T(8,128)(2,1)} %fusion.15.refs_0_.refs_1_, bf16[512,1536]{1,0:T(8,128)(2,1)} %collective-permute-done.9.refs_2_.refs_3_, bf16[512,1536]{1,0:T(8,128)(2,1)} %collective-permute-done.9.refs_2_.refs_3_, ...), custom_call_target="tpu_custom_call" | custom-call | tf_op jit(solution)/shard_map/pallas_call | solution.py:109
  176.9 16.0 %shard_map.57 = (f32[1024,768]{1,0:T(8,128)}, f32[1024,768]{1,0:T(8,128)}, f32[1024,768]{1,0:T(8,128)}) custom-call(f32[1,1024]{1,0:T(1,128)} %pad_maximum_fusion.refs_0_, bf16[1024,768]{1,0:T(8,128)(2,1)} %fusion.15.refs_0_.refs_1_, bf16[256,1536]{1,0:T(8,128)(2,1)} %collective-permute-done.5.refs_2_.refs_3_, ...), custom_call_target="tpu_custom_call" | custom-call | tf_op jit(solution)/shard_map/pallas_call | solution.py:109
  193.6 14.2 %shard_map.58 = (f32[1024,768]{1,0:T(8,128)}, f32[1024,768]{1,0:T(8,128)}, f32[1024,768]{1,0:T(8,128)}) custom-call(f32[1,1024]{1,0:T(1,128)} %bitcast.66, bf16[1024,768]{1,0:T(8,128)(2,1)} %fusion.15.refs_0_.refs_1_, bf16[512,1536]{1,0:T(8,128)(2,1)} %collective-permute-done.10.refs_2_.refs_3_, bf16[512,1536]{1,0:T(8,128)(2,1)} %collective-permute-done.10.refs_2_.refs_3_, ...), custom_call_target="tpu_custom_call" | custom-call | tf_op jit(solution)/shard_map/pallas_call | solution.py:109
  208.4 11.7 %shard_map.59 = (f32[1024,768]{1,0:T(8,128)}, f32[1024,768]{1,0:T(8,128)}, f32[1024,768]{1,0:T(8,128)}) custom-call(f32[1,512]{1,0:T(1,128)} %bitcast.70, bf16[1024,768]{1,0:T(8,128)(2,1)} %fusion.15.refs_0_.refs_1_, bf16[256,1536]{1,0:T(8,128)(2,1)} %collective-permute-done.6.refs_2_.refs_3_, bf16[256,1536]{1,0:T(8,128)(2,1)} %collective-permute-done.6.refs_2_.refs_3_, ...), custom_call_target="tpu_custom_call" | custom-call | tf_op jit(solution)/shard_map/pallas_call | solution.py:109
  221.1 7.5 %shard_map.60 = bf16[512,768]{1,0:T(8,128)(2,1)} custom-call(f32[1,512]{1,0:T(1,128)} %bitcast.64, bf16[1024,768]{1,0:T(8,128)(2,1)} %fusion.15.refs_0_.refs_1_, bf16[256,1536]{1,0:T(8,128)(2,1)} %copy-done.1, bf16[256,1536]{1,0:T(8,128)(2,1)} %copy-done.1, bf16[256,1536]{1,0:T(8,128)(2,1)} %collective-permute-done.4.refs_4_.refs_5_, ...), custom_call_target="tpu_custom_call" | custom-call | tf_op jit(solution)/shard_map/pallas_call | solution.py:109
  228.6 3.1 %convolution_multiply_fusion.1 = f32[512,768]{1,0:T(8,128)} fusion(bf16[512,768]{1,0:T(8,128)(2,1)} %shard_map.60, bf16[768,1536]{1,0:T(8,128)(2,1)S(1)} %copy-done, s32[]{:T(128)S(6)} %select_n.131, f32[]{:T(128)S(6)} %select_n.114), kind=kOutput, calls=%fused_computation.27 | convolution fusion | flops 604372992 | bytes 3538952 | tf_op jit(solution)/shard_map/dot_general | solution.py:208
  239.4 7.5 %shard_map.61 = bf16[512,768]{1,0:T(8,128)(2,1)} custom-call(f32[1,512]{1,0:T(1,128)} %bitcast.65, bf16[1024,768]{1,0:T(8,128)(2,1)} %fusion.15.refs_0_.refs_1_, bf16[256,1536]{1,0:T(8,128)(2,1)} %copy-done.1, bf16[256,1536]{1,0:T(8,128)(2,1)} %copy-done.1, bf16[256,1536]{1,0:T(8,128)(2,1)} %collective-permute-done.4.refs_4_.refs_5_, ...), custom_call_target="tpu_custom_call" | custom-call | tf_op jit(solution)/shard_map/pallas_call | solution.py:109
  251.9 17.9 %collective-permute-done.15 = bf16[512,768]{1,0:T(8,128)(2,1)S(1)} collective-permute-done((bf16[512,768]{1,0:T(8,128)(2,1)S(1)}, bf16[512,768]{1,0:T(8,128)(2,1)S(1)}, u32[]{:S(2)}, u32[]{:S(2)}) %collective-permute-start.15) | collective-permute-done | bytes 786464 | tf_op jit(solution)/shard_map/ppermute | solution.py:25
  (63 shorter events, 26.7 us)
Async XLA Ops:
  0.0 228.6 %copy-start = (bf16[768,1536]{1,0:T(8,128)(2,1)S(1)}, bf16[768,1536]{1,0:T(8,128)(2,1)}, u32[]{:S(2)}) copy-start(bf16[768,1536]{1,0:T(8,128)(2,1)} %param.8) | copy-start | bytes 7077892
  0.0 2.8 %copy-start.2 = (bf16[1,1,512,1536]{3,2,1,0:T(8,128)(2,1)S(1)}, bf16[1,1,512,1536]{3,2,1,0:T(8,128)(2,1)}, u32[]{:S(2)}) copy-start(bf16[1,1,512,1536]{3,2,1,0:T(8,128)(2,1)} %param.5) | copy-start | bytes 4718596
  4.5 37.6 %collective-permute-start = (bf16[512,1536]{1,0:T(8,128)(2,1)}, bf16[512,1536]{1,0:T(8,128)(2,1)}, u32[]{:S(2)}, u32[]{:S(2)}) collective-permute-start(bf16[512,1536]{1,0:T(8,128)(2,1)} %fusion.5), channel_id=1, source_target_pairs={{0,1},{1,0},{2,3},{3,2},{4,5},{5,4},{6,7},{7,6},{8,9},{9,8},{10,11... | collective-permute-start | bytes 4718600 | tf_op jit(solution)/shard_map/ppermute | solution.py:25
  19.5 22.6 %copy-start.3 = (bf16[1536,2,768]{0,2,1:T(8,128)(2,1)S(1)}, bf16[1536,2,768]{0,2,1:T(8,128)(2,1)}, u32[]{:S(2)}) copy-start(bf16[1536,2,768]{0,2,1:T(8,128)(2,1)} %copy.7) | copy-start | bytes 14155780
  26.4 55.8 %collective-permute-start.11 = (bf16[512,1536]{1,0:T(8,128)(2,1)}, bf16[512,1536]{1,0:T(8,128)(2,1)}, u32[]{:S(2)}, u32[]{:S(2)}) collective-permute-start(bf16[512,1536]{1,0:T(8,128)(2,1)} %convolution_convert_fusion.refs_1_.refs_2_), channel_id=1, source_target_pairs={{0,62},{2,0},{4,2},{6,4},{8,6},{10,8},{12,10},{14,12},{16,14},{18,... | collective-permute-start | bytes 4718600 | tf_op jit(solution)/shard_map/ppermute | solution.py:21
  32.6 49.5 %collective-permute-start.9 = (bf16[512,1536]{1,0:T(8,128)(2,1)}, bf16[512,1536]{1,0:T(8,128)(2,1)}, u32[]{:S(2)}, u32[]{:S(2)}) collective-permute-start(bf16[512,1536]{1,0:T(8,128)(2,1)} %convolution_convert_fusion.refs_1_.refs_2_), channel_id=1, source_target_pairs={{0,2},{2,4},{4,6},{6,8},{8,10},{10,12},{12,14},{14,16},{16,18},{18... | collective-permute-start | bytes 4718600 | tf_op jit(solution)/shard_map/ppermute | solution.py:21
  67.0 32.0 %copy-start.6 = (s32[1,4,8]{2,1,0:T(4,128)S(1)}, s32[1,4,8]{2,1,0:T(4,128)}, u32[]{:S(2)}) copy-start(s32[1,4,8]{2,1,0:T(4,128)} %param.9) | copy-start | bytes 388
  69.3 29.7 %collective-permute-start.1 = (bf16[256,1536]{1,0:T(8,128)(2,1)S(1)}, bf16[256,1536]{1,0:T(8,128)(2,1)}, u32[]{:S(2)}, u32[]{:S(2)}) collective-permute-start(bf16[256,1536]{1,0:T(8,128)(2,1)S(1)} %get-tuple-element.54), channel_id=1, source_target_pairs={{0,2},{2,4},{4,6},{6,8},{8,10},{10,12},{12,14},{14,16},{16,18},{18... | collective-permute-start | bytes 2359304 | tf_op jit(solution)/shard_map/ppermute | solution.py:21
  82.1 73.1 %collective-permute-start.10 = (bf16[512,1536]{1,0:T(8,128)(2,1)}, bf16[512,1536]{1,0:T(8,128)(2,1)}, u32[]{:S(2)}, u32[]{:S(2)}) collective-permute-start(bf16[512,1536]{1,0:T(8,128)(2,1)} %collective-permute-done.9.refs_2_.refs_3_), channel_id=1, source_target_pairs={{0,2},{2,4},{4,6},{6,8},{8,10},{10,12},{12,14},{14,16},{16,18},{18... | collective-permute-start | bytes 4718600 | tf_op jit(solution)/shard_map/ppermute | solution.py:21
  82.1 110.8 %collective-permute-start.12 = (bf16[512,1536]{1,0:T(8,128)(2,1)}, bf16[512,1536]{1,0:T(8,128)(2,1)}, u32[]{:S(2)}, u32[]{:S(2)}) collective-permute-start(bf16[512,1536]{1,0:T(8,128)(2,1)} %collective-permute-done.11.refs_4_.refs_5_), channel_id=1, source_target_pairs={{0,62},{2,0},{4,2},{6,4},{8,6},{10,8},{12,10},{14,12},{16,14},{18,... | collective-permute-start | bytes 4718600 | tf_op jit(solution)/shard_map/ppermute | solution.py:21
  87.8 61.7 %collective-permute-start.5 = (bf16[256,1536]{1,0:T(8,128)(2,1)}, bf16[256,1536]{1,0:T(8,128)(2,1)}, u32[]{:S(2)}, u32[]{:S(2)}) collective-permute-start(bf16[256,1536]{1,0:T(8,128)(2,1)} %get-tuple-element.53), channel_id=1, source_target_pairs={{0,2},{2,4},{4,6},{6,8},{8,10},{10,12},{12,14},{14,16},{16,18},{18... | collective-permute-start | bytes 2359304 | tf_op jit(solution)/shard_map/ppermute | solution.py:21
  87.8 61.7 %collective-permute-start.7 = (bf16[256,1536]{1,0:T(8,128)(2,1)}, bf16[256,1536]{1,0:T(8,128)(2,1)}, u32[]{:S(2)}, u32[]{:S(2)}) collective-permute-start(bf16[256,1536]{1,0:T(8,128)(2,1)} %get-tuple-element.53), channel_id=1, source_target_pairs={{0,62},{2,0},{4,2},{6,4},{8,6},{10,8},{12,10},{14,12},{16,14},{18,... | collective-permute-start | bytes 2359304 | tf_op jit(solution)/shard_map/ppermute | solution.py:21
  99.0 56.3 %collective-permute-start.3 = (bf16[256,1536]{1,0:T(8,128)(2,1)S(1)}, bf16[256,1536]{1,0:T(8,128)(2,1)}, u32[]{:S(2)}, u32[]{:S(2)}) collective-permute-start(bf16[256,1536]{1,0:T(8,128)(2,1)S(1)} %get-tuple-element.54), channel_id=1, source_target_pairs={{0,62},{2,0},{4,2},{6,4},{8,6},{10,8},{12,10},{14,12},{16,14},{18,... | collective-permute-start | bytes 2359304 | tf_op jit(solution)/shard_map/ppermute | solution.py:21
  149.6 58.2 %collective-permute-start.6 = (bf16[256,1536]{1,0:T(8,128)(2,1)}, bf16[256,1536]{1,0:T(8,128)(2,1)}, u32[]{:S(2)}, u32[]{:S(2)}) collective-permute-start(bf16[256,1536]{1,0:T(8,128)(2,1)} %collective-permute-done.5.refs_2_.refs_3_), channel_id=1, source_target_pairs={{0,2},{2,4},{4,6},{6,8},{8,10},{10,12},{12,14},{14,16},{16,18},{18... | collective-permute-start | bytes 2359304 | tf_op jit(solution)/shard_map/ppermute | solution.py:21
  149.6 58.2 %collective-permute-start.8 = (bf16[256,1536]{1,0:T(8,128)(2,1)}, bf16[256,1536]{1,0:T(8,128)(2,1)}, u32[]{:S(2)}, u32[]{:S(2)}) collective-permute-start(bf16[256,1536]{1,0:T(8,128)(2,1)} %collective-permute-done.7.refs_4_.refs_5_), channel_id=1, source_target_pairs={{0,62},{2,0},{4,2},{6,4},{8,6},{10,8},{12,10},{14,12},{16,14},{18,... | collective-permute-start | bytes 2359304 | tf_op jit(solution)/shard_map/ppermute | solution.py:21
  155.2 64.9 %collective-permute-start.2 = (bf16[256,1536]{1,0:T(8,128)(2,1)}, bf16[256,1536]{1,0:T(8,128)(2,1)S(1)}, u32[]{:S(2)}, u32[]{:S(2)}) collective-permute-start(bf16[256,1536]{1,0:T(8,128)(2,1)} %collective-permute-done.1.refs_6_.refs_7_), channel_id=1, source_target_pairs={{0,2},{2,4},{4,6},{6,8},{8,10},{10,12},{12,14},{14,16},{16,18},{18... | collective-permute-start | bytes 2359304 | tf_op jit(solution)/shard_map/ppermute | solution.py:21
  155.3 64.9 %collective-permute-start.4 = (bf16[256,1536]{1,0:T(8,128)(2,1)}, bf16[256,1536]{1,0:T(8,128)(2,1)}, u32[]{:S(2)}, u32[]{:S(2)}) collective-permute-start(bf16[256,1536]{1,0:T(8,128)(2,1)} %collective-permute-done.3.refs_8_.refs_9_), channel_id=1, source_target_pairs={{0,62},{2,0},{4,2},{6,4},{8,6},{10,8},{12,10},{14,12},{16,14},{18,... | collective-permute-start | bytes 2359304 | tf_op jit(solution)/shard_map/ppermute | solution.py:21
  220.2 0.9 copy-start.1
  228.6 5.8 %copy-start.5 = (bf16[512,768]{1,0:T(8,128)(2,1)S(1)}, bf16[512,768]{1,0:T(8,128)(2,1)}, u32[]{:S(2)}) copy-start(bf16[512,768]{1,0:T(8,128)(2,1)} %shard_map.60) | copy-start | bytes 2359300
  231.7 6.0 %collective-permute-start.13 = (f32[512,768]{1,0:T(8,128)}, f32[512,768]{1,0:T(8,128)}, u32[]{:S(2)}, u32[]{:S(2)}) collective-permute-start(f32[512,768]{1,0:T(8,128)} %convolution_multiply_fusion.1), channel_id=1, source_target_pairs={{0,64},{64,0},{1,65},{65,1},{2,66},{66,2},{3,67},{67,3},{4,68},{68... | collective-permute-start | bytes 4718600 | tf_op jit(solution)/shard_map/ppermute | solution.py:25
  246.9 4.2 %copy-start.4 = (bf16[512,768]{1,0:T(8,128)(2,1)S(1)}, bf16[512,768]{1,0:T(8,128)(2,1)}, u32[]{:S(2)}) copy-start(bf16[512,768]{1,0:T(8,128)(2,1)} %shard_map.61) | copy-start | bytes 2359300
  248.9 20.9 %collective-permute-start.14 = (f32[512,768]{1,0:T(8,128)S(1)}, f32[512,768]{1,0:T(8,128)S(1)}, u32[]{:S(2)}, u32[]{:S(2)}) collective-permute-start(f32[512,768]{1,0:T(8,128)S(1)} %convolution_multiply_fusion), channel_id=1, source_target_pairs={{0,64},{64,0},{1,65},{65,1},{2,66},{66,2},{3,67},{67,3},{4,68},{68... | collective-permute-start | bytes 4718600 | tf_op jit(solution)/shard_map/ppermute | solution.py:25
  249.4 20.5 %collective-permute-start.15 = (bf16[512,768]{1,0:T(8,128)(2,1)S(1)}, bf16[512,768]{1,0:T(8,128)(2,1)S(1)}, u32[]{:S(2)}, u32[]{:S(2)}) collective-permute-start(bf16[512,768]{1,0:T(8,128)(2,1)S(1)} %add_convert_fusion.1), channel_id=1, source_target_pairs={{0,1},{1,0},{2,3},{3,2},{4,5},{5,4},{6,7},{7,6},{8,9},{9,8},{10,11... | collective-permute-start | bytes 2359304 | tf_op jit(solution)/shard_map/ppermute | solution.py:25

commit v11 on v9

--- a/solution.py
+++ b/solution.py
@@ -132,7 +132,6 @@
     q_w = w_qkv[:, 0, :]
     pair_own = jnp.dot(normed, kv_w, preferred_element_type=jnp.float32).astype(jnp.bfloat16)
 
-    pair_own, partner_normed = lax.optimization_barrier((pair_own, partner_normed))
     near_own = {sign: from_behind(pair_own, "orbit", -sign) for sign in (1, -1)}
 
     pair_other = jnp.dot(partner_normed, kv_w, preferred_element_type=jnp.float32).astype(
@@ -184,13 +183,15 @@
     owner = lax.axis_index("cfg")
     half_width = width // 2
     weight_now = jnp.where(owner == 0, guide_scale, 1.0 - guide_scale).astype(jnp.float32)
+    weight_other = jnp.where(owner == 0, 1.0 - guide_scale, guide_scale).astype(jnp.float32)
     w_mine = lax.dynamic_slice_in_dim(w_out, owner * half_width, half_width, 1)
-    w_theirs = lax.dynamic_slice_in_dim(w_out, (1 - owner) * half_width, half_width, 1)
 
     def project(context):
-        theirs = weight_now * jnp.dot(context, w_theirs, preferred_element_type=jnp.float32)
+        other_branch = swap(context, "cfg")
         mine = weight_now * jnp.dot(context, w_mine, preferred_element_type=jnp.float32)
-        return mine + swap(theirs, "cfg")
+        return mine + weight_other * jnp.dot(
+            other_branch, w_mine, preferred_element_type=jnp.float32
+        )
 
     to_partner = project(context_other).astype(jnp.bfloat16)
     to_partner, carry = lax.optimization_barrier((to_partner, carry))

time: 251 us -> 232 us (0.924)
  waiting for transfers between devices: 94.9 us -> 82.1 us
  matrix products: 25.1 us -> 22.4 us
  other arithmetic: 7.57 us -> 4.87 us
    ppermute x8, waiting for transfers between devices: 59.3 us -> 52.4 us  [from_behind(): lax.ppermute(array, axis, [(i, (i + by) % count) for i in range(count)])]
    ppermute x4, waiting for transfers between devices: 35.6 us -> 29.7 us  [swap(): return lax.ppermute(array, axis, [(0, 1), (1, 0)])]
    dot_general x2, matrix products: 5.17 us -> 1.55 us  [project(): jnp.dot(other_branch, w_mine, preferred_element_type=jnp.float32)]
    unnamed x15 -> x13, local copies, waits for them, and re-layouts: 6.74 us -> 6.65 us
  transfers between devices with their start and end apart: 12 -> 12, of which waited for: 6 -> 7; matrix products, arithmetic and copies ran while one was open for 9% -> 14% of each run, Pallas kernels for 22% -> 24%
where the time goes in v11:
time: 232 us; the launch traced here: 230 us
  waiting for transfers between devices  82.1 us (35%)
  Pallas kernels  74.3 us (32%)
  starting transfers between devices  32.4 us (14%)
  matrix products  22.4 us (10%)
  local copies, waits for them, and re-layouts  14.2 us (6%)
  other arithmetic  4.87 us (2%)
    pallas_call x6, Pallas kernels, attend_stage(): pl.pallas_call(kernel, out_shape=out_shape, grid=(heads,), in_specs=in_sp...  74.3 us
    ppermute x8, waiting for transfers between devices, from_behind(): lax.ppermute(array, axis, [(i, (i + by) % count) for i in range(count)])  52.4 us
    ppermute x4, waiting for transfers between devices, swap(): return lax.ppermute(array, axis, [(0, 1), (1, 0)])  29.7 us
    ppermute x8, starting transfers between devices, from_behind(): lax.ppermute(array, axis, [(i, (i + by) % count) for i in range(count)])  25.1 us
    ppermute x4, starting transfers between devices, swap(): return lax.ppermute(array, axis, [(0, 1), (1, 0)])  7.29 us
    dot_general x1, matrix products, per_device_body(): jnp.dot(normed, kv_w, preferred_element_type=jnp.float32)  6.8 us
    unnamed x13, local copies, waits for them, and re-layouts  6.65 us
    dot_general x1, matrix products, per_device_body(): jnp.dot(both_rows, q_w, preferred_element_type=jnp.float32)  6.39 us
  transfers between devices with their start and end apart: 12, of which 7 were waited for; matrix products, arithmetic and copies ran while one was open for 14% of the time, Pallas kernels for 24%

profile of v11, /device:TPU:1, one launch (start us, length us, event | category | flops | bytes accessed | tf_op | source)
XLA Modules:
  0.0 230.4 jit_solution(737884591572145511)
XLA Ops:
  0.9 1.9 fusion.2
  2.8 1.8 fusion.5
  4.6 3.6 %collective-permute-start = (bf16[512,1536]{1,0:T(8,128)(2,1)}, bf16[512,1536]{1,0:T(8,128)(2,1)}, u32[]{:S(2)}, u32[]{:S(2)}) collective-permute-start(bf16[512,1536]{1,0:T(8,128)(2,1)} %fusion.5), channel_id=1, source_target_pairs={{0,1},{1,0},{2,3},{3,2},{4,5},{5,4},{6,7},{7,6},{8,9},{9,8},{10,11... | collective-permute-start | bytes 4718600 | tf_op jit(solution)/shard_map/ppermute | solution.py:25
  8.1 4.7 %slice.39 = bf16[1536,2,768]{2,0,1:T(8,128)(2,1)} slice(bf16[1536,3,768]{2,0,1:T(8,128)(2,1)} %param.7), slice={[0:1536], [1:3], [0:768]} | slice | bytes 9437184 | tf_op jit(solution)/shard_map/slice | solution.py:131
  12.9 6.6 %copy.7 = bf16[1536,2,768]{0,2,1:T(8,128)(2,1)} copy(bf16[1536,2,768]{2,0,1:T(8,128)(2,1)} %slice.39) | data formatting | bytes 9437184
  19.5 6.8 %convolution_convert_fusion.refs_1_.refs_2_ = bf16[512,1536]{1,0:T(8,128)(2,1)} fusion(bf16[1536,1536]{0,1:T(8,128)(2,1)} %bitcast.52, bf16[1,1,512,1536]{3,2,1,0:T(8,128)(2,1)} %param.5, f32[1536]{0:T(1024)S(1)} %get-tuple-element.46, f32[1536]{0:T(1024)S(1)} %get-tuple-element.45, f32[512]{0:T(512)S(1)} %add_rsqrt_fusion), kind=kOutput, calls=%fused_computation.15 | convolution fusion | flops 2420637696 | bytes 7878656 | tf_op jit(solution)/shard_map/dot_general | solution.py:133
  27.6 4.9 %collective-permute-start.7 = (bf16[512,1536]{1,0:T(8,128)(2,1)}, bf16[512,1536]{1,0:T(8,128)(2,1)}, u32[]{:S(2)}, u32[]{:S(2)}) collective-permute-start(bf16[512,1536]{1,0:T(8,128)(2,1)} %convolution_convert_fusion.refs_1_.refs_2_), channel_id=1, source_target_pairs={{0,62},{2,0},{4,2},{6,4},{8,6},{10,8},{12,10},{14,12},{16,14},{18,... | collective-permute-start | bytes 4718600 | tf_op jit(solution)/shard_map/ppermute | solution.py:21
  32.5 9.6 %collective-permute-done = bf16[512,1536]{1,0:T(8,128)(2,1)} collective-permute-done((bf16[512,1536]{1,0:T(8,128)(2,1)}, bf16[512,1536]{1,0:T(8,128)(2,1)}, u32[]{:S(2)}, u32[]{:S(2)}) %collective-permute-start) | collective-permute-done | bytes 1572896 | tf_op jit(solution)/shard_map/ppermute | solution.py:25
  42.2 5.2 %convolution_convert_fusion.1.refs_3_.refs_4_ = bf16[512,1536]{1,0:T(8,128)(2,1)} fusion(bf16[512,1536]{1,0:T(8,128)(2,1)} %collective-permute-done, bf16[1536,1536]{0,1:T(8,128)(2,1)S(1)} %bitcast.53), kind=kOutput, calls=%fused_computation.16 | convolution fusion | flops 2416705536 | bytes 7864320 | tf_op jit(solution)/shard_map/dot_general | solution.py:137
  47.4 6.4 %fusion.15.refs_0_.refs_1_ = bf16[1024,768]{1,0:T(8,128)(2,1)} fusion(bf16[1536,3,768]{2,0,1:T(8,128)(2,1)} %param.7, bf16[512,1536]{1,0:T(8,128)(2,1)} %collective-permute-done, bf16[512,1536]{1,0:T(8,128)(2,1)} %fusion.5), kind=kOutput, calls=%fused_computation.19 | convolution fusion | flops 2422996992 | bytes 7077888 | tf_op jit(solution)/shard_map/dot_general | solution.py:141
  53.8 13.3 %shard_map.55 = (f32[1024,768]{1,0:T(8,128)}, f32[1024,768]{1,0:T(8,128)}, f32[1024,768]{1,0:T(8,128)}) custom-call(bf16[1024,768]{1,0:T(8,128)(2,1)} %fusion.15.refs_0_.refs_1_, bf16[512,1536]{1,0:T(8,128)(2,1)} %convolution_convert_fusion.refs_1_.refs_2_, bf16[512,1536]{1,0:T(8,128)(2,1)} %convolution_convert_fusion.refs_1_.refs_2_, ...), custom_call_target="tpu_custom_call" | custom-call | tf_op jit(solution)/shard_map/pallas_call | solution.py:109
  68.7 5.9 %collective-permute-start.3 = (bf16[512,1536]{1,0:T(8,128)(2,1)}, bf16[512,1536]{1,0:T(8,128)(2,1)}, u32[]{:S(2)}, u32[]{:S(2)}) collective-permute-start(bf16[512,1536]{1,0:T(8,128)(2,1)} %convolution_convert_fusion.1.refs_3_.refs_4_), channel_id=1, source_target_pairs={{0,62},{2,0},{4,2},{6,4},{8,6},{10,8},{12,10},{14,12},{16,14},{18,... | collective-permute-start | bytes 4718600 | tf_op jit(solution)/shard_map/ppermute | solution.py:21
  74.6 7.6 %collective-permute-done.5.refs_2_.refs_3_ = bf16[512,1536]{1,0:T(8,128)(2,1)} collective-permute-done((bf16[512,1536]{1,0:T(8,128)(2,1)}, bf16[512,1536]{1,0:T(8,128)(2,1)}, u32[]{:S(2)}, u32[]{:S(2)}) %collective-permute-start.5) | collective-permute-done | bytes 1572896 | tf_op jit(solution)/shard_map/ppermute | solution.py:21
  82.2 5.7 %collective-permute-start.8 = (bf16[512,1536]{1,0:T(8,128)(2,1)}, bf16[512,1536]{1,0:T(8,128)(2,1)}, u32[]{:S(2)}, u32[]{:S(2)}) collective-permute-start(bf16[512,1536]{1,0:T(8,128)(2,1)} %collective-permute-done.7.refs_4_.refs_5_), channel_id=1, source_target_pairs={{0,62},{2,0},{4,2},{6,4},{8,6},{10,8},{12,10},{14,12},{16,14},{18,... | collective-permute-start | bytes 4718600 | tf_op jit(solution)/shard_map/ppermute | solution.py:21
  87.9 28.0 %collective-permute-done.1.refs_2_.refs_3_ = bf16[512,1536]{1,0:T(8,128)(2,1)} collective-permute-done((bf16[512,1536]{1,0:T(8,128)(2,1)}, bf16[512,1536]{1,0:T(8,128)(2,1)}, u32[]{:S(2)}, u32[]{:S(2)}) %collective-permute-start.1) | collective-permute-done | bytes 1572896 | tf_op jit(solution)/shard_map/ppermute | solution.py:21
  115.9 5.7 %collective-permute-start.4 = (bf16[512,1536]{1,0:T(8,128)(2,1)}, bf16[512,1536]{1,0:T(8,128)(2,1)}, u32[]{:S(2)}, u32[]{:S(2)}) collective-permute-start(bf16[512,1536]{1,0:T(8,128)(2,1)} %collective-permute-done.3.refs_4_.refs_5_), channel_id=1, source_target_pairs={{0,62},{2,0},{4,2},{6,4},{8,6},{10,8},{12,10},{14,12},{16,14},{18,... | collective-permute-start | bytes 4718600 | tf_op jit(solution)/shard_map/ppermute | solution.py:21
  122.7 14.2 %shard_map.56 = (f32[1024,768]{1,0:T(8,128)}, f32[1024,768]{1,0:T(8,128)}, f32[1024,768]{1,0:T(8,128)}) custom-call(f32[1,1024]{1,0:T(1,128)} %bitcast.57, bf16[1024,768]{1,0:T(8,128)(2,1)} %fusion.15.refs_0_.refs_1_, bf16[512,1536]{1,0:T(8,128)(2,1)} %collective-permute-done.5.refs_2_.refs_3_, bf16[512,1536]{1,0:T(8,128)(2,1)} %collective-permute-done.5.refs_2_.refs_3_, ...), custom_call_target="tpu_custom_call" | custom-call | tf_op jit(solution)/shard_map/pallas_call | solution.py:109
  137.6 14.2 %shard_map.57 = (f32[1024,768]{1,0:T(8,128)}, f32[1024,768]{1,0:T(8,128)}, f32[1024,768]{1,0:T(8,128)}) custom-call(f32[1,1024]{1,0:T(1,128)} %bitcast.58, bf16[1024,768]{1,0:T(8,128)(2,1)} %fusion.15.refs_0_.refs_1_, bf16[512,1536]{1,0:T(8,128)(2,1)} %collective-permute-done.1.refs_2_.refs_3_, bf16[512,1536]{1,0:T(8,128)(2,1)} %collective-permute-done.1.refs_2_.refs_3_, ...), custom_call_target="tpu_custom_call" | custom-call | tf_op jit(solution)/shard_map/pallas_call | solution.py:109
  152.4 14.1 %shard_map.58 = (f32[1024,768]{1,0:T(8,128)}, f32[1024,768]{1,0:T(8,128)}, f32[1024,768]{1,0:T(8,128)}) custom-call(f32[1,1024]{1,0:T(1,128)} %bitcast.56, bf16[1024,768]{1,0:T(8,128)(2,1)} %fusion.15.refs_0_.refs_1_, bf16[512,1536]{1,0:T(8,128)(2,1)} %collective-permute-done.6.refs_2_.refs_3_, bf16[512,1536]{1,0:T(8,128)(2,1)} %collective-permute-done.6.refs_2_.refs_3_, ...), custom_call_target="tpu_custom_call" | custom-call | tf_op jit(solution)/shard_map/pallas_call | solution.py:109
  166.6 16.8 %collective-permute-done.2.refs_2_.refs_3_ = bf16[512,1536]{1,0:T(8,128)(2,1)} collective-permute-done((bf16[512,1536]{1,0:T(8,128)(2,1)}, bf16[512,1536]{1,0:T(8,128)(2,1)}, u32[]{:S(2)}, u32[]{:S(2)}) %collective-permute-start.2) | collective-permute-done | bytes 1572896 | tf_op jit(solution)/shard_map/ppermute | solution.py:21
  184.0 9.3 %shard_map.59 = bf16[512,768]{1,0:T(8,128)(2,1)} custom-call(f32[1,1024]{1,0:T(1,128)} %bitcast.54, bf16[1024,768]{1,0:T(8,128)(2,1)} %fusion.15.refs_0_.refs_1_, bf16[512,1536]{1,0:T(8,128)(2,1)} %collective-permute-done.2.refs_2_.refs_3_, bf16[512,1536]{1,0:T(8,128)(2,1)} %collective-permute-done.2.refs_2_.refs_3_, ...), custom_call_target="tpu_custom_call" | custom-call | tf_op jit(solution)/shard_map/pallas_call | solution.py:109
  194.8 2.1 collective-permute-done.9
  198.5 9.3 %shard_map.60 = bf16[512,768]{1,0:T(8,128)(2,1)} custom-call(f32[1,1024]{1,0:T(1,128)} %bitcast.55, bf16[1024,768]{1,0:T(8,128)(2,1)} %fusion.15.refs_0_.refs_1_, bf16[512,1536]{1,0:T(8,128)(2,1)} %collective-permute-done.2.refs_2_.refs_3_, bf16[512,1536]{1,0:T(8,128)(2,1)} %collective-permute-done.2.refs_2_.refs_3_, ...), custom_call_target="tpu_custom_call" | custom-call | tf_op jit(solution)/shard_map/pallas_call | solution.py:109
  211.1 17.6 %collective-permute-done.11 = bf16[512,768]{1,0:T(8,128)(2,1)S(1)} collective-permute-done((bf16[512,768]{1,0:T(8,128)(2,1)S(1)}, bf16[512,768]{1,0:T(8,128)(2,1)S(1)}, u32[]{:S(2)}, u32[]{:S(2)}) %collective-permute-start.11) | collective-permute-done | bytes 786464 | tf_op jit(solution)/shard_map/ppermute | solution.py:25
  (42 shorter events, 15.2 us)
Async XLA Ops:
  0.0 196.9 %copy-start = (bf16[768,1536]{1,0:T(8,128)(2,1)S(1)}, bf16[768,1536]{1,0:T(8,128)(2,1)}, u32[]{:S(2)}) copy-start(bf16[768,1536]{1,0:T(8,128)(2,1)} %param.8) | copy-start | bytes 7077892
  0.0 2.8 %copy-start.1 = (bf16[1,1,512,1536]{3,2,1,0:T(8,128)(2,1)S(1)}, bf16[1,1,512,1536]{3,2,1,0:T(8,128)(2,1)}, u32[]{:S(2)}) copy-start(bf16[1,1,512,1536]{3,2,1,0:T(8,128)(2,1)} %param.5) | copy-start | bytes 4718596
  4.6 37.6 %collective-permute-start = (bf16[512,1536]{1,0:T(8,128)(2,1)}, bf16[512,1536]{1,0:T(8,128)(2,1)}, u32[]{:S(2)}, u32[]{:S(2)}) collective-permute-start(bf16[512,1536]{1,0:T(8,128)(2,1)} %fusion.5), channel_id=1, source_target_pairs={{0,1},{1,0},{2,3},{3,2},{4,5},{5,4},{6,7},{7,6},{8,9},{9,8},{10,11... | collective-permute-start | bytes 4718600 | tf_op jit(solution)/shard_map/ppermute | solution.py:25
  19.5 22.7 %copy-start.2 = (bf16[1536,2,768]{0,2,1:T(8,128)(2,1)S(1)}, bf16[1536,2,768]{0,2,1:T(8,128)(2,1)}, u32[]{:S(2)}) copy-start(bf16[1536,2,768]{0,2,1:T(8,128)(2,1)} %copy.7) | copy-start | bytes 14155780
  26.3 55.9 %collective-permute-start.5 = (bf16[512,1536]{1,0:T(8,128)(2,1)}, bf16[512,1536]{1,0:T(8,128)(2,1)}, u32[]{:S(2)}, u32[]{:S(2)}) collective-permute-start(bf16[512,1536]{1,0:T(8,128)(2,1)} %convolution_convert_fusion.refs_1_.refs_2_), channel_id=1, source_target_pairs={{0,2},{2,4},{4,6},{6,8},{8,10},{10,12},{12,14},{14,16},{16,18},{18... | collective-permute-start | bytes 4718600 | tf_op jit(solution)/shard_map/ppermute | solution.py:21
  27.6 54.6 %collective-permute-start.7 = (bf16[512,1536]{1,0:T(8,128)(2,1)}, bf16[512,1536]{1,0:T(8,128)(2,1)}, u32[]{:S(2)}, u32[]{:S(2)}) collective-permute-start(bf16[512,1536]{1,0:T(8,128)(2,1)} %convolution_convert_fusion.refs_1_.refs_2_), channel_id=1, source_target_pairs={{0,62},{2,0},{4,2},{6,4},{8,6},{10,8},{12,10},{14,12},{16,14},{18,... | collective-permute-start | bytes 4718600 | tf_op jit(solution)/shard_map/ppermute | solution.py:21
  53.8 67.9 %copy-start.5 = (s32[1,4,8]{2,1,0:T(4,128)S(1)}, s32[1,4,8]{2,1,0:T(4,128)}, u32[]{:S(2)}) copy-start(s32[1,4,8]{2,1,0:T(4,128)} %param.9) | copy-start | bytes 388
  67.1 48.8 %collective-permute-start.1 = (bf16[512,1536]{1,0:T(8,128)(2,1)}, bf16[512,1536]{1,0:T(8,128)(2,1)}, u32[]{:S(2)}, u32[]{:S(2)}) collective-permute-start(bf16[512,1536]{1,0:T(8,128)(2,1)} %convolution_convert_fusion.1.refs_3_.refs_4_), channel_id=1, source_target_pairs={{0,2},{2,4},{4,6},{6,8},{8,10},{10,12},{12,14},{14,16},{16,18},{18... | collective-permute-start | bytes 4718600 | tf_op jit(solution)/shard_map/ppermute | solution.py:21
  68.7 47.2 %collective-permute-start.3 = (bf16[512,1536]{1,0:T(8,128)(2,1)}, bf16[512,1536]{1,0:T(8,128)(2,1)}, u32[]{:S(2)}, u32[]{:S(2)}) collective-permute-start(bf16[512,1536]{1,0:T(8,128)(2,1)} %convolution_convert_fusion.1.refs_3_.refs_4_), channel_id=1, source_target_pairs={{0,62},{2,0},{4,2},{6,4},{8,6},{10,8},{12,10},{14,12},{16,14},{18,... | collective-permute-start | bytes 4718600 | tf_op jit(solution)/shard_map/ppermute | solution.py:21
  82.2 69.5 %collective-permute-start.6 = (bf16[512,1536]{1,0:T(8,128)(2,1)}, bf16[512,1536]{1,0:T(8,128)(2,1)}, u32[]{:S(2)}, u32[]{:S(2)}) collective-permute-start(bf16[512,1536]{1,0:T(8,128)(2,1)} %collective-permute-done.5.refs_2_.refs_3_), channel_id=1, source_target_pairs={{0,2},{2,4},{4,6},{6,8},{8,10},{10,12},{12,14},{14,16},{16,18},{18... | collective-permute-start | bytes 4718600 | tf_op jit(solution)/shard_map/ppermute | solution.py:21
  82.2 69.5 %collective-permute-start.8 = (bf16[512,1536]{1,0:T(8,128)(2,1)}, bf16[512,1536]{1,0:T(8,128)(2,1)}, u32[]{:S(2)}, u32[]{:S(2)}) collective-permute-start(bf16[512,1536]{1,0:T(8,128)(2,1)} %collective-permute-done.7.refs_4_.refs_5_), channel_id=1, source_target_pairs={{0,62},{2,0},{4,2},{6,4},{8,6},{10,8},{12,10},{14,12},{16,14},{18,... | collective-permute-start | bytes 4718600 | tf_op jit(solution)/shard_map/ppermute | solution.py:21
  115.9 67.4 %collective-permute-start.2 = (bf16[512,1536]{1,0:T(8,128)(2,1)}, bf16[512,1536]{1,0:T(8,128)(2,1)}, u32[]{:S(2)}, u32[]{:S(2)}) collective-permute-start(bf16[512,1536]{1,0:T(8,128)(2,1)} %collective-permute-done.1.refs_2_.refs_3_), channel_id=1, source_target_pairs={{0,2},{2,4},{4,6},{6,8},{8,10},{10,12},{12,14},{14,16},{16,18},{18... | collective-permute-start | bytes 4718600 | tf_op jit(solution)/shard_map/ppermute | solution.py:21
  115.9 67.4 %collective-permute-start.4 = (bf16[512,1536]{1,0:T(8,128)(2,1)}, bf16[512,1536]{1,0:T(8,128)(2,1)}, u32[]{:S(2)}, u32[]{:S(2)}) collective-permute-start(bf16[512,1536]{1,0:T(8,128)(2,1)} %collective-permute-done.3.refs_4_.refs_5_), channel_id=1, source_target_pairs={{0,62},{2,0},{4,2},{6,4},{8,6},{10,8},{12,10},{14,12},{16,14},{18,... | collective-permute-start | bytes 4718600 | tf_op jit(solution)/shard_map/ppermute | solution.py:21
  193.3 3.7 %collective-permute-start.9 = (bf16[512,768]{1,0:T(8,128)(2,1)}, bf16[512,768]{1,0:T(8,128)(2,1)S(1)}, u32[]{:S(2)}, u32[]{:S(2)}) collective-permute-start(bf16[512,768]{1,0:T(8,128)(2,1)} %shard_map.59), channel_id=1, source_target_pairs={{0,64},{64,0},{1,65},{65,1},{2,66},{66,2},{3,67},{67,3},{4,68},{68... | collective-permute-start | bytes 2359304 | tf_op jit(solution)/shard_map/ppermute | solution.py:25
  194.8 2.9 %copy-start.3 = (bf16[512,768]{1,0:T(8,128)(2,1)S(1)}, bf16[512,768]{1,0:T(8,128)(2,1)}, u32[]{:S(2)}) copy-start(bf16[512,768]{1,0:T(8,128)(2,1)} %shard_map.59) | copy-start | bytes 2359300
  207.8 21.0 %copy-start.4 = (bf16[512,768]{1,0:T(8,128)(2,1)S(1)}, bf16[512,768]{1,0:T(8,128)(2,1)}, u32[]{:S(2)}) copy-start(bf16[512,768]{1,0:T(8,128)(2,1)} %shard_map.60) | copy-start | bytes 2359300
  207.8 2.6 %collective-permute-start.10 = (bf16[512,768]{1,0:T(8,128)(2,1)}, bf16[512,768]{1,0:T(8,128)(2,1)S(1)}, u32[]{:S(2)}, u32[]{:S(2)}) collective-permute-start(bf16[512,768]{1,0:T(8,128)(2,1)} %shard_map.60), channel_id=1, source_target_pairs={{0,64},{64,0},{1,65},{65,1},{2,66},{66,2},{3,67},{67,3},{4,68},{68... | collective-permute-start | bytes 2359304 | tf_op jit(solution)/shard_map/ppermute | solution.py:25
  208.2 20.5 %collective-permute-start.11 = (bf16[512,768]{1,0:T(8,128)(2,1)S(1)}, bf16[512,768]{1,0:T(8,128)(2,1)S(1)}, u32[]{:S(2)}, u32[]{:S(2)}) collective-permute-start(bf16[512,768]{1,0:T(8,128)(2,1)S(1)} %add_convert_fusion.1), channel_id=1, source_target_pairs={{0,1},{1,0},{2,3},{3,2},{4,5},{5,4},{6,7},{7,6},{8,9},{9,8},{10,11... | collective-permute-start | bytes 2359304 | tf_op jit(solution)/shard_map/ppermute | solution.py:25

commit v12 on v11

--- a/solution.py
+++ b/solution.py
@@ -130,7 +130,9 @@
     partner_normed = swap(normed, "tp")
     kv_w = w_qkv[:, 1:, :].reshape(width, 2 * half_heads)
     q_w = w_qkv[:, 0, :]
-    pair_own = jnp.dot(normed, kv_w, preferred_element_type=jnp.float32).astype(jnp.bfloat16)
+    pair_own = jnp.einsum(
+        "rk,kjn->rjn", normed, w_qkv[:, 1:, :], preferred_element_type=jnp.float32
+    ).astype(jnp.bfloat16).reshape(half_rows, 2 * half_heads)
 
     near_own = {sign: from_behind(pair_own, "orbit", -sign) for sign in (1, -1)}
 
@@ -158,7 +160,6 @@
     carry = attend_stage(
         queries, [pair_own, pair_other], None, None, first=True, last=False, heads=heads
     )
-    pair_other, carry = lax.optimization_barrier((pair_other, carry))
     near_other = {sign: from_behind(pair_other, "orbit", -sign) for sign in (1, -1)}
     far_own = {sign: from_behind(near_own[sign], "orbit", -sign) for sign in (1, -1)}
     carry = attend_stage(

time: 232 us -> 236 us (1.017)
  waiting for transfers between devices: 82.1 us -> 86.1 us
  starting transfers between devices: 32.4 us -> 35.2 us
    unnamed x13 -> x16, local copies, waits for them, and re-layouts: 6.65 us -> 0.03 us
    slice x1 -> x2, local copies, waits for them, and re-layouts: 4.72 us -> 9.06 us  [per_device_body(): kv_w = w_qkv[:, 1:, :].reshape(width, 2 * half_heads)]
    ppermute x4, waiting for transfers between devices: 29.7 us -> 32.1 us  [swap(): return lax.ppermute(array, axis, [(0, 1), (1, 0)])]
  transfers between devices with their start and end apart: 12 -> 12, of which waited for: 7 -> 6; matrix products, arithmetic and copies ran while one was open for 14% -> 13% of each run, Pallas kernels for 24% -> 24%
where the time goes in v12:
time: 236 us; the launch traced here: 235 us
  waiting for transfers between devices  86.1 us (36%)
  Pallas kernels  74.5 us (32%)
  starting transfers between devices  35.2 us (15%)
  matrix products  21.3 us (9%)
  local copies, waits for them, and re-layouts  13.2 us (6%)
  other arithmetic  4.79 us (2%)
    pallas_call x6, Pallas kernels, attend_stage(): pl.pallas_call(kernel, out_shape=out_shape, grid=(heads,), in_specs=in_sp...  74.5 us
    ppermute x8, waiting for transfers between devices, from_behind(): lax.ppermute(array, axis, [(i, (i + by) % count) for i in range(count)])  54 us
    ppermute x4, waiting for transfers between devices, swap(): return lax.ppermute(array, axis, [(0, 1), (1, 0)])  32.1 us
    ppermute x8, starting transfers between devices, from_behind(): lax.ppermute(array, axis, [(i, (i + by) % count) for i in range(count)])  26.2 us
    slice x2, local copies, waits for them, and re-layouts, per_device_body(): kv_w = w_qkv[:, 1:, :].reshape(width, 2 * half_heads)  9.06 us
    ppermute x4, starting transfers between devices, swap(): return lax.ppermute(array, axis, [(0, 1), (1, 0)])  8.98 us
    dot_general x1, matrix products, per_device_body(): jnp.dot(both_rows, q_w, preferred_element_type=jnp.float32)  6.38 us
    dot_general x1, matrix products, per_device_body(): jnp.dot(partner_normed, kv_w, preferred_element_type=jnp.float32)  5.46 us
  transfers between devices with their start and end apart: 12, of which 6 were waited for; matrix products, arithmetic and copies ran while one was open for 13% of the time, Pallas kernels for 24%

profile of v12, /device:TPU:1, one launch (start us, length us, event | category | flops | bytes accessed | tf_op | source)
XLA Modules:
  0.0 235.2 jit_solution(3542385102263292274)
XLA Ops:
  0.9 1.9 fusion
  4.5 3.6 %collective-permute-start = (bf16[512,1536]{1,0:T(8,128)(2,1)}, bf16[512,1536]{1,0:T(8,128)(2,1)}, u32[]{:S(2)}, u32[]{:S(2)}) collective-permute-start(bf16[512,1536]{1,0:T(8,128)(2,1)} %fusion.3), channel_id=1, source_target_pairs={{0,1},{1,0},{2,3},{3,2},{4,5},{5,4},{6,7},{7,6},{8,9},{9,8},{10,11... | collective-permute-start | bytes 4718600 | tf_op jit(solution)/shard_map/ppermute | solution.py:25
  8.1 5.4 %fusion.16 = bf16[2,64,8,768]{3,2,1,0:T(8,128)(2,1)S(1)} fusion(bf16[512,1536]{1,0:T(8,128)(2,1)} %fusion.3, bf16[1536,3,768]{2,0,1:T(8,128)(2,1)} %param.7), kind=kOutput, calls=%fused_computation.18 | convolution fusion | flops 2416705536 | bytes 7864320 | tf_op jit(solution)/shard_map/rk,kjn->rjn/dot_general | solution.py:133
  16.1 4.9 %collective-permute-start.7 = (bf16[512,1536]{1,0:T(8,128)(2,1)}, bf16[512,1536]{1,0:T(8,128)(2,1)}, u32[]{:S(2)}, u32[]{:S(2)}) collective-permute-start(bf16[512,1536]{1,0:T(8,128)(2,1)} %bitcast.19.refs_1_.refs_2_), channel_id=1, source_target_pairs={{0,62},{2,0},{4,2},{6,4},{8,6},{10,8},{12,10},{14,12},{16,14},{18,... | collective-permute-start | bytes 4718600 | tf_op jit(solution)/shard_map/ppermute | solution.py:21
  21.0 2.4 %slice.40 = bf16[1536,2,768]{2,0,1:T(8,128)(2,1)} slice(bf16[1536,3,768]{2,0,1:T(8,128)(2,1)S(1)} %bitcast.48), slice={[0:1536], [1:3], [0:768]} | slice | bytes 9437184 | tf_op jit(solution)/shard_map/slice | solution.py:131
  23.5 6.6 %copy.7 = bf16[1536,2,768]{0,2,1:T(8,128)(2,1)} copy(bf16[1536,2,768]{2,0,1:T(8,128)(2,1)} %slice.40) | data formatting | bytes 9437184 | tf_op jit(solution)/shard_map/slice | solution.py:131
  30.1 12.0 %collective-permute-done = bf16[512,1536]{1,0:T(8,128)(2,1)} collective-permute-done((bf16[512,1536]{1,0:T(8,128)(2,1)}, bf16[512,1536]{1,0:T(8,128)(2,1)}, u32[]{:S(2)}, u32[]{:S(2)}) %collective-permute-start) | collective-permute-done | bytes 1572896 | tf_op jit(solution)/shard_map/ppermute | solution.py:25
  42.1 5.5 %convolution_convert_fusion.refs_3_.refs_4_ = bf16[512,1536]{1,0:T(8,128)(2,1)S(1)} fusion(bf16[512,1536]{1,0:T(8,128)(2,1)} %collective-permute-done, bf16[1536,1536]{0,1:T(8,128)(2,1)} %bitcast.46), kind=kOutput, calls=%fused_computation.10 | convolution fusion | flops 2416705536 | bytes 7864320 | tf_op jit(solution)/shard_map/dot_general | solution.py:139
  49.3 6.9 %collective-permute-start.3 = (bf16[512,1536]{1,0:T(8,128)(2,1)S(1)}, bf16[512,1536]{1,0:T(8,128)(2,1)}, u32[]{:S(2)}, u32[]{:S(2)}) collective-permute-start(bf16[512,1536]{1,0:T(8,128)(2,1)S(1)} %convolution_convert_fusion.refs_3_.refs_4_), channel_id=1, source_target_pairs={{0,62},{2,0},{4,2},{6,4},{8,6},{10,8},{12,10},{14,12},{16,14},{18,... | collective-permute-start | bytes 4718600 | tf_op jit(solution)/shard_map/ppermute | solution.py:21
  56.2 26.0 %collective-permute-done.5.refs_2_.refs_3_ = bf16[512,1536]{1,0:T(8,128)(2,1)} collective-permute-done((bf16[512,1536]{1,0:T(8,128)(2,1)}, bf16[512,1536]{1,0:T(8,128)(2,1)}, u32[]{:S(2)}, u32[]{:S(2)}) %collective-permute-start.5) | collective-permute-done | bytes 1572896 | tf_op jit(solution)/shard_map/ppermute | solution.py:21
  82.2 5.7 %collective-permute-start.8 = (bf16[512,1536]{1,0:T(8,128)(2,1)}, bf16[512,1536]{1,0:T(8,128)(2,1)}, u32[]{:S(2)}, u32[]{:S(2)}) collective-permute-start(bf16[512,1536]{1,0:T(8,128)(2,1)} %collective-permute-done.7.refs_4_.refs_5_), channel_id=1, source_target_pairs={{0,62},{2,0},{4,2},{6,4},{8,6},{10,8},{12,10},{14,12},{16,14},{18,... | collective-permute-start | bytes 4718600 | tf_op jit(solution)/shard_map/ppermute | solution.py:21
  87.8 28.0 %collective-permute-done.1.refs_2_.refs_3_ = bf16[512,1536]{1,0:T(8,128)(2,1)} collective-permute-done((bf16[512,1536]{1,0:T(8,128)(2,1)S(1)}, bf16[512,1536]{1,0:T(8,128)(2,1)}, u32[]{:S(2)}, u32[]{:S(2)}) %collective-permute-start.1) | collective-permute-done | bytes 1572896 | tf_op jit(solution)/shard_map/ppermute | solution.py:21
  115.9 5.7 %collective-permute-start.4 = (bf16[512,1536]{1,0:T(8,128)(2,1)}, bf16[512,1536]{1,0:T(8,128)(2,1)}, u32[]{:S(2)}, u32[]{:S(2)}) collective-permute-start(bf16[512,1536]{1,0:T(8,128)(2,1)} %collective-permute-done.3.refs_4_.refs_5_), channel_id=1, source_target_pairs={{0,62},{2,0},{4,2},{6,4},{8,6},{10,8},{12,10},{14,12},{16,14},{18,... | collective-permute-start | bytes 4718600 | tf_op jit(solution)/shard_map/ppermute | solution.py:21
  122.0 6.4 %fusion.10.refs_0_.refs_1_ = bf16[1024,768]{1,0:T(8,128)(2,1)} fusion(bf16[1536,3,768]{2,0,1:T(8,128)(2,1)} %param.7, bf16[512,1536]{1,0:T(8,128)(2,1)} %collective-permute-done, bf16[512,1536]{1,0:T(8,128)(2,1)} %fusion.3), kind=kOutput, calls=%fused_computation.13 | convolution fusion | flops 2422996992 | bytes 7077888 | tf_op jit(solution)/shard_map/dot_general | solution.py:143
  128.4 13.5 %shard_map.55 = (f32[1024,768]{1,0:T(8,128)}, f32[1024,768]{1,0:T(8,128)}, f32[1024,768]{1,0:T(8,128)}) custom-call(bf16[1024,768]{1,0:T(8,128)(2,1)} %fusion.10.refs_0_.refs_1_, bf16[512,1536]{1,0:T(8,128)(2,1)} %bitcast.19.refs_1_.refs_2_, bf16[512,1536]{1,0:T(8,128)(2,1)} %bitcast.19.refs_1_.refs_2_, bf16[512,1536]{1,0:T(8,128)(2,1)} %copy-done.2, ...), custom_call_target="tpu_custom_call" | custom-call | tf_op jit(solution)/shard_map/pallas_call | solution.py:109
  142.5 14.1 %shard_map.56 = (f32[1024,768]{1,0:T(8,128)}, f32[1024,768]{1,0:T(8,128)}, f32[1024,768]{1,0:T(8,128)}) custom-call(f32[1,1024]{1,0:T(1,128)} %bitcast.52, bf16[1024,768]{1,0:T(8,128)(2,1)} %fusion.10.refs_0_.refs_1_, bf16[512,1536]{1,0:T(8,128)(2,1)} %collective-permute-done.5.refs_2_.refs_3_, bf16[512,1536]{1,0:T(8,128)(2,1)} %collective-permute-done.5.refs_2_.refs_3_, ...), custom_call_target="tpu_custom_call" | custom-call | tf_op jit(solution)/shard_map/pallas_call | solution.py:109
  157.3 14.3 %shard_map.57 = (f32[1024,768]{1,0:T(8,128)}, f32[1024,768]{1,0:T(8,128)}, f32[1024,768]{1,0:T(8,128)}) custom-call(f32[1,1024]{1,0:T(1,128)} %bitcast.53, bf16[1024,768]{1,0:T(8,128)(2,1)} %fusion.10.refs_0_.refs_1_, bf16[512,1536]{1,0:T(8,128)(2,1)} %collective-permute-done.1.refs_2_.refs_3_, bf16[512,1536]{1,0:T(8,128)(2,1)} %collective-permute-done.1.refs_2_.refs_3_, ...), custom_call_target="tpu_custom_call" | custom-call | tf_op jit(solution)/shard_map/pallas_call | solution.py:109
  172.3 14.1 %shard_map.58 = (f32[1024,768]{1,0:T(8,128)}, f32[1024,768]{1,0:T(8,128)}, f32[1024,768]{1,0:T(8,128)}) custom-call(f32[1,1024]{1,0:T(1,128)} %bitcast.51, bf16[1024,768]{1,0:T(8,128)(2,1)} %fusion.10.refs_0_.refs_1_, bf16[512,1536]{1,0:T(8,128)(2,1)} %collective-permute-done.6.refs_2_.refs_3_, bf16[512,1536]{1,0:T(8,128)(2,1)} %collective-permute-done.6.refs_2_.refs_3_, ...), custom_call_target="tpu_custom_call" | custom-call | tf_op jit(solution)/shard_map/pallas_call | solution.py:109
  187.1 9.2 %shard_map.59 = bf16[512,768]{1,0:T(8,128)(2,1)} custom-call(f32[1,1024]{1,0:T(1,128)} %bitcast.49, bf16[1024,768]{1,0:T(8,128)(2,1)} %fusion.10.refs_0_.refs_1_, bf16[512,1536]{1,0:T(8,128)(2,1)} %collective-permute-done.2.refs_2_.refs_3_, bf16[512,1536]{1,0:T(8,128)(2,1)} %collective-permute-done.2.refs_2_.refs_3_, ...), custom_call_target="tpu_custom_call" | custom-call | tf_op jit(solution)/shard_map/pallas_call | solution.py:109
  196.3 3.2 %collective-permute-start.9 = (bf16[512,768]{1,0:T(8,128)(2,1)}, bf16[512,768]{1,0:T(8,128)(2,1)S(1)}, u32[]{:S(2)}, u32[]{:S(2)}) collective-permute-start(bf16[512,768]{1,0:T(8,128)(2,1)} %shard_map.59), channel_id=1, source_target_pairs={{0,64},{64,0},{1,65},{65,1},{2,66},{66,2},{3,67},{67,3},{4,68},{68... | collective-permute-start | bytes 2359304 | tf_op jit(solution)/shard_map/ppermute | solution.py:25
  199.5 2.1 collective-permute-done.9
  203.3 9.3 %shard_map.60 = bf16[512,768]{1,0:T(8,128)(2,1)} custom-call(f32[1,1024]{1,0:T(1,128)} %bitcast.50, bf16[1024,768]{1,0:T(8,128)(2,1)} %fusion.10.refs_0_.refs_1_, bf16[512,1536]{1,0:T(8,128)(2,1)} %collective-permute-done.2.refs_2_.refs_3_, bf16[512,1536]{1,0:T(8,128)(2,1)} %collective-permute-done.2.refs_2_.refs_3_, ...), custom_call_target="tpu_custom_call" | custom-call | tf_op jit(solution)/shard_map/pallas_call | solution.py:109
  213.0 1.7 collective-permute-start.11
  215.9 17.6 %collective-permute-done.11 = bf16[512,768]{1,0:T(8,128)(2,1)S(1)} collective-permute-done((bf16[512,768]{1,0:T(8,128)(2,1)S(1)}, bf16[512,768]{1,0:T(8,128)(2,1)S(1)}, u32[]{:S(2)}, u32[]{:S(2)}) %collective-permute-start.11) | collective-permute-done | bytes 786464 | tf_op jit(solution)/shard_map/ppermute | solution.py:25
  (48 shorter events, 15.0 us)
Async XLA Ops:
  0.0 201.7 %copy-start = (bf16[768,1536]{1,0:T(8,128)(2,1)S(1)}, bf16[768,1536]{1,0:T(8,128)(2,1)}, u32[]{:S(2)}) copy-start(bf16[768,1536]{1,0:T(8,128)(2,1)} %param.8) | copy-start | bytes 7077892
  0.0 2.8 %copy-start.1 = (bf16[1,1,512,1536]{3,2,1,0:T(8,128)(2,1)S(1)}, bf16[1,1,512,1536]{3,2,1,0:T(8,128)(2,1)}, u32[]{:S(2)}) copy-start(bf16[1,1,512,1536]{3,2,1,0:T(8,128)(2,1)} %param.5) | copy-start | bytes 4718596
  2.8 18.2 %slice-start = ((s8[7077888]{0:T(1024)(128)(4,1)}), s8[4194304]{0:T(1024)(128)(4,1)S(1)}, s32[]{:S(2)}) async-start(s8[7077888]{0:T(1024)(128)(4,1)} %bitcast.47), calls=%async_computation | async-start | bytes 8388608
  4.5 16.5 %slice-start.1 = ((s8[7077888]{0:T(1024)(128)(4,1)}), s8[2883584]{0:T(1024)(128)(4,1)S(1)}, s32[]{:S(2)}) async-start(s8[7077888]{0:T(1024)(128)(4,1)} %bitcast.47), calls=%async_computation.1 | async-start | bytes 5767168
  4.5 37.6 %collective-permute-start = (bf16[512,1536]{1,0:T(8,128)(2,1)}, bf16[512,1536]{1,0:T(8,128)(2,1)}, u32[]{:S(2)}, u32[]{:S(2)}) collective-permute-start(bf16[512,1536]{1,0:T(8,128)(2,1)} %fusion.3), channel_id=1, source_target_pairs={{0,1},{1,0},{2,3},{3,2},{4,5},{5,4},{6,7},{7,6},{8,9},{9,8},{10,11... | collective-permute-start | bytes 4718600 | tf_op jit(solution)/shard_map/ppermute | solution.py:25
  14.8 67.4 %collective-permute-start.5 = (bf16[512,1536]{1,0:T(8,128)(2,1)}, bf16[512,1536]{1,0:T(8,128)(2,1)}, u32[]{:S(2)}, u32[]{:S(2)}) collective-permute-start(bf16[512,1536]{1,0:T(8,128)(2,1)} %bitcast.19.refs_1_.refs_2_), channel_id=1, source_target_pairs={{0,2},{2,4},{4,6},{6,8},{8,10},{10,12},{12,14},{14,16},{16,18},{18... | collective-permute-start | bytes 4718600 | tf_op jit(solution)/shard_map/ppermute | solution.py:21
  16.1 66.1 %collective-permute-start.7 = (bf16[512,1536]{1,0:T(8,128)(2,1)}, bf16[512,1536]{1,0:T(8,128)(2,1)}, u32[]{:S(2)}, u32[]{:S(2)}) collective-permute-start(bf16[512,1536]{1,0:T(8,128)(2,1)} %bitcast.19.refs_1_.refs_2_), channel_id=1, source_target_pairs={{0,62},{2,0},{4,2},{6,4},{8,6},{10,8},{12,10},{14,12},{16,14},{18,... | collective-permute-start | bytes 4718600 | tf_op jit(solution)/shard_map/ppermute | solution.py:21
  42.1 79.5 %copy-start.5 = (s32[1,4,8]{2,1,0:T(4,128)S(1)}, s32[1,4,8]{2,1,0:T(4,128)}, u32[]{:S(2)}) copy-start(s32[1,4,8]{2,1,0:T(4,128)} %param.9) | copy-start | bytes 388
  47.6 1.7 copy-start.2
  47.6 68.3 %collective-permute-start.1 = (bf16[512,1536]{1,0:T(8,128)(2,1)S(1)}, bf16[512,1536]{1,0:T(8,128)(2,1)}, u32[]{:S(2)}, u32[]{:S(2)}) collective-permute-start(bf16[512,1536]{1,0:T(8,128)(2,1)S(1)} %convolution_convert_fusion.refs_3_.refs_4_), channel_id=1, source_target_pairs={{0,2},{2,4},{4,6},{6,8},{8,10},{10,12},{12,14},{14,16},{16,18},{18... | collective-permute-start | bytes 4718600 | tf_op jit(solution)/shard_map/ppermute | solution.py:21
  49.3 66.6 %collective-permute-start.3 = (bf16[512,1536]{1,0:T(8,128)(2,1)S(1)}, bf16[512,1536]{1,0:T(8,128)(2,1)}, u32[]{:S(2)}, u32[]{:S(2)}) collective-permute-start(bf16[512,1536]{1,0:T(8,128)(2,1)S(1)} %convolution_convert_fusion.refs_3_.refs_4_), channel_id=1, source_target_pairs={{0,62},{2,0},{4,2},{6,4},{8,6},{10,8},{12,10},{14,12},{16,14},{18,... | collective-permute-start | bytes 4718600 | tf_op jit(solution)/shard_map/ppermute | solution.py:21
  82.1 89.4 %collective-permute-start.6 = (bf16[512,1536]{1,0:T(8,128)(2,1)}, bf16[512,1536]{1,0:T(8,128)(2,1)}, u32[]{:S(2)}, u32[]{:S(2)}) collective-permute-start(bf16[512,1536]{1,0:T(8,128)(2,1)} %collective-permute-done.5.refs_2_.refs_3_), channel_id=1, source_target_pairs={{0,2},{2,4},{4,6},{6,8},{8,10},{10,12},{12,14},{14,16},{16,18},{18... | collective-permute-start | bytes 4718600 | tf_op jit(solution)/shard_map/ppermute | solution.py:21
  82.2 89.4 %collective-permute-start.8 = (bf16[512,1536]{1,0:T(8,128)(2,1)}, bf16[512,1536]{1,0:T(8,128)(2,1)}, u32[]{:S(2)}, u32[]{:S(2)}) collective-permute-start(bf16[512,1536]{1,0:T(8,128)(2,1)} %collective-permute-done.7.refs_4_.refs_5_), channel_id=1, source_target_pairs={{0,62},{2,0},{4,2},{6,4},{8,6},{10,8},{12,10},{14,12},{16,14},{18,... | collective-permute-start | bytes 4718600 | tf_op jit(solution)/shard_map/ppermute | solution.py:21
  115.9 70.5 %collective-permute-start.2 = (bf16[512,1536]{1,0:T(8,128)(2,1)}, bf16[512,1536]{1,0:T(8,128)(2,1)}, u32[]{:S(2)}, u32[]{:S(2)}) collective-permute-start(bf16[512,1536]{1,0:T(8,128)(2,1)} %collective-permute-done.1.refs_2_.refs_3_), channel_id=1, source_target_pairs={{0,2},{2,4},{4,6},{6,8},{8,10},{10,12},{12,14},{14,16},{16,18},{18... | collective-permute-start | bytes 4718600 | tf_op jit(solution)/shard_map/ppermute | solution.py:21
  115.9 70.5 %collective-permute-start.4 = (bf16[512,1536]{1,0:T(8,128)(2,1)}, bf16[512,1536]{1,0:T(8,128)(2,1)}, u32[]{:S(2)}, u32[]{:S(2)}) collective-permute-start(bf16[512,1536]{1,0:T(8,128)(2,1)} %collective-permute-done.3.refs_4_.refs_5_), channel_id=1, source_target_pairs={{0,62},{2,0},{4,2},{6,4},{8,6},{10,8},{12,10},{14,12},{16,14},{18,... | collective-permute-start | bytes 4718600 | tf_op jit(solution)/shard_map/ppermute | solution.py:21
  196.3 5.3 %collective-permute-start.9 = (bf16[512,768]{1,0:T(8,128)(2,1)}, bf16[512,768]{1,0:T(8,128)(2,1)S(1)}, u32[]{:S(2)}, u32[]{:S(2)}) collective-permute-start(bf16[512,768]{1,0:T(8,128)(2,1)} %shard_map.59), channel_id=1, source_target_pairs={{0,64},{64,0},{1,65},{65,1},{2,66},{66,2},{3,67},{67,3},{4,68},{68... | collective-permute-start | bytes 2359304 | tf_op jit(solution)/shard_map/ppermute | solution.py:25
  199.5 2.9 %copy-start.3 = (bf16[512,768]{1,0:T(8,128)(2,1)S(1)}, bf16[512,768]{1,0:T(8,128)(2,1)}, u32[]{:S(2)}) copy-start(bf16[512,768]{1,0:T(8,128)(2,1)} %shard_map.59) | copy-start | bytes 2359300
  212.5 20.9 %copy-start.4 = (bf16[512,768]{1,0:T(8,128)(2,1)S(1)}, bf16[512,768]{1,0:T(8,128)(2,1)}, u32[]{:S(2)}) copy-start(bf16[512,768]{1,0:T(8,128)(2,1)} %shard_map.60) | copy-start | bytes 2359300
  212.5 2.6 %collective-permute-start.10 = (bf16[512,768]{1,0:T(8,128)(2,1)}, bf16[512,768]{1,0:T(8,128)(2,1)S(1)}, u32[]{:S(2)}, u32[]{:S(2)}) collective-permute-start(bf16[512,768]{1,0:T(8,128)(2,1)} %shard_map.60), channel_id=1, source_target_pairs={{0,64},{64,0},{1,65},{65,1},{2,66},{66,2},{3,67},{67,3},{4,68},{68... | collective-permute-start | bytes 2359304 | tf_op jit(solution)/shard_map/ppermute | solution.py:25
  213.0 20.5 %collective-permute-start.11 = (bf16[512,768]{1,0:T(8,128)(2,1)S(1)}, bf16[512,768]{1,0:T(8,128)(2,1)S(1)}, u32[]{:S(2)}, u32[]{:S(2)}) collective-permute-start(bf16[512,768]{1,0:T(8,128)(2,1)S(1)} %add_convert_fusion.1), channel_id=1, source_target_pairs={{0,1},{1,0},{2,3},{3,2},{4,5},{5,4},{6,7},{7,6},{8,9},{9,8},{10,11... | collective-permute-start | bytes 2359304 | tf_op jit(solution)/shard_map/ppermute | solution.py:25

commit v13 on v11

--- a/solution.py
+++ b/solution.py
@@ -56,8 +56,8 @@
         if masked:
             scores = scores + bias_ref[:, index * width : (index + 1) * width]
         m_new = jnp.maximum(m, jnp.max(scores, axis=1, keepdims=True))
-        alpha = jnp.exp(m - m_new)
-        expon = jnp.exp(scores - jnp.tile(m_new, (1, width // HEAD_DIM)))
+        alpha = jnp.exp2(m - m_new)
+        expon = jnp.exp2(scores - jnp.tile(m_new, (1, width // HEAD_DIM)))
         l = alpha * l + jnp.sum(expon, axis=1, keepdims=True)
         acc = alpha * acc + jnp.dot(
             expon.astype(jnp.bfloat16), values, preferred_element_type=jnp.float32
@@ -81,7 +81,7 @@
         first=first,
         last=last,
         masked=masked,
-        scale=HEAD_DIM ** (-0.5),
+        scale=HEAD_DIM ** (-0.5) * 1.4426950408889634,
     )
     row_spec = pl.BlockSpec((rows, HEAD_DIM), lambda h: (row_block, h))
     in_specs = []

time: 232 us -> 231 us (level)
  Pallas kernels: 74.3 us -> 71.7 us
  waiting for transfers between devices: 82.1 us -> 84.5 us
    pallas_call x6, Pallas kernels: 74.3 us -> 71.7 us  [attend_stage(): pl.pallas_call(kernel, out_shape=out_shape, grid=(heads,), in_specs=in_sp...]
    ppermute x8, waiting for transfers between devices: 52.4 us -> 54.8 us  [from_behind(): lax.ppermute(array, axis, [(i, (i + by) % count) for i in range(count)])]
  transfers between devices with their start and end apart: 12 -> 12, of which waited for: 7 -> 7; matrix products, arithmetic and copies ran while one was open for 14% -> 14% of each run, Pallas kernels for 24% -> 23%
where the time goes in v13:
time: 231 us; the launch traced here: 230 us
  waiting for transfers between devices  84.5 us (37%)
  Pallas kernels  71.7 us (31%)
  starting transfers between devices  32.4 us (14%)
  matrix products  22.4 us (10%)
  local copies, waits for them, and re-layouts  14.2 us (6%)
  other arithmetic  4.87 us (2%)
    pallas_call x6, Pallas kernels, attend_stage(): pl.pallas_call(kernel, out_shape=out_shape, grid=(heads,), in_specs=in_sp...  71.7 us
    ppermute x8, waiting for transfers between devices, from_behind(): lax.ppermute(array, axis, [(i, (i + by) % count) for i in range(count)])  54.8 us
    ppermute x4, waiting for transfers between devices, swap(): return lax.ppermute(array, axis, [(0, 1), (1, 0)])  29.7 us
    ppermute x8, starting transfers between devices, from_behind(): lax.ppermute(array, axis, [(i, (i + by) % count) for i in range(count)])  25.2 us
    ppermute x4, starting transfers between devices, swap(): return lax.ppermute(array, axis, [(0, 1), (1, 0)])  7.29 us
    dot_general x1, matrix products, per_device_body(): jnp.dot(normed, kv_w, preferred_element_type=jnp.float32)  6.8 us
    unnamed x13, local copies, waits for them, and re-layouts  6.65 us
    dot_general x1, matrix products, per_device_body(): jnp.dot(both_rows, q_w, preferred_element_type=jnp.float32)  6.39 us
  transfers between devices with their start and end apart: 12, of which 7 were waited for; matrix products, arithmetic and copies ran while one was open for 14% of the time, Pallas kernels for 23%

profile of v13, /device:TPU:1, one launch (start us, length us, event | category | flops | bytes accessed | tf_op | source)
XLA Modules:
  0.0 230.2 jit_solution(6504978670507087762)
XLA Ops:
  0.9 1.9 fusion.2
  2.8 1.8 fusion.5
  4.6 3.6 %collective-permute-start = (bf16[512,1536]{1,0:T(8,128)(2,1)}, bf16[512,1536]{1,0:T(8,128)(2,1)}, u32[]{:S(2)}, u32[]{:S(2)}) collective-permute-start(bf16[512,1536]{1,0:T(8,128)(2,1)} %fusion.5), channel_id=1, source_target_pairs={{0,1},{1,0},{2,3},{3,2},{4,5},{5,4},{6,7},{7,6},{8,9},{9,8},{10,11... | collective-permute-start | bytes 4718600 | tf_op jit(solution)/shard_map/ppermute | solution.py:25
  8.1 4.7 %slice.39 = bf16[1536,2,768]{2,0,1:T(8,128)(2,1)} slice(bf16[1536,3,768]{2,0,1:T(8,128)(2,1)} %param.7), slice={[0:1536], [1:3], [0:768]} | slice | bytes 9437184 | tf_op jit(solution)/shard_map/slice | solution.py:131
  12.9 6.6 %copy.7 = bf16[1536,2,768]{0,2,1:T(8,128)(2,1)} copy(bf16[1536,2,768]{2,0,1:T(8,128)(2,1)} %slice.39) | data formatting | bytes 9437184
  19.5 6.8 %convolution_convert_fusion.refs_1_.refs_2_ = bf16[512,1536]{1,0:T(8,128)(2,1)} fusion(bf16[1536,1536]{0,1:T(8,128)(2,1)} %bitcast.52, bf16[1,1,512,1536]{3,2,1,0:T(8,128)(2,1)} %param.5, f32[1536]{0:T(1024)S(1)} %get-tuple-element.46, f32[1536]{0:T(1024)S(1)} %get-tuple-element.45, f32[512]{0:T(512)S(1)} %add_rsqrt_fusion), kind=kOutput, calls=%fused_computation.15 | convolution fusion | flops 2420637696 | bytes 7878656 | tf_op jit(solution)/shard_map/dot_general | solution.py:133
  27.6 4.9 %collective-permute-start.7 = (bf16[512,1536]{1,0:T(8,128)(2,1)}, bf16[512,1536]{1,0:T(8,128)(2,1)}, u32[]{:S(2)}, u32[]{:S(2)}) collective-permute-start(bf16[512,1536]{1,0:T(8,128)(2,1)} %convolution_convert_fusion.refs_1_.refs_2_), channel_id=1, source_target_pairs={{0,62},{2,0},{4,2},{6,4},{8,6},{10,8},{12,10},{14,12},{16,14},{18,... | collective-permute-start | bytes 4718600 | tf_op jit(solution)/shard_map/ppermute | solution.py:21
  32.5 9.6 %collective-permute-done = bf16[512,1536]{1,0:T(8,128)(2,1)} collective-permute-done((bf16[512,1536]{1,0:T(8,128)(2,1)}, bf16[512,1536]{1,0:T(8,128)(2,1)}, u32[]{:S(2)}, u32[]{:S(2)}) %collective-permute-start) | collective-permute-done | bytes 1572896 | tf_op jit(solution)/shard_map/ppermute | solution.py:25
  42.2 5.2 %convolution_convert_fusion.1.refs_3_.refs_4_ = bf16[512,1536]{1,0:T(8,128)(2,1)} fusion(bf16[512,1536]{1,0:T(8,128)(2,1)} %collective-permute-done, bf16[1536,1536]{0,1:T(8,128)(2,1)S(1)} %bitcast.53), kind=kOutput, calls=%fused_computation.16 | convolution fusion | flops 2416705536 | bytes 7864320 | tf_op jit(solution)/shard_map/dot_general | solution.py:137
  47.4 6.4 %fusion.15.refs_0_.refs_1_ = bf16[1024,768]{1,0:T(8,128)(2,1)} fusion(bf16[1536,3,768]{2,0,1:T(8,128)(2,1)} %param.7, bf16[512,1536]{1,0:T(8,128)(2,1)} %collective-permute-done, bf16[512,1536]{1,0:T(8,128)(2,1)} %fusion.5), kind=kOutput, calls=%fused_computation.19 | convolution fusion | flops 2422996992 | bytes 7077888 | tf_op jit(solution)/shard_map/dot_general | solution.py:141
  53.8 12.4 %shard_map.55 = (f32[1024,768]{1,0:T(8,128)}, f32[1024,768]{1,0:T(8,128)}, f32[1024,768]{1,0:T(8,128)}) custom-call(bf16[1024,768]{1,0:T(8,128)(2,1)} %fusion.15.refs_0_.refs_1_, bf16[512,1536]{1,0:T(8,128)(2,1)} %convolution_convert_fusion.refs_1_.refs_2_, bf16[512,1536]{1,0:T(8,128)(2,1)} %convolution_convert_fusion.refs_1_.refs_2_, ...), custom_call_target="tpu_custom_call" | custom-call | tf_op jit(solution)/shard_map/pallas_call | solution.py:109
  67.8 5.9 %collective-permute-start.3 = (bf16[512,1536]{1,0:T(8,128)(2,1)}, bf16[512,1536]{1,0:T(8,128)(2,1)}, u32[]{:S(2)}, u32[]{:S(2)}) collective-permute-start(bf16[512,1536]{1,0:T(8,128)(2,1)} %convolution_convert_fusion.1.refs_3_.refs_4_), channel_id=1, source_target_pairs={{0,62},{2,0},{4,2},{6,4},{8,6},{10,8},{12,10},{14,12},{16,14},{18,... | collective-permute-start | bytes 4718600 | tf_op jit(solution)/shard_map/ppermute | solution.py:21
  73.7 8.6 %collective-permute-done.5.refs_2_.refs_3_ = bf16[512,1536]{1,0:T(8,128)(2,1)} collective-permute-done((bf16[512,1536]{1,0:T(8,128)(2,1)}, bf16[512,1536]{1,0:T(8,128)(2,1)}, u32[]{:S(2)}, u32[]{:S(2)}) %collective-permute-start.5) | collective-permute-done | bytes 1572896 | tf_op jit(solution)/shard_map/ppermute | solution.py:21
  82.2 5.7 %collective-permute-start.8 = (bf16[512,1536]{1,0:T(8,128)(2,1)}, bf16[512,1536]{1,0:T(8,128)(2,1)}, u32[]{:S(2)}, u32[]{:S(2)}) collective-permute-start(bf16[512,1536]{1,0:T(8,128)(2,1)} %collective-permute-done.7.refs_4_.refs_5_), channel_id=1, source_target_pairs={{0,62},{2,0},{4,2},{6,4},{8,6},{10,8},{12,10},{14,12},{16,14},{18,... | collective-permute-start | bytes 4718600 | tf_op jit(solution)/shard_map/ppermute | solution.py:21
  87.9 28.0 %collective-permute-done.1.refs_2_.refs_3_ = bf16[512,1536]{1,0:T(8,128)(2,1)} collective-permute-done((bf16[512,1536]{1,0:T(8,128)(2,1)}, bf16[512,1536]{1,0:T(8,128)(2,1)}, u32[]{:S(2)}, u32[]{:S(2)}) %collective-permute-start.1) | collective-permute-done | bytes 1572896 | tf_op jit(solution)/shard_map/ppermute | solution.py:21
  115.9 5.7 %collective-permute-start.4 = (bf16[512,1536]{1,0:T(8,128)(2,1)}, bf16[512,1536]{1,0:T(8,128)(2,1)}, u32[]{:S(2)}, u32[]{:S(2)}) collective-permute-start(bf16[512,1536]{1,0:T(8,128)(2,1)} %collective-permute-done.3.refs_4_.refs_5_), channel_id=1, source_target_pairs={{0,62},{2,0},{4,2},{6,4},{8,6},{10,8},{12,10},{14,12},{16,14},{18,... | collective-permute-start | bytes 4718600 | tf_op jit(solution)/shard_map/ppermute | solution.py:21
  122.7 13.7 %shard_map.56 = (f32[1024,768]{1,0:T(8,128)}, f32[1024,768]{1,0:T(8,128)}, f32[1024,768]{1,0:T(8,128)}) custom-call(f32[1,1024]{1,0:T(1,128)} %bitcast.57, bf16[1024,768]{1,0:T(8,128)(2,1)} %fusion.15.refs_0_.refs_1_, bf16[512,1536]{1,0:T(8,128)(2,1)} %collective-permute-done.5.refs_2_.refs_3_, bf16[512,1536]{1,0:T(8,128)(2,1)} %collective-permute-done.5.refs_2_.refs_3_, ...), custom_call_target="tpu_custom_call" | custom-call | tf_op jit(solution)/shard_map/pallas_call | solution.py:109
  137.1 13.7 %shard_map.57 = (f32[1024,768]{1,0:T(8,128)}, f32[1024,768]{1,0:T(8,128)}, f32[1024,768]{1,0:T(8,128)}) custom-call(f32[1,1024]{1,0:T(1,128)} %bitcast.58, bf16[1024,768]{1,0:T(8,128)(2,1)} %fusion.15.refs_0_.refs_1_, bf16[512,1536]{1,0:T(8,128)(2,1)} %collective-permute-done.1.refs_2_.refs_3_, bf16[512,1536]{1,0:T(8,128)(2,1)} %collective-permute-done.1.refs_2_.refs_3_, ...), custom_call_target="tpu_custom_call" | custom-call | tf_op jit(solution)/shard_map/pallas_call | solution.py:109
  151.5 13.7 %shard_map.58 = (f32[1024,768]{1,0:T(8,128)}, f32[1024,768]{1,0:T(8,128)}, f32[1024,768]{1,0:T(8,128)}) custom-call(f32[1,1024]{1,0:T(1,128)} %bitcast.56, bf16[1024,768]{1,0:T(8,128)(2,1)} %fusion.15.refs_0_.refs_1_, bf16[512,1536]{1,0:T(8,128)(2,1)} %collective-permute-done.6.refs_2_.refs_3_, bf16[512,1536]{1,0:T(8,128)(2,1)} %collective-permute-done.6.refs_2_.refs_3_, ...), custom_call_target="tpu_custom_call" | custom-call | tf_op jit(solution)/shard_map/pallas_call | solution.py:109
  165.2 18.2 %collective-permute-done.2.refs_2_.refs_3_ = bf16[512,1536]{1,0:T(8,128)(2,1)} collective-permute-done((bf16[512,1536]{1,0:T(8,128)(2,1)}, bf16[512,1536]{1,0:T(8,128)(2,1)}, u32[]{:S(2)}, u32[]{:S(2)}) %collective-permute-start.2) | collective-permute-done | bytes 1572896 | tf_op jit(solution)/shard_map/ppermute | solution.py:21
  184.0 9.2 %shard_map.59 = bf16[512,768]{1,0:T(8,128)(2,1)} custom-call(f32[1,1024]{1,0:T(1,128)} %bitcast.54, bf16[1024,768]{1,0:T(8,128)(2,1)} %fusion.15.refs_0_.refs_1_, bf16[512,1536]{1,0:T(8,128)(2,1)} %collective-permute-done.2.refs_2_.refs_3_, bf16[512,1536]{1,0:T(8,128)(2,1)} %collective-permute-done.2.refs_2_.refs_3_, ...), custom_call_target="tpu_custom_call" | custom-call | tf_op jit(solution)/shard_map/pallas_call | solution.py:109
  194.7 2.1 collective-permute-done.9
  198.4 9.1 %shard_map.60 = bf16[512,768]{1,0:T(8,128)(2,1)} custom-call(f32[1,1024]{1,0:T(1,128)} %bitcast.55, bf16[1024,768]{1,0:T(8,128)(2,1)} %fusion.15.refs_0_.refs_1_, bf16[512,1536]{1,0:T(8,128)(2,1)} %collective-permute-done.2.refs_2_.refs_3_, bf16[512,1536]{1,0:T(8,128)(2,1)} %collective-permute-done.2.refs_2_.refs_3_, ...), custom_call_target="tpu_custom_call" | custom-call | tf_op jit(solution)/shard_map/pallas_call | solution.py:109
  210.9 17.6 %collective-permute-done.11 = bf16[512,768]{1,0:T(8,128)(2,1)S(1)} collective-permute-done((bf16[512,768]{1,0:T(8,128)(2,1)S(1)}, bf16[512,768]{1,0:T(8,128)(2,1)S(1)}, u32[]{:S(2)}, u32[]{:S(2)}) %collective-permute-start.11) | collective-permute-done | bytes 786464 | tf_op jit(solution)/shard_map/ppermute | solution.py:25
  (42 shorter events, 15.2 us)
Async XLA Ops:
  0.0 196.8 %copy-start = (bf16[768,1536]{1,0:T(8,128)(2,1)S(1)}, bf16[768,1536]{1,0:T(8,128)(2,1)}, u32[]{:S(2)}) copy-start(bf16[768,1536]{1,0:T(8,128)(2,1)} %param.8) | copy-start | bytes 7077892
  0.0 2.8 %copy-start.1 = (bf16[1,1,512,1536]{3,2,1,0:T(8,128)(2,1)S(1)}, bf16[1,1,512,1536]{3,2,1,0:T(8,128)(2,1)}, u32[]{:S(2)}) copy-start(bf16[1,1,512,1536]{3,2,1,0:T(8,128)(2,1)} %param.5) | copy-start | bytes 4718596
  4.6 37.6 %collective-permute-start = (bf16[512,1536]{1,0:T(8,128)(2,1)}, bf16[512,1536]{1,0:T(8,128)(2,1)}, u32[]{:S(2)}, u32[]{:S(2)}) collective-permute-start(bf16[512,1536]{1,0:T(8,128)(2,1)} %fusion.5), channel_id=1, source_target_pairs={{0,1},{1,0},{2,3},{3,2},{4,5},{5,4},{6,7},{7,6},{8,9},{9,8},{10,11... | collective-permute-start | bytes 4718600 | tf_op jit(solution)/shard_map/ppermute | solution.py:25
  19.5 22.7 %copy-start.2 = (bf16[1536,2,768]{0,2,1:T(8,128)(2,1)S(1)}, bf16[1536,2,768]{0,2,1:T(8,128)(2,1)}, u32[]{:S(2)}) copy-start(bf16[1536,2,768]{0,2,1:T(8,128)(2,1)} %copy.7) | copy-start | bytes 14155780
  26.3 55.9 %collective-permute-start.5 = (bf16[512,1536]{1,0:T(8,128)(2,1)}, bf16[512,1536]{1,0:T(8,128)(2,1)}, u32[]{:S(2)}, u32[]{:S(2)}) collective-permute-start(bf16[512,1536]{1,0:T(8,128)(2,1)} %convolution_convert_fusion.refs_1_.refs_2_), channel_id=1, source_target_pairs={{0,2},{2,4},{4,6},{6,8},{8,10},{10,12},{12,14},{14,16},{16,18},{18... | collective-permute-start | bytes 4718600 | tf_op jit(solution)/shard_map/ppermute | solution.py:21
  27.6 54.6 %collective-permute-start.7 = (bf16[512,1536]{1,0:T(8,128)(2,1)}, bf16[512,1536]{1,0:T(8,128)(2,1)}, u32[]{:S(2)}, u32[]{:S(2)}) collective-permute-start(bf16[512,1536]{1,0:T(8,128)(2,1)} %convolution_convert_fusion.refs_1_.refs_2_), channel_id=1, source_target_pairs={{0,62},{2,0},{4,2},{6,4},{8,6},{10,8},{12,10},{14,12},{16,14},{18,... | collective-permute-start | bytes 4718600 | tf_op jit(solution)/shard_map/ppermute | solution.py:21
  53.8 67.9 %copy-start.5 = (s32[1,4,8]{2,1,0:T(4,128)S(1)}, s32[1,4,8]{2,1,0:T(4,128)}, u32[]{:S(2)}) copy-start(s32[1,4,8]{2,1,0:T(4,128)} %param.9) | copy-start | bytes 388
  66.1 49.8 %collective-permute-start.1 = (bf16[512,1536]{1,0:T(8,128)(2,1)}, bf16[512,1536]{1,0:T(8,128)(2,1)}, u32[]{:S(2)}, u32[]{:S(2)}) collective-permute-start(bf16[512,1536]{1,0:T(8,128)(2,1)} %convolution_convert_fusion.1.refs_3_.refs_4_), channel_id=1, source_target_pairs={{0,2},{2,4},{4,6},{6,8},{8,10},{10,12},{12,14},{14,16},{16,18},{18... | collective-permute-start | bytes 4718600 | tf_op jit(solution)/shard_map/ppermute | solution.py:21
  67.8 48.2 %collective-permute-start.3 = (bf16[512,1536]{1,0:T(8,128)(2,1)}, bf16[512,1536]{1,0:T(8,128)(2,1)}, u32[]{:S(2)}, u32[]{:S(2)}) collective-permute-start(bf16[512,1536]{1,0:T(8,128)(2,1)} %convolution_convert_fusion.1.refs_3_.refs_4_), channel_id=1, source_target_pairs={{0,62},{2,0},{4,2},{6,4},{8,6},{10,8},{12,10},{14,12},{16,14},{18,... | collective-permute-start | bytes 4718600 | tf_op jit(solution)/shard_map/ppermute | solution.py:21
  82.2 68.6 %collective-permute-start.6 = (bf16[512,1536]{1,0:T(8,128)(2,1)}, bf16[512,1536]{1,0:T(8,128)(2,1)}, u32[]{:S(2)}, u32[]{:S(2)}) collective-permute-start(bf16[512,1536]{1,0:T(8,128)(2,1)} %collective-permute-done.5.refs_2_.refs_3_), channel_id=1, source_target_pairs={{0,2},{2,4},{4,6},{6,8},{8,10},{10,12},{12,14},{14,16},{16,18},{18... | collective-permute-start | bytes 4718600 | tf_op jit(solution)/shard_map/ppermute | solution.py:21
  82.2 68.6 %collective-permute-start.8 = (bf16[512,1536]{1,0:T(8,128)(2,1)}, bf16[512,1536]{1,0:T(8,128)(2,1)}, u32[]{:S(2)}, u32[]{:S(2)}) collective-permute-start(bf16[512,1536]{1,0:T(8,128)(2,1)} %collective-permute-done.7.refs_4_.refs_5_), channel_id=1, source_target_pairs={{0,62},{2,0},{4,2},{6,4},{8,6},{10,8},{12,10},{14,12},{16,14},{18,... | collective-permute-start | bytes 4718600 | tf_op jit(solution)/shard_map/ppermute | solution.py:21
  115.9 67.4 %collective-permute-start.2 = (bf16[512,1536]{1,0:T(8,128)(2,1)}, bf16[512,1536]{1,0:T(8,128)(2,1)}, u32[]{:S(2)}, u32[]{:S(2)}) collective-permute-start(bf16[512,1536]{1,0:T(8,128)(2,1)} %collective-permute-done.1.refs_2_.refs_3_), channel_id=1, source_target_pairs={{0,2},{2,4},{4,6},{6,8},{8,10},{10,12},{12,14},{14,16},{16,18},{18... | collective-permute-start | bytes 4718600 | tf_op jit(solution)/shard_map/ppermute | solution.py:21
  115.9 67.4 %collective-permute-start.4 = (bf16[512,1536]{1,0:T(8,128)(2,1)}, bf16[512,1536]{1,0:T(8,128)(2,1)}, u32[]{:S(2)}, u32[]{:S(2)}) collective-permute-start(bf16[512,1536]{1,0:T(8,128)(2,1)} %collective-permute-done.3.refs_4_.refs_5_), channel_id=1, source_target_pairs={{0,62},{2,0},{4,2},{6,4},{8,6},{10,8},{12,10},{14,12},{16,14},{18,... | collective-permute-start | bytes 4718600 | tf_op jit(solution)/shard_map/ppermute | solution.py:21
  193.2 3.7 %collective-permute-start.9 = (bf16[512,768]{1,0:T(8,128)(2,1)}, bf16[512,768]{1,0:T(8,128)(2,1)S(1)}, u32[]{:S(2)}, u32[]{:S(2)}) collective-permute-start(bf16[512,768]{1,0:T(8,128)(2,1)} %shard_map.59), channel_id=1, source_target_pairs={{0,64},{64,0},{1,65},{65,1},{2,66},{66,2},{3,67},{67,3},{4,68},{68... | collective-permute-start | bytes 2359304 | tf_op jit(solution)/shard_map/ppermute | solution.py:25
  194.7 2.9 %copy-start.3 = (bf16[512,768]{1,0:T(8,128)(2,1)S(1)}, bf16[512,768]{1,0:T(8,128)(2,1)}, u32[]{:S(2)}) copy-start(bf16[512,768]{1,0:T(8,128)(2,1)} %shard_map.59) | copy-start | bytes 2359300
  207.5 20.9 %copy-start.4 = (bf16[512,768]{1,0:T(8,128)(2,1)S(1)}, bf16[512,768]{1,0:T(8,128)(2,1)}, u32[]{:S(2)}) copy-start(bf16[512,768]{1,0:T(8,128)(2,1)} %shard_map.60) | copy-start | bytes 2359300
  207.6 2.6 %collective-permute-start.10 = (bf16[512,768]{1,0:T(8,128)(2,1)}, bf16[512,768]{1,0:T(8,128)(2,1)S(1)}, u32[]{:S(2)}, u32[]{:S(2)}) collective-permute-start(bf16[512,768]{1,0:T(8,128)(2,1)} %shard_map.60), channel_id=1, source_target_pairs={{0,64},{64,0},{1,65},{65,1},{2,66},{66,2},{3,67},{67,3},{4,68},{68... | collective-permute-start | bytes 2359304 | tf_op jit(solution)/shard_map/ppermute | solution.py:25
  208.0 20.5 %collective-permute-start.11 = (bf16[512,768]{1,0:T(8,128)(2,1)S(1)}, bf16[512,768]{1,0:T(8,128)(2,1)S(1)}, u32[]{:S(2)}, u32[]{:S(2)}) collective-permute-start(bf16[512,768]{1,0:T(8,128)(2,1)S(1)} %add_convert_fusion.1), channel_id=1, source_target_pairs={{0,1},{1,0},{2,3},{3,2},{4,5},{5,4},{6,7},{7,6},{8,9},{9,8},{10,11... | collective-permute-start | bytes 2359304 | tf_op jit(solution)/shard_map/ppermute | solution.py:25
